TPU v7x, 128 devices: a whole 4x4x4 slice. The times are simulated.
128 devices in a mesh: seq: 32 (over z, y, core), head: 4 (over x).
Axes of the slice: x: 4, y: 4, z: 4, core: 2. Of those that a mesh axis runs over, the one named last changes fastest.
Arguments:
- queries: bfloat16 [32768, 4096], P(('seq', 'head')), may hold values from -6 to 6
- key_rows: bfloat16 [32768, 4096], P(('seq', 'head')), may hold values from -6 to 6
- value_rows: bfloat16 [32768, 4096], P(('seq', 'head')), may hold values from -6 to 6
- decay_rates: float32 [32], replicated, as said below
- norm_gain: float32 [4096], replicated, may hold values from 0.5 to 1.5
Outputs:
- attended: bfloat16 [32768, 4096], P(('seq', 'head'))
Inputs may be any that keep to these rules, and one draw needn't show every extreme that they name: `decay_rates`: one positive rate per head.
All inputs are finite; a program needn't handle non-finite values.
Results may differ from a plain program's by a relative error of at most 0.003.
Values may be sent and summed in bfloat16 or wider, within the bound.
No kernel may reach another device: no remote copies, remote signals or barrier semaphores. Data moves between devices by JAX's collectives and lax.ppermute only.
A program may use at most 512 MiB of HBM per device.

v0:
```python
import jax
import jax.numpy as jnp
from jax import lax
from jax.sharding import PartitionSpec as P

HEADS = 32
HEAD_DIM = 128
BLOCK = 256


def carried_in(shard, axis, combine, identity):
    size, here = (lax.axis_size(axis), lax.axis_index(axis))
    everything = jax.tree.map(lambda part: lax.all_gather(part, axis), shard)
    start = jax.tree.map(
        lambda part, zero: jnp.broadcast_to(jnp.asarray(zero, part.dtype), part.shape),
        shard,
        identity,
    )

    def hop(k, before):
        reached = k < here
        new = combine(before, jax.tree.map(lambda part: part[k], everything))
        return jax.tree.map(lambda a, b: jnp.where(reached, a, b), new, before)

    return lax.fori_loop(0, size, hop, start)


def block_chain(queries, key_rows, value_rows, rates, block):
    tokens, heads, width = queries.shape
    count = tokens // block
    q_blocks = queries.reshape(count, block, heads, width)
    k_blocks = key_rows.reshape(count, block, heads, width)
    v_blocks = value_rows.reshape(count, block, heads, width)
    positions = jnp.arange(block, dtype=jnp.float32)
    offsets = positions[:, None] - positions[None, :]
    within = jnp.where(
        offsets[None] >= 0.0, jnp.exp(-rates[:, None, None] * jnp.maximum(offsets, 0.0)[None]), 0.0
    )
    q_decay = jnp.exp(-rates[None, :] * (positions[:, None] + 1.0))[:, :, None]
    k_decay = jnp.exp(-rates[None, :] * (block - 1.0 - positions[:, None]))[:, :, None]
    carry_decay = jnp.exp(-rates * block)[:, None, None]

    def advance(state, items):
        q_part, k_part, v_part = items
        scores = jnp.einsum("ihe,jhe->hij", q_part, k_part, preferred_element_type=jnp.float32)
        weights = (scores * within).astype(jnp.bfloat16)
        intra = jnp.einsum("hij,jhe->ihe", weights, v_part, preferred_element_type=jnp.float32)
        inter = jnp.einsum(
            "ihe,hef->ihf",
            q_part.astype(jnp.float32) * q_decay,
            state,
            precision=lax.Precision.HIGHEST,
        )
        added = jnp.einsum(
            "jhe,jhf->hef",
            k_part.astype(jnp.float32) * k_decay,
            v_part.astype(jnp.float32),
            precision=lax.Precision.HIGHEST,
        )
        return (carry_decay * state + added, intra + inter)

    start = jnp.zeros((heads, width, width), jnp.float32)
    state, outputs = lax.scan(advance, start, (q_blocks, k_blocks, v_blocks))
    return (outputs.reshape(tokens, heads, width), state)


def combine_states(earlier, later):
    return (earlier[0] * later[0], later[0][:, None, None] * earlier[1] + later[1])


def add_incoming(partial_value, queries, rates, incoming):
    span = queries.shape[0]
    positions = jnp.arange(span, dtype=jnp.float32)
    q_decay = jnp.exp(-rates[None, :] * (positions[:, None] + 1.0))[:, :, None]
    return partial_value + jnp.einsum(
        "ihe,hef->ihf",
        queries.astype(jnp.float32) * q_decay,
        incoming,
        precision=lax.Precision.HIGHEST,
    )


def normalize(total, gains):
    mean_square = jnp.mean(total * total, axis=-1, keepdims=True)
    normed = (total * lax.rsqrt(mean_square + 1e-06) * gains).astype(jnp.bfloat16)
    return normed.reshape(total.shape[0], total.shape[1] * total.shape[2])


def body(queries, key_rows, value_rows, decay_rates, norm_gain):
    group_heads = HEADS // lax.axis_size("head")
    first_head = lax.axis_index("head") * group_heads
    rates = lax.dynamic_slice_in_dim(decay_rates, first_head, group_heads)
    gains = lax.dynamic_slice_in_dim(
        norm_gain, first_head * HEAD_DIM, group_heads * HEAD_DIM
    ).reshape(group_heads, HEAD_DIM)
    q_group, k_group, v_group = (
        lax.all_to_all(queries, "head", split_axis=1, concat_axis=0, tiled=True),
        lax.all_to_all(key_rows, "head", split_axis=1, concat_axis=0, tiled=True),
        lax.all_to_all(value_rows, "head", split_axis=1, concat_axis=0, tiled=True),
    )
    span = q_group.shape[0]
    shaped = (span, group_heads, HEAD_DIM)
    q_group = q_group.reshape(shaped)
    partial_value, local_state = block_chain(
        q_group, k_group.reshape(shaped), v_group.reshape(shaped), rates, BLOCK
    )
    span_decay = jnp.exp(-rates * span)
    identity = (jnp.ones_like(span_decay), jnp.zeros_like(local_state))
    _, incoming = carried_in((span_decay, local_state), "seq", combine_states, identity)
    total = add_incoming(partial_value, q_group, rates, incoming)
    normed = normalize(total, gains)
    return lax.all_to_all(normed, "head", split_axis=0, concat_axis=1, tiled=True)


def solution(mesh):
    return jax.shard_map(
        body,
        mesh=mesh,
        in_specs=(
            P(("seq", "head"), None),
            P(("seq", "head"), None),
            P(("seq", "head"), None),
            P(),
            P(),
        ),
        out_specs=P(("seq", "head"), None),
        check_vma=False,
    )
```

profile of v0, /device:TPU:1, one launch (start us, length us, event | category | flops | bytes accessed | tf_op | source)
XLA Modules:
  0.0 419.5 jit_solution(12384549919905973251)
XLA Ops:
  6.5 4.1 copy.57
  10.6 5.0 %all-to-all-start.2 = ((bf16[256,4,1024]{0,2,1:T(8,128)(2,1)}), bf16[256,4,1024]{0,2,1:T(8,128)(2,1)}, u32[]{:S(2)}, u32[]{:S(2)}) async-start(bf16[256,4,1024]{0,2,1:T(8,128)(2,1)} %bitcast.7), calls=%async_computation.2 | async-start | bytes 4194304 | tf_op jit(solution)/shard_map/all_to_all | solution.py:97
  15.6 2.4 copy.55
  18.1 23.4 %all-to-all-done.2 = bf16[256,4,1024]{0,2,1:T(8,128)(2,1)} async-done(((bf16[256,4,1024]{0,2,1:T(8,128)(2,1)}), bf16[256,4,1024]{0,2,1:T(8,128)(2,1)}, u32[]{:S(2)}, u32[]{:S(2)}) %all-to-all-start.2) | async-done | bytes 2097184 | tf_op jit(solution)/shard_map/all_to_all | solution.py:97
  41.5 4.6 %all-to-all-start = ((bf16[256,4,1024]{0,2,1:T(8,128)(2,1)}), bf16[256,4,1024]{0,2,1:T(8,128)(2,1)}, u32[]{:S(2)}, u32[]{:S(2)}) async-start(bf16[256,4,1024]{0,2,1:T(8,128)(2,1)} %bitcast.1), calls=%async_computation | async-start | bytes 4194304 | tf_op jit(solution)/shard_map/all_to_all | solution.py:98
  46.0 2.5 copy.56
  48.5 22.2 %all-to-all-done = bf16[256,4,1024]{0,2,1:T(8,128)(2,1)} async-done(((bf16[256,4,1024]{0,2,1:T(8,128)(2,1)}), bf16[256,4,1024]{0,2,1:T(8,128)(2,1)}, u32[]{:S(2)}, u32[]{:S(2)}) %all-to-all-start) | async-done | bytes 2097184 | tf_op jit(solution)/shard_map/all_to_all | solution.py:98
  70.7 4.6 %all-to-all-start.1 = ((bf16[256,4,1024]{0,2,1:T(8,128)(2,1)}), bf16[256,4,1024]{0,2,1:T(8,128)(2,1)}, u32[]{:S(2)}, u32[]{:S(2)}) async-start(bf16[256,4,1024]{0,2,1:T(8,128)(2,1)} %bitcast.4), calls=%async_computation.1 | async-start | bytes 4194304 | tf_op jit(solution)/shard_map/all_to_all | solution.py:99
  77.0 22.1 %all-to-all-done.1 = bf16[256,4,1024]{0,2,1:T(8,128)(2,1)} async-done(((bf16[256,4,1024]{0,2,1:T(8,128)(2,1)}), bf16[256,4,1024]{0,2,1:T(8,128)(2,1)}, u32[]{:S(2)}, u32[]{:S(2)}) %all-to-all-start.1) | async-done | bytes 2097184 | tf_op jit(solution)/shard_map/all_to_all | solution.py:99
  99.1 139.2 %while.30 = (s32[]{:T(128)}, f32[8,128,128]{2,1,0:T(8,128)S(1)}, f32[4,256,8,128]{1,0,3,2:T(4,128)}, f32[8,1,1]{0,2,1:T(1,128)S(1)}, bf16[4,256,8,128]{1,3,2,0:T...) while((s32[]{:T(128)}, f32[8,128,128]{2,1,0:T(8,128)S(1)}, ...), condition=%wide.region_1.2_spmd.clone.clone.clone, body=%wide.region_0.1_spmd.clone.clone.clone.sunk | while | flops 1077678080 | bytes 16617720 | solution.py:63
  99.1 1.3 constant_dynamic-slice_fusion.7
  100.7 1.4 convolution_bitcast_fusion.2
  102.1 3.3 fusion.63
  105.4 2.3 copy.90
  107.7 23.4 %dynamic_update_slice.8 = f32[4,256,8,128]{1,0,3,2:T(4,128)} dynamic-update-slice(f32[4,256,8,128]{1,0,3,2:T(4,128)} %get-tuple-element.510, f32[1,256,8,128]{1,0,3,2:T(1,128)S(1)} %copy.90, s32[]{:T(128)} %get-tuple-element.508, s32[]{:T(128)} %constant.58.clone.1..sunk.1, s32[]{:T(128)} %constant.58.clone.1..sunk.1, s32[]{:T(128)} %constant.58.clone.1..sunk.1) | dynamic-update-slice | bytes 2097156 | tf_op jit(solution)/shard_map/while/body/jit(dynamic_update_index_in_dim)/dynamic_update_slice | solution.py:63
  131.4 2.4 convolution_add_fusion.2
  133.9 1.3 constant_dynamic-slice_fusion.7
  135.5 1.4 convolution_bitcast_fusion.2
  136.9 3.3 fusion.63
  140.2 2.3 copy.90
  142.5 23.4 %dynamic_update_slice.8 = f32[4,256,8,128]{1,0,3,2:T(4,128)} dynamic-update-slice(f32[4,256,8,128]{1,0,3,2:T(4,128)} %get-tuple-element.510, f32[1,256,8,128]{1,0,3,2:T(1,128)S(1)} %copy.90, s32[]{:T(128)} %get-tuple-element.508, s32[]{:T(128)} %constant.58.clone.1..sunk.1, s32[]{:T(128)} %constant.58.clone.1..sunk.1, s32[]{:T(128)} %constant.58.clone.1..sunk.1) | dynamic-update-slice | bytes 2097156 | tf_op jit(solution)/shard_map/while/body/jit(dynamic_update_index_in_dim)/dynamic_update_slice | solution.py:63
  166.2 2.4 convolution_add_fusion.2
  168.7 1.3 constant_dynamic-slice_fusion.7
  170.3 1.4 convolution_bitcast_fusion.2
  171.7 3.3 fusion.63
  175.0 2.3 copy.90
  177.4 23.4 %dynamic_update_slice.8 = f32[4,256,8,128]{1,0,3,2:T(4,128)} dynamic-update-slice(f32[4,256,8,128]{1,0,3,2:T(4,128)} %get-tuple-element.510, f32[1,256,8,128]{1,0,3,2:T(1,128)S(1)} %copy.90, s32[]{:T(128)} %get-tuple-element.508, s32[]{:T(128)} %constant.58.clone.1..sunk.1, s32[]{:T(128)} %constant.58.clone.1..sunk.1, s32[]{:T(128)} %constant.58.clone.1..sunk.1) | dynamic-update-slice | bytes 2097156 | tf_op jit(solution)/shard_map/while/body/jit(dynamic_update_index_in_dim)/dynamic_update_slice | solution.py:63
  201.1 2.4 convolution_add_fusion.2
  203.5 1.3 constant_dynamic-slice_fusion.7
  205.1 1.4 convolution_bitcast_fusion.2
  206.5 3.3 fusion.63
  209.9 2.3 copy.90
  212.2 23.4 %dynamic_update_slice.8 = f32[4,256,8,128]{1,0,3,2:T(4,128)} dynamic-update-slice(f32[4,256,8,128]{1,0,3,2:T(4,128)} %get-tuple-element.510, f32[1,256,8,128]{1,0,3,2:T(1,128)S(1)} %copy.90, s32[]{:T(128)} %get-tuple-element.508, s32[]{:T(128)} %constant.58.clone.1..sunk.1, s32[]{:T(128)} %constant.58.clone.1..sunk.1, s32[]{:T(128)} %constant.58.clone.1..sunk.1) | dynamic-update-slice | bytes 2097156 | tf_op jit(solution)/shard_map/while/body/jit(dynamic_update_index_in_dim)/dynamic_update_slice | solution.py:63
  235.9 2.4 convolution_add_fusion.2
  239.1 69.0 %all-reduce = f32[256]{0:T(256)S(1)} all-reduce(f32[256]{0:T(256)S(1)} %get-tuple-element.372), channel_id=2, replica_groups=mesh['seq'=32,'head'=4] {'seq'}, use_global_device_ids=true, to_apply=%add | all-reduce | flops 256 | bytes 2048
  308.6 5.8 %reshape.189 = f32[1024,8,128]{0,2,1:T(8,128)} reshape(f32[4,256,8,128]{1,0,3,2:T(4,128)} %get-tuple-element.152) | data formatting | bytes 8388608 | tf_op jit(solution)/shard_map/reshape | solution.py:64
  314.4 4.1 bitcast_convert_fusion
  318.5 5.4 %copy.62 = f32[4,256,1024]{2,1,0:T(8,128)} copy(f32[4,256,1024]{1,2,0:T(8,128)} %bitcast_convert_fusion) | data formatting | bytes 8388608 | tf_op jit(solution)/shard_map/convert_element_type | solution.py:77
  323.9 3.2 copy.78
  327.1 3.9 bitcast_multiply_fusion
  330.9 38.8 %while.29 = (s32[]{:T(128)}, f32[8,128,128]{2,1,0:T(8,128)S(1)}, s32[]{:T(128)}, f32[32,8]{1,0:T(8,128)S(1)}, f32[32,8,128,128]{3,2,1,0:T(8,128)}, /*index=5*/s32[]{:T(128)}, s32[]{:T(128)}) while((s32[]{:T(128)}, f32[8,128,128]{2,1,0:T(8,128)S(1)}, s32[]{:T(128)}, f32[32,8]{1,0:T(8,128)S(1)}, f32[32,8,128,128]{3,2,1,0:T(8,128)}, ...), condition=%wide.region_3.4_spmd.clone, body=%wide.region_2.3_spmd.clone.sunk | while | flops 524292 | bytes 1573065 | solution.py:25
  333.4 1.2 fusion.55
  334.6 1.2 fusion.55
  335.8 1.2 fusion.55
  339.5 1.2 fusion.55
  340.7 1.2 fusion.55
  341.9 1.2 fusion.55
  345.5 1.2 fusion.55
  346.7 1.2 fusion.55
  348.0 1.2 fusion.55
  351.6 1.2 fusion.55
  352.8 1.2 fusion.55
  356.4 1.2 fusion.55
  357.7 1.2 fusion.55
  358.9 1.2 fusion.55
  362.5 1.2 fusion.55
  363.7 1.2 fusion.55
  364.9 1.2 fusion.55
  368.6 1.2 fusion.55
  369.8 8.1 %multiply_reduce_fusion = (f32[1024,8]{0,1:T(8,128)S(1)}, f32[1024,8,128]{0,2,1:T(8,128)S(1)}) fusion(f32[1024,8,128]{0,2,1:T(8,128)} %reshape.189, f32[8,128,128]{2,1,0:T(8,128)S(1)} %get-tuple-element.154, f32[1024,8,128]{2,1,0:T(8,128)} %bitcast_multiply_fusion), kind=kOutput, calls=%fused_computation.48 | convolution fusion | flops 1613750272 | bytes 13139968 | tf_op jit(solution)/shard_map/ihe,hef->ihf/dot_general | solution.py:75
  377.9 1.8 multiply_convert_fusion
  379.7 3.3 all_to_all.59
  383.3 26.5 %all_to_all.67 = bf16[4,256,1024]{1,2,0:T(8,128)(2,1)S(1)} all-to-all(bf16[4,256,1024]{1,2,0:T(8,128)(2,1)S(1)} %copy.66), channel_id=1, replica_groups=mesh['seq'=32,'head'=4] {'head'}, dimensions={0} | all-to-all | bytes 4194304 | tf_op jit(solution)/shard_map/all_to_all | solution.py:112
  409.8 2.8 copy.67
  (92 shorter events, 21.7 us)
Async XLA Ops:
  6.5 302.0 %copy-start = (f32[4096]{0:T(1024)S(1)}, f32[4096]{0:T(1024)}, u32[]{:S(2)}) copy-start(f32[4096]{0:T(1024)} %param.13) | copy-start | bytes 49156
  10.6 5.0 %copy-start.3 = (bf16[256,4096]{1,0:T(8,128)(2,1)S(1)}, bf16[256,4096]{1,0:T(8,128)(2,1)}, u32[]{:S(2)}) copy-start(bf16[256,4096]{1,0:T(8,128)(2,1)} %param.10) | copy-start | bytes 6291460
  10.6 30.8 %all-to-all-start.2 = ((bf16[256,4,1024]{0,2,1:T(8,128)(2,1)}), bf16[256,4,1024]{0,2,1:T(8,128)(2,1)}, u32[]{:S(2)}, u32[]{:S(2)}) async-start(bf16[256,4,1024]{0,2,1:T(8,128)(2,1)} %bitcast.7), calls=%async_computation.2 | async-start | bytes 4194304 | tf_op jit(solution)/shard_map/all_to_all | solution.py:97
  41.4 4.6 %copy-start.4 = (bf16[256,4096]{1,0:T(8,128)(2,1)S(1)}, bf16[256,4096]{1,0:T(8,128)(2,1)}, u32[]{:S(2)}) copy-start(bf16[256,4096]{1,0:T(8,128)(2,1)} %param.11) | copy-start | bytes 6291460
  41.5 29.3 %all-to-all-start = ((bf16[256,4,1024]{0,2,1:T(8,128)(2,1)}), bf16[256,4,1024]{0,2,1:T(8,128)(2,1)}, u32[]{:S(2)}, u32[]{:S(2)}) async-start(bf16[256,4,1024]{0,2,1:T(8,128)(2,1)} %bitcast.1), calls=%async_computation | async-start | bytes 4194304 | tf_op jit(solution)/shard_map/all_to_all | solution.py:98
  70.7 4.7 %copy-start.6 = (u32[128]{0:T(128)S(1)}, u32[128]{0:T(128)}, u32[]{:S(2)}) copy-start(u32[128]{0:T(128)} %constant.75) | copy-start | bytes 1540
  70.7 6.0 %copy-start.5 = (f32[32]{0:T(128)S(1)}, f32[32]{0:T(128)}, u32[]{:S(2)}) copy-start(f32[32]{0:T(128)} %param.12) | copy-start | bytes 388
  70.7 28.4 %all-to-all-start.1 = ((bf16[256,4,1024]{0,2,1:T(8,128)(2,1)}), bf16[256,4,1024]{0,2,1:T(8,128)(2,1)}, u32[]{:S(2)}, u32[]{:S(2)}) async-start(bf16[256,4,1024]{0,2,1:T(8,128)(2,1)} %bitcast.4), calls=%async_computation.1 | async-start | bytes 4194304 | tf_op jit(solution)/shard_map/all_to_all | solution.py:99
  75.3 255.6 %all-gather.4.cloned.1.call-start = ((), (), s32[]{:S(2)}) async-start(), calls=%async_computation.4 | async-start | bytes 17301504 | tf_op jit(solution)/shard_map/all_gather | solution.py:13
  238.3 0.8 copy-start.2
  409.8 2.9 copy-start.1
Sparse Core Ops, SparseCore 0:
  239.2 77.5 all-gather.3
where the time goes:
time: 426 us; the launch traced here: 420 us
  local copies, waits for them, and re-layouts  142 us (33%)
  blocking collectives  95.5 us (22%)
  waiting for transfers between devices  67.7 us (16%)
  other arithmetic  48 us (11%)
  matrix products  36.6 us (9%)
  between operations  14.3 us (3%)
  starting transfers between devices  14.2 us (3%)
    dynamic_update_slice x8, local copies, waits for them, and re-layouts, block_chain(): state, outputs = lax.scan(advance, start, (q_blocks, k_blocks, v_blocks))  103 us
    unnamed x1, blocking collectives  69 us
    select_n x32, other arithmetic, hop(): return jax.tree.map(lambda a, b: jnp.where(reached, a, b), new, before)  37.5 us
    all_to_all x1, blocking collectives, body(): lax.all_to_all(normed, 'head', split_axis=0, concat_axis=1, tiled=True)  26.5 us
    all_to_all x1, waiting for transfers between devices, body(): lax.all_to_all(queries, 'head', split_axis=1, concat_axis=0, tiled=True)  23.4 us
    all_to_all x1, waiting for transfers between devices, body(): lax.all_to_all(key_rows, 'head', split_axis=1, concat_axis=0, tiled=True)  22.2 us
    all_to_all x1, waiting for transfers between devices, body(): lax.all_to_all(value_rows, 'head', split_axis=1, concat_axis=0, tiled=True)  22.1 us
    unnamed x20, local copies, waits for them, and re-layouts  13.6 us
  transfers between devices with their start and end apart: 4, of which 3 were waited for; matrix products, arithmetic and copies ran while one was open for 7% of the time, Pallas kernels for 0%

commit v1 on v0

v1 whole, which is shorter than its diff:
```python
import jax
import jax.numpy as jnp
from jax import lax
from jax.sharding import PartitionSpec as P

HEADS = 32
HEAD_DIM = 128
BLOCK = 256
AXES = ("seq", "head")


def split_hi_lo(x):
    hi = x.astype(jnp.bfloat16)
    lo = (x - hi.astype(jnp.float32)).astype(jnp.bfloat16)
    return hi, lo


def dot_f32(a_bf16, b_f32, spec):
    hi, lo = split_hi_lo(b_f32)
    return jnp.einsum(spec, a_bf16, hi, preferred_element_type=jnp.float32) + jnp.einsum(
        spec, a_bf16, lo, preferred_element_type=jnp.float32
    )


def body(n, queries, key_rows, value_rows, decay_rates, norm_gain):
    span = queries.shape[0]
    shaped = (span, HEADS, HEAD_DIM)
    q = queries.reshape(shaped)
    k = key_rows.reshape(shaped)
    v = value_rows.reshape(shaped)
    me = lax.axis_index(AXES)

    positions = jnp.arange(span, dtype=jnp.float32)
    offsets = positions[:, None] - positions[None, :]
    within = jnp.where(
        offsets[None] >= 0.0,
        jnp.exp(-decay_rates[:, None, None] * jnp.maximum(offsets, 0.0)[None]),
        0.0,
    )
    q_decay = jnp.exp(-decay_rates[None, :] * (positions[:, None] + 1.0))[:, :, None]
    k_decay = jnp.exp(-decay_rates[None, :] * (span - 1.0 - positions[:, None]))[:, :, None]

    local_state = dot_f32(v, k.astype(jnp.float32) * k_decay, "jhf,jhe->hef")

    rows = HEADS * HEAD_DIM // n
    chunks = local_state.reshape(n, rows, HEAD_DIM)
    gathered = lax.all_to_all(chunks, AXES, 0, 0, tiled=True)
    head_of_chunk = me // (n // HEADS)
    rate = lax.dynamic_slice_in_dim(decay_rates, head_of_chunk, 1)[0]
    blocks = jnp.arange(n, dtype=jnp.float32)
    gaps = blocks[:, None] - 1.0 - blocks[None, :]
    chain = jnp.where(
        gaps >= 0.0, jnp.exp(-rate * float(span) * jnp.maximum(gaps, 0.0)), 0.0
    )
    before = jnp.einsum(
        "ab,bxy->axy", chain, gathered, precision=lax.Precision.HIGHEST
    )
    incoming = lax.all_to_all(before, AXES, 0, 0, tiled=True).reshape(
        HEADS, HEAD_DIM, HEAD_DIM
    )

    scores = jnp.einsum("ihe,jhe->hij", q, k, preferred_element_type=jnp.float32)
    weights = (scores * within).astype(jnp.bfloat16)
    intra = jnp.einsum("hij,jhe->ihe", weights, v, preferred_element_type=jnp.float32)
    inter = dot_f32(q, incoming, "ihe,hef->ihf") * q_decay
    total = intra + inter

    mean_square = jnp.mean(total * total, axis=-1, keepdims=True)
    gains = norm_gain.reshape(HEADS, HEAD_DIM)
    normed = (total * lax.rsqrt(mean_square + 1e-06) * gains).astype(jnp.bfloat16)
    return normed.reshape(span, HEADS * HEAD_DIM)


def solution(mesh):
    n = mesh.shape["seq"] * mesh.shape["head"]

    def run(queries, key_rows, value_rows, decay_rates, norm_gain):
        return body(n, queries, key_rows, value_rows, decay_rates, norm_gain)

    return jax.shard_map(
        run,
        mesh=mesh,
        in_specs=(
            P(AXES, None),
            P(AXES, None),
            P(AXES, None),
            P(),
            P(),
        ),
        out_specs=P(AXES, None),
        check_vma=False,
    )
```

time: 426 us -> 110 us (0.26); the launches traced: 420 us -> 109 us
  local copies, waits for them, and re-layouts: 142 us -> 15.5 us
  blocking collectives: 95.5 us -> 0 us
  other arithmetic: 48 us -> 2.77 us
  matrix products: 36.6 us -> 21 us
  waiting for transfers between devices: 67.7 us -> 52.4 us
  between operations: 14.3 us -> 0.74 us
    dynamic_update_slice x8 -> x0, local copies, waits for them, and re-layouts: 103 us -> none  [block_chain(): state, outputs = lax.scan(advance, start, (q_blocks, k_blocks, v_blocks))]
    unnamed x1 -> x0, blocking collectives: 69 us -> none
    select_n x32 -> x0, other arithmetic: 37.5 us -> none  [hop(): return jax.tree.map(lambda a, b: jnp.where(reached, a, b), new, before)]
    all_to_all x1 -> x0, blocking collectives: 26.5 us -> none  [body(): lax.all_to_all(normed, 'head', split_axis=0, concat_axis=1, tiled=True)]
    dot_general x13 -> x6, matrix products: 36.6 us -> 21 us  [the longest x1 7.29 us: body(): jnp.einsum('hij,jhe->ihe', weights, v, preferred_element_type=jnp.float32)]
    all_to_all x3 -> x2, waiting for transfers between devices: 67.6 us -> 52.4 us  [the longest x1 29.3 us: body(): gathered = lax.all_to_all(chunks, AXES, 0, 0, tiled=True)]
    unnamed x20 -> x14, local copies, waits for them, and re-layouts: 13.6 us -> 1.37 us
    dynamic_slice x12 -> x1, local copies, waits for them, and re-layouts: 7.26 us -> 0.59 us  [body(): rate = lax.dynamic_slice_in_dim(decay_rates, head_of_chunk, 1)[0]]
  transfers between devices with their start and end apart: 4 -> 2, of which waited for: 3 -> 2; matrix products, arithmetic and copies ran while one was open for 7% -> 7% of each run, Pallas kernels for 0% -> 0%
where the time goes in v1:
time: 110 us; the launch traced here: 109 us
  waiting for transfers between devices  52.4 us (48%)
  matrix products  21 us (19%)
  starting transfers between devices  16.9 us (15%)
  local copies, waits for them, and re-layouts  15.5 us (14%)
  other arithmetic  2.77 us (3%)
    all_to_all x1, waiting for transfers between devices, body(): gathered = lax.all_to_all(chunks, AXES, 0, 0, tiled=True)  29.3 us
    all_to_all x1, waiting for transfers between devices, body(): lax.all_to_all(before, AXES, 0, 0, tiled=True)  23.1 us
    all_to_all x1, starting transfers between devices, body(): gathered = lax.all_to_all(chunks, AXES, 0, 0, tiled=True)  12 us
    dot_general x1, matrix products, body(): jnp.einsum('hij,jhe->ihe', weights, v, preferred_element_type=jnp.float32)  7.29 us
    dot_general x2, matrix products, dot_f32(): jnp.einsum(spec, a_bf16, hi, preferred_element_type=jnp.float32)  5.54 us
    all_to_all x1, starting transfers between devices, body(): lax.all_to_all(before, AXES, 0, 0, tiled=True)  4.92 us
    dot_general x1, matrix products, body(): jnp.einsum('ab,bxy->axy', chain, gathered, precision=lax.Precision.HIGHEST)  4.55 us
    reshape x1, local copies, waits for them, and re-layouts, body(): k = key_rows.reshape(shaped)  4.06 us
  transfers between devices with their start and end apart: 2, of which 2 were waited for; matrix products, arithmetic and copies ran while one was open for 7% of the time, Pallas kernels for 0%

profile of v1, /device:TPU:1, one launch (start us, length us, event | category | flops | bytes accessed | tf_op | source)
XLA Modules:
  0.0 109.3 jit_solution(641359621320742586)
XLA Ops:
  0.0 0.0 copy-start
  0.0 0.8 neg.11
  0.8 4.1 %copy.38 = bf16[256,4096]{0,1:T(8,128)(2,1)} copy(bf16[256,4096]{1,0:T(8,128)(2,1)} %param.6) | data formatting | bytes 4194304 | tf_op jit(solution)/shard_map/reshape | solution.py:29
  4.9 0.1 multiply_exponential_fusion
  5.0 0.0 copy-start.1
  5.0 0.0 copy-start.3
  5.0 3.1 %fusion.9 = f32[32,128,128]{2,1,0:T(8,128)S(1)} fusion(bf16[256,32,128]{0,2,1:T(8,128)(2,1)} %bitcast.56, f32[256,32]{0,1:T(8,128)S(1)} %get-tuple-element.6, bf16[256,4096]{1,0:T(8,128)(2,1)} %param.7), kind=kOutput, calls=%fused_computation.14 | convolution fusion | flops 271581184 | bytes 6324224 | tf_op jit(solution)/shard_map/jhf,jhe->hef/dot_general | solution.py:20
  8.1 0.0 copy-done.1
  8.1 0.4 copy-done.3
  8.5 2.1 %fusion.24 = f32[32,128,128]{2,1,0:T(8,128)} fusion(f32[32,128,128]{2,1,0:T(8,128)S(1)} %fusion.9, bf16[256,32,128]{0,2,1:T(8,128)(2,1)S(1)} %bitcast.58, f32[256,32]{0,1:T(8,128)S(1)} %get-tuple-element.6, bf16[256,4096]{1,0:T(8,128)(2,1)S(1)} %copy-done.3), kind=kOutput, calls=%fused_computation.28 | convolution fusion | flops 275251200 | bytes 8421376 | tf_op jit(solution)/shard_map/jhf,jhe->hef/dot_general | solution.py:20
  10.6 0.0 copy-start.6
  10.6 12.0 %all-to-all-start = ((f32[128,32,128]{2,1,0:T(8,128)}), f32[128,32,128]{2,1,0:T(8,128)}, u32[]{:S(2)}, u32[]{:S(2)}) async-start(f32[128,32,128]{2,1,0:T(8,128)} %bitcast.60), calls=%async_computation | async-start | bytes 4194304 | tf_op jit(solution)/shard_map/all_to_all | solution.py:47
  22.6 0.0 copy-done.6
  22.6 0.6 dynamic_slice.3
  23.8 29.3 %all-to-all-done = f32[128,32,128]{2,1,0:T(8,128)} async-done(((f32[128,32,128]{2,1,0:T(8,128)}), f32[128,32,128]{2,1,0:T(8,128)}, u32[]{:S(2)}, u32[]{:S(2)}) %all-to-all-start) | async-done | bytes 2097184 | tf_op jit(solution)/shard_map/all_to_all | solution.py:47
  53.0 4.6 %fusion.20 = f32[128,32,128]{2,0,1:T(8,128)S(1)} fusion(f32[128,32,128]{2,1,0:T(8,128)} %all-to-all-done, f32[]{:T(128)} %bitcast.1, f32[128]{0:T(128)S(1)} %iota_add_fusion.1), kind=kOutput, calls=%fused_computation.23 | convolution fusion | flops 805388288 | bytes 4194820 | tf_op jit(solution)/shard_map/ab,bxy->axy/dot_general | solution.py:55
  57.6 2.6 %copy.32 = f32[128,32,128]{2,1,0:T(8,128)} copy(f32[128,32,128]{2,0,1:T(8,128)S(1)} %fusion.20) | data formatting | bytes 4194304 | tf_op jit(solution)/shard_map/ab,bxy->axy/dot_general | solution.py:55
  60.2 4.9 %all-to-all-start.1 = ((f32[128,32,128]{2,1,0:T(8,128)}), f32[128,32,128]{2,1,0:T(8,128)}, u32[]{:S(2)}, u32[]{:S(2)}) async-start(f32[128,32,128]{2,1,0:T(8,128)} %copy.32), calls=%async_computation.1 | async-start | bytes 4194304 | tf_op jit(solution)/shard_map/all_to_all | solution.py:58
  65.1 0.1 fusion.37
  65.2 0.1 fusion.36
  65.2 0.0 copy-done
  65.2 7.3 %fusion = f32[32,256,128]{1,2,0:T(8,128)} fusion(f32[256,256]{1,0:T(8,128)S(1)} %fusion.36, f32[32]{0:T(128)S(1)} %neg.11, pred[256,256]{1,0:T(8,128)(4,1)S(1)} %fusion.37, bf16[256,32,128]{0,2,1:T(8,128)(2,1)} %bitcast.57, bf16[256,4096]{1,0:T(8,128)(2,1)} %param.7, bf16[256,4096]{1,0:T(8,128)(2,1)S(1)} %copy-done), kind=kOutput, calls=%fused_computation.1 | convolution fusion | flops 1082130432 | bytes 10813568 | tf_op jit(solution)/shard_map/hij,jhe->ihe/dot_general | solution.py:64
  72.5 23.1 %all-to-all-done.1 = f32[128,32,128]{2,1,0:T(8,128)} async-done(((f32[128,32,128]{2,1,0:T(8,128)}), f32[128,32,128]{2,1,0:T(8,128)}, u32[]{:S(2)}, u32[]{:S(2)}) %all-to-all-start.1) | async-done | bytes 2097184 | tf_op jit(solution)/shard_map/all_to_all | solution.py:58
  95.7 2.9 %copy.33 = f32[32,128,128]{1,2,0:T(8,128)} copy(f32[32,128,128]{2,1,0:T(8,128)} %bitcast.4) | data formatting | bytes 4194304 | tf_op jit(solution)/shard_map/reshape | solution.py:58
  98.6 0.0 copy-start.2
  98.6 0.0 copy-start.4
  98.6 2.5 %fusion.16 = f32[32,128,256]{2,1,0:T(8,128)S(1)} fusion(f32[32,128,128]{1,2,0:T(8,128)} %copy.33, bf16[256,4096]{1,0:T(8,128)(2,1)S(1)} %copy-done), kind=kOutput, calls=%fused_computation.20 | convolution fusion | flops 268959744 | bytes 8388608 | tf_op jit(solution)/shard_map/ihe,hef->ihf/dot_general | solution.py:20
  101.0 0.0 copy-done.2
  101.0 1.0 copy-done.4
  102.0 0.0 copy-start.5
  102.0 1.5 %multiply_reduce_fusion = (f32[256,32]{0,1:T(8,128)S(1)}, f32[256,32,128]{0,2,1:T(8,128)S(1)}) fusion(f32[256,32]{0,1:T(8,128)S(1)} %get-tuple-element.5, f32[32,128,256]{2,1,0:T(8,128)S(1)} %fusion.16, f32[32,128,128]{1,2,0:T(8,128)S(1)} %copy-done.2, f32[32,256,128]{1,2,0:T(8,128)S(1)} %copy-done.4, bf16[256,4096]{1,0:T(8,128)(2,1)S(1)} %copy-done), kind=kOutput, calls=%fused_computation.5 | convolution fusion | flops 275767296 | bytes 16842752 | tf_op jit(solution)/shard_map/ihe,hef->ihf/dot_general | solution.py:20
  103.5 0.0 copy-done.5
  103.5 1.7 %multiply_convert_fusion.2 = bf16[256,32,128]{0,2,1:T(8,128)(2,1)} fusion(f32[256,32,128]{0,2,1:T(8,128)S(1)} %get-tuple-element.8, f32[32,128]{1,0:T(8,128)S(1)} %bitcast.61, f32[256,32]{0,1:T(8,128)S(1)} %add_rsqrt_fusion), kind=kLoop, calls=%fused_computation.4 | loop fusion | flops 3145728 | bytes 6340608 | tf_op jit(solution)/shard_map/convert_element_type | solution.py:70
  105.3 4.1 %copy.37 = bf16[256,4096]{1,0:T(8,128)(2,1)} copy(bf16[256,4096]{0,1:T(8,128)(2,1)} %bitcast.59) | data formatting | bytes 4194304 | tf_op jit(solution)/shard_map/reshape | solution.py:71
  (3 shorter events, 0.0 us)
Async XLA Ops:
  0.0 65.2 %copy-start = (bf16[256,4096]{1,0:T(8,128)(2,1)S(1)}, bf16[256,4096]{1,0:T(8,128)(2,1)}, u32[]{:S(2)}) copy-start(bf16[256,4096]{1,0:T(8,128)(2,1)} %param.5) | copy-start | bytes 6291460
  5.0 3.1 %copy-start.1 = (bf16[256,4096]{0,1:T(8,128)(2,1)S(1)}, bf16[256,4096]{0,1:T(8,128)(2,1)}, u32[]{:S(2)}) copy-start(bf16[256,4096]{0,1:T(8,128)(2,1)} %copy.38) | copy-start | bytes 6291460
  5.0 3.5 %copy-start.3 = (bf16[256,4096]{1,0:T(8,128)(2,1)S(1)}, bf16[256,4096]{1,0:T(8,128)(2,1)}, u32[]{:S(2)}) copy-start(bf16[256,4096]{1,0:T(8,128)(2,1)} %param.7) | copy-start | bytes 6291460
  10.6 12.0 %copy-start.6 = (f32[32]{0:T(128)S(1)}, f32[32]{0:T(128)}, u32[]{:S(2)}) copy-start(f32[32]{0:T(128)} %param.8) | copy-start | bytes 388
  10.6 42.4 %all-to-all-start = ((f32[128,32,128]{2,1,0:T(8,128)}), f32[128,32,128]{2,1,0:T(8,128)}, u32[]{:S(2)}, u32[]{:S(2)}) async-start(f32[128,32,128]{2,1,0:T(8,128)} %bitcast.60), calls=%async_computation | async-start | bytes 4194304 | tf_op jit(solution)/shard_map/all_to_all | solution.py:47
  60.2 35.5 %all-to-all-start.1 = ((f32[128,32,128]{2,1,0:T(8,128)}), f32[128,32,128]{2,1,0:T(8,128)}, u32[]{:S(2)}, u32[]{:S(2)}) async-start(f32[128,32,128]{2,1,0:T(8,128)} %copy.32), calls=%async_computation.1 | async-start | bytes 4194304 | tf_op jit(solution)/shard_map/all_to_all | solution.py:58
  98.6 2.5 %copy-start.2 = (f32[32,128,128]{1,2,0:T(8,128)S(1)}, f32[32,128,128]{1,2,0:T(8,128)}, u32[]{:S(2)}) copy-start(f32[32,128,128]{1,2,0:T(8,128)} %copy.33) | copy-start | bytes 6291460
  98.6 3.5 %copy-start.4 = (f32[32,256,128]{1,2,0:T(8,128)S(1)}, f32[32,256,128]{1,2,0:T(8,128)}, u32[]{:S(2)}) copy-start(f32[32,256,128]{1,2,0:T(8,128)} %fusion) | copy-start | bytes 12582916
  102.0 1.5 %copy-start.5 = (f32[4096]{0:T(1024)S(1)}, f32[4096]{0:T(1024)}, u32[]{:S(2)}) copy-start(f32[4096]{0:T(1024)} %param.9) | copy-start | bytes 49156

commit v2 on v1

--- a/solution.py
+++ b/solution.py
@@ -10,9 +10,8 @@
 
 
 def split_hi_lo(x):
-    hi = x.astype(jnp.bfloat16)
-    lo = (x - hi.astype(jnp.float32)).astype(jnp.bfloat16)
-    return hi, lo
+    hi = lax.reduce_precision(x, exponent_bits=8, mantissa_bits=7)
+    return hi.astype(jnp.bfloat16), (x - hi).astype(jnp.bfloat16)
 
 
 def dot_f32(a_bf16, b_f32, spec):

time: 110 us -> 110 us (level)
    dot_general x2, matrix products: 3.62 us -> 4.81 us  [dot_f32(): jnp.einsum(spec, a_bf16, lo, preferred_element_type=jnp.float32)]
where the time goes in v2:
time: 110 us; the launch traced here: 109 us
  waiting for transfers between devices  52.4 us (48%)
  matrix products  21.2 us (19%)
  starting transfers between devices  16.9 us (15%)
  local copies, waits for them, and re-layouts  15.3 us (14%)
  other arithmetic  2.77 us (3%)
    all_to_all x1, waiting for transfers between devices, body(): gathered = lax.all_to_all(chunks, AXES, 0, 0, tiled=True)  29.3 us
    all_to_all x1, waiting for transfers between devices, body(): lax.all_to_all(before, AXES, 0, 0, tiled=True)  23.1 us
    all_to_all x1, starting transfers between devices, body(): gathered = lax.all_to_all(chunks, AXES, 0, 0, tiled=True)  12 us
    dot_general x1, matrix products, body(): jnp.einsum('hij,jhe->ihe', weights, v, preferred_element_type=jnp.float32)  7.29 us
    all_to_all x1, starting transfers between devices, body(): lax.all_to_all(before, AXES, 0, 0, tiled=True)  4.92 us
    dot_general x2, matrix products, dot_f32(): jnp.einsum(spec, a_bf16, lo, preferred_element_type=jnp.float32)  4.81 us
    dot_general x2, matrix products, dot_f32(): jnp.einsum(spec, a_bf16, hi, preferred_element_type=jnp.float32)  4.58 us
    dot_general x1, matrix products, body(): jnp.einsum('ab,bxy->axy', chain, gathered, precision=lax.Precision.HIGHEST)  4.56 us
  transfers between devices with their start and end apart: 2, of which 2 were waited for; matrix products, arithmetic and copies ran while one was open for 7% of the time, Pallas kernels for 0%

profile of v2, /device:TPU:1, one launch (start us, length us, event | category | flops | bytes accessed | tf_op | source)
XLA Modules:
  0.0 109.4 jit_solution(9775353391292727102)
XLA Ops:
  0.0 0.0 copy-start
  0.0 0.8 neg.11
  0.8 4.1 %copy.38 = bf16[256,4096]{0,1:T(8,128)(2,1)} copy(bf16[256,4096]{1,0:T(8,128)(2,1)} %param.6) | data formatting | bytes 4194304 | tf_op jit(solution)/shard_map/reshape | solution.py:28
  4.9 0.1 multiply_exponential_fusion
  5.0 0.0 copy-start.2
  5.0 0.0 copy-start.4
  5.0 3.3 %fusion.10 = f32[32,128,128]{2,1,0:T(8,128)S(1)} fusion(bf16[256,32,128]{0,2,1:T(8,128)(2,1)} %bitcast.57, f32[256,32]{0,1:T(8,128)S(1)} %get-tuple-element.6, bf16[256,4096]{1,0:T(8,128)(2,1)} %param.7), kind=kOutput, calls=%fused_computation.18 | convolution fusion | flops 273678336 | bytes 6324224 | tf_op jit(solution)/shard_map/jhf,jhe->hef/dot_general | solution.py:19
  8.3 0.0 copy-done.2
  8.3 0.2 copy-done.4
  8.5 2.1 %fusion.25 = f32[32,128,128]{2,1,0:T(8,128)} fusion(f32[32,128,128]{2,1,0:T(8,128)S(1)} %fusion.10, bf16[256,32,128]{0,2,1:T(8,128)(2,1)S(1)} %bitcast.59, f32[256,32]{0,1:T(8,128)S(1)} %get-tuple-element.6, bf16[256,4096]{1,0:T(8,128)(2,1)S(1)} %copy-done.4), kind=kOutput, calls=%fused_computation.31 | convolution fusion | flops 273154048 | bytes 8421376 | tf_op jit(solution)/shard_map/jhf,jhe->hef/dot_general | solution.py:19
  10.6 0.0 copy-start.6
  10.6 12.0 %all-to-all-start = ((f32[128,32,128]{2,1,0:T(8,128)}), f32[128,32,128]{2,1,0:T(8,128)}, u32[]{:S(2)}, u32[]{:S(2)}) async-start(f32[128,32,128]{2,1,0:T(8,128)} %bitcast.60), calls=%async_computation | async-start | bytes 4194304 | tf_op jit(solution)/shard_map/all_to_all | solution.py:46
  22.6 0.0 copy-done.6
  22.6 0.6 dynamic_slice.3
  23.8 29.3 %all-to-all-done = f32[128,32,128]{2,1,0:T(8,128)} async-done(((f32[128,32,128]{2,1,0:T(8,128)}), f32[128,32,128]{2,1,0:T(8,128)}, u32[]{:S(2)}, u32[]{:S(2)}) %all-to-all-start) | async-done | bytes 2097184 | tf_op jit(solution)/shard_map/all_to_all | solution.py:46
  53.0 4.6 %fusion.21 = f32[128,32,128]{2,0,1:T(8,128)S(1)} fusion(f32[128,32,128]{2,1,0:T(8,128)} %all-to-all-done, f32[]{:T(128)} %bitcast.1, f32[128]{0:T(128)S(1)} %iota_add_fusion.1), kind=kOutput, calls=%fused_computation.27 | convolution fusion | flops 805388288 | bytes 4194820 | tf_op jit(solution)/shard_map/ab,bxy->axy/dot_general | solution.py:54
  57.6 2.6 %copy.32 = f32[128,32,128]{2,1,0:T(8,128)} copy(f32[128,32,128]{2,0,1:T(8,128)S(1)} %fusion.21) | data formatting | bytes 4194304 | tf_op jit(solution)/shard_map/ab,bxy->axy/dot_general | solution.py:54
  60.1 4.9 %all-to-all-start.1 = ((f32[128,32,128]{2,1,0:T(8,128)}), f32[128,32,128]{2,1,0:T(8,128)}, u32[]{:S(2)}, u32[]{:S(2)}) async-start(f32[128,32,128]{2,1,0:T(8,128)} %copy.32), calls=%async_computation.1 | async-start | bytes 4194304 | tf_op jit(solution)/shard_map/all_to_all | solution.py:57
  65.1 0.1 fusion.37
  65.2 0.1 fusion.36
  65.2 0.0 copy-done
  65.2 7.3 %fusion.1 = f32[32,256,128]{1,2,0:T(8,128)} fusion(f32[256,256]{1,0:T(8,128)S(1)} %fusion.36, f32[32]{0:T(128)S(1)} %neg.11, pred[256,256]{1,0:T(8,128)(4,1)S(1)} %fusion.37, bf16[256,32,128]{0,2,1:T(8,128)(2,1)} %bitcast.58, bf16[256,4096]{1,0:T(8,128)(2,1)} %param.7, bf16[256,4096]{1,0:T(8,128)(2,1)S(1)} %copy-done), kind=kOutput, calls=%fused_computation.4 | convolution fusion | flops 1082130432 | bytes 10813568 | tf_op jit(solution)/shard_map/hij,jhe->ihe/dot_general | solution.py:63
  72.5 23.1 %all-to-all-done.1 = f32[128,32,128]{2,1,0:T(8,128)} async-done(((f32[128,32,128]{2,1,0:T(8,128)}), f32[128,32,128]{2,1,0:T(8,128)}, u32[]{:S(2)}, u32[]{:S(2)}) %all-to-all-start.1) | async-done | bytes 2097184 | tf_op jit(solution)/shard_map/all_to_all | solution.py:57
  95.7 2.9 %copy.33 = f32[32,128,128]{1,2,0:T(8,128)} copy(f32[32,128,128]{2,1,0:T(8,128)} %bitcast.4) | data formatting | bytes 4194304 | tf_op jit(solution)/shard_map/reshape | solution.py:57
  98.5 0.0 copy-start.1
  98.5 0.0 copy-start.3
  98.5 2.5 %fusion.17 = f32[32,128,256]{2,1,0:T(8,128)S(1)} fusion(f32[32,128,128]{1,2,0:T(8,128)} %copy.33, bf16[256,4096]{1,0:T(8,128)(2,1)S(1)} %copy-done), kind=kOutput, calls=%fused_computation.24 | convolution fusion | flops 269484032 | bytes 8388608 | tf_op jit(solution)/shard_map/ihe,hef->ihf/dot_general | solution.py:19
  101.0 0.0 copy-done.1
  101.0 1.0 copy-done.3
  102.0 0.0 copy-start.5
  102.0 1.5 %multiply_reduce_fusion = (f32[256,32]{0,1:T(8,128)S(1)}, f32[256,32,128]{0,2,1:T(8,128)S(1)}) fusion(f32[256,32]{0,1:T(8,128)S(1)} %get-tuple-element.5, f32[32,128,256]{2,1,0:T(8,128)S(1)} %fusion.17, f32[32,128,128]{1,2,0:T(8,128)S(1)} %copy-done.1, f32[32,256,128]{1,2,0:T(8,128)S(1)} %copy-done.3, bf16[256,4096]{1,0:T(8,128)(2,1)S(1)} %copy-done), kind=kOutput, calls=%fused_computation.8 | convolution fusion | flops 275243008 | bytes 16842752 | tf_op jit(solution)/shard_map/ihe,hef->ihf/dot_general | solution.py:19
  103.6 0.0 copy-done.5
  103.6 1.7 %multiply_convert_fusion.2 = bf16[256,32,128]{0,2,1:T(8,128)(2,1)} fusion(f32[256,32,128]{0,2,1:T(8,128)S(1)} %get-tuple-element.8, f32[32,128]{1,0:T(8,128)S(1)} %bitcast.61, f32[256,32]{0,1:T(8,128)S(1)} %add_rsqrt_fusion), kind=kLoop, calls=%fused_computation.7 | loop fusion | flops 3145728 | bytes 6340608 | tf_op jit(solution)/shard_map/convert_element_type | solution.py:69
  105.3 4.1 %copy.37 = bf16[256,4096]{1,0:T(8,128)(2,1)} copy(bf16[256,4096]{0,1:T(8,128)(2,1)} %bitcast.56) | data formatting | bytes 4194304 | tf_op jit(solution)/shard_map/reshape | solution.py:70
  (3 shorter events, 0.0 us)
Async XLA Ops:
  0.0 65.2 %copy-start = (bf16[256,4096]{1,0:T(8,128)(2,1)S(1)}, bf16[256,4096]{1,0:T(8,128)(2,1)}, u32[]{:S(2)}) copy-start(bf16[256,4096]{1,0:T(8,128)(2,1)} %param.5) | copy-start | bytes 6291460
  5.0 3.3 %copy-start.2 = (bf16[256,4096]{0,1:T(8,128)(2,1)S(1)}, bf16[256,4096]{0,1:T(8,128)(2,1)}, u32[]{:S(2)}) copy-start(bf16[256,4096]{0,1:T(8,128)(2,1)} %copy.38) | copy-start | bytes 6291460
  5.0 3.5 %copy-start.4 = (bf16[256,4096]{1,0:T(8,128)(2,1)S(1)}, bf16[256,4096]{1,0:T(8,128)(2,1)}, u32[]{:S(2)}) copy-start(bf16[256,4096]{1,0:T(8,128)(2,1)} %param.7) | copy-start | bytes 6291460
  10.6 12.0 %copy-start.6 = (f32[32]{0:T(128)S(1)}, f32[32]{0:T(128)}, u32[]{:S(2)}) copy-start(f32[32]{0:T(128)} %param.8) | copy-start | bytes 388
  10.6 42.4 %all-to-all-start = ((f32[128,32,128]{2,1,0:T(8,128)}), f32[128,32,128]{2,1,0:T(8,128)}, u32[]{:S(2)}, u32[]{:S(2)}) async-start(f32[128,32,128]{2,1,0:T(8,128)} %bitcast.60), calls=%async_computation | async-start | bytes 4194304 | tf_op jit(solution)/shard_map/all_to_all | solution.py:46
  60.1 35.5 %all-to-all-start.1 = ((f32[128,32,128]{2,1,0:T(8,128)}), f32[128,32,128]{2,1,0:T(8,128)}, u32[]{:S(2)}, u32[]{:S(2)}) async-start(f32[128,32,128]{2,1,0:T(8,128)} %copy.32), calls=%async_computation.1 | async-start | bytes 4194304 | tf_op jit(solution)/shard_map/all_to_all | solution.py:57
  98.5 2.5 %copy-start.1 = (f32[32,128,128]{1,2,0:T(8,128)S(1)}, f32[32,128,128]{1,2,0:T(8,128)}, u32[]{:S(2)}) copy-start(f32[32,128,128]{1,2,0:T(8,128)} %copy.33) | copy-start | bytes 6291460
  98.5 3.5 %copy-start.3 = (f32[32,256,128]{1,2,0:T(8,128)S(1)}, f32[32,256,128]{1,2,0:T(8,128)}, u32[]{:S(2)}) copy-start(f32[32,256,128]{1,2,0:T(8,128)} %fusion.1) | copy-start | bytes 12582916
  102.0 1.6 %copy-start.5 = (f32[4096]{0:T(1024)S(1)}, f32[4096]{0:T(1024)}, u32[]{:S(2)}) copy-start(f32[4096]{0:T(1024)} %param.9) | copy-start | bytes 49156

commit v3 on v2

v3 whole, which is shorter than its diff:
```python
import jax
import jax.numpy as jnp
from jax import lax
from jax.experimental import pallas as pl
from jax.experimental.pallas import tpu as pltpu
from jax.sharding import PartitionSpec as P

HEADS = 32
HEAD_DIM = 128
BLOCK = 256
AXES = ("seq", "head")
GROUP = 8


def split_hi_lo(x):
    hi = lax.reduce_precision(x, exponent_bits=8, mantissa_bits=7)
    return hi.astype(jnp.bfloat16), (x - hi).astype(jnp.bfloat16)


def kernel_split(x):
    hi = x.astype(jnp.bfloat16)
    return hi, (x - hi.astype(jnp.float32)).astype(jnp.bfloat16)


def state_kernel(rates_ref, k_ref, v_ref, out_ref):
    g = pl.program_id(0)
    span = k_ref.shape[0]
    tail = (span - 1.0) - lax.broadcasted_iota(jnp.int32, (span, 1), 0).astype(jnp.float32)
    for hh in range(GROUP):
        rate = rates_ref[g * GROUP + hh]
        cols = slice(hh * HEAD_DIM, (hh + 1) * HEAD_DIM)
        kd = k_ref[:, cols].astype(jnp.float32) * jnp.exp(-rate * tail)
        hi, lo = kernel_split(kd)
        v = v_ref[:, cols]
        dims = (((0,), (0,)), ((), ()))
        out_ref[hh] = lax.dot_general(
            hi, v, dims, preferred_element_type=jnp.float32
        ) + lax.dot_general(lo, v, dims, preferred_element_type=jnp.float32)


def block_state(decay_rates, k, v):
    span = k.shape[0]
    groups = HEADS // GROUP
    width = GROUP * HEAD_DIM
    return pl.pallas_call(
        state_kernel,
        grid=(groups,),
        in_specs=[
            pl.BlockSpec(memory_space=pltpu.SMEM),
            pl.BlockSpec((span, width), lambda g: (0, g)),
            pl.BlockSpec((span, width), lambda g: (0, g)),
        ],
        out_specs=pl.BlockSpec((GROUP, HEAD_DIM, HEAD_DIM), lambda g: (g, 0, 0)),
        out_shape=jax.ShapeDtypeStruct((HEADS, HEAD_DIM, HEAD_DIM), jnp.float32),
        cost_estimate=pl.CostEstimate(
            flops=4 * span * HEADS * HEAD_DIM * HEAD_DIM,
            transcendentals=span * HEADS * HEAD_DIM,
            bytes_accessed=2 * 2 * span * HEADS * HEAD_DIM + 4 * HEADS * HEAD_DIM * HEAD_DIM,
        ),
    )(decay_rates, k, v)


def output_kernel(rates_ref, q_ref, k_ref, v_ref, s_ref, gain_ref, out_ref):
    g = pl.program_id(0)
    span = q_ref.shape[0]
    rows = lax.broadcasted_iota(jnp.int32, (span, span), 0).astype(jnp.float32)
    cols_i = lax.broadcasted_iota(jnp.int32, (span, span), 1).astype(jnp.float32)
    offsets = rows - cols_i
    causal = offsets >= 0.0
    gap = jnp.maximum(offsets, 0.0)
    lead = lax.broadcasted_iota(jnp.int32, (span, 1), 0).astype(jnp.float32) + 1.0
    for hh in range(GROUP):
        rate = rates_ref[g * GROUP + hh]
        cols = slice(hh * HEAD_DIM, (hh + 1) * HEAD_DIM)
        q = q_ref[:, cols]
        k = k_ref[:, cols]
        v = v_ref[:, cols]
        scores = lax.dot_general(
            q, k, (((1,), (1,)), ((), ())), preferred_element_type=jnp.float32
        )
        within = jnp.where(causal, jnp.exp(-rate * gap), 0.0)
        weights = (scores * within).astype(jnp.bfloat16)
        intra = jnp.dot(weights, v, preferred_element_type=jnp.float32)
        hi, lo = kernel_split(s_ref[hh])
        inter = jnp.dot(q, hi, preferred_element_type=jnp.float32) + jnp.dot(
            q, lo, preferred_element_type=jnp.float32
        )
        total = intra + inter * jnp.exp(-rate * lead)
        mean_square = jnp.mean(total * total, axis=-1, keepdims=True)
        normed = total * lax.rsqrt(mean_square + 1e-06) * gain_ref[hh : hh + 1, :]
        out_ref[:, cols] = normed.astype(out_ref.dtype)


def block_output(decay_rates, q, k, v, incoming, gains):
    span = q.shape[0]
    groups = HEADS // GROUP
    width = GROUP * HEAD_DIM
    return pl.pallas_call(
        output_kernel,
        grid=(groups,),
        in_specs=[
            pl.BlockSpec(memory_space=pltpu.SMEM),
            pl.BlockSpec((span, width), lambda g: (0, g)),
            pl.BlockSpec((span, width), lambda g: (0, g)),
            pl.BlockSpec((span, width), lambda g: (0, g)),
            pl.BlockSpec((GROUP, HEAD_DIM, HEAD_DIM), lambda g: (g, 0, 0)),
            pl.BlockSpec((GROUP, HEAD_DIM), lambda g: (g, 0)),
        ],
        out_specs=pl.BlockSpec((span, width), lambda g: (0, g)),
        out_shape=jax.ShapeDtypeStruct((span, HEADS * HEAD_DIM), jnp.bfloat16),
        cost_estimate=pl.CostEstimate(
            flops=HEADS * (4 * span * span * HEAD_DIM + 4 * span * HEAD_DIM * HEAD_DIM),
            transcendentals=HEADS * span * span,
            bytes_accessed=4 * 2 * span * HEADS * HEAD_DIM + 4 * HEADS * HEAD_DIM * HEAD_DIM,
        ),
    )(decay_rates, q, k, v, incoming, gains)


def body(n, queries, key_rows, value_rows, decay_rates, norm_gain):
    span = queries.shape[0]
    me = lax.axis_index(AXES)

    local_state = block_state(decay_rates, key_rows, value_rows)

    rows = HEADS * HEAD_DIM // n
    chunks = local_state.reshape(n, rows, HEAD_DIM)
    gathered = lax.all_to_all(chunks, AXES, 0, 0, tiled=True)
    head_of_chunk = me // (n // HEADS)
    rate = lax.dynamic_slice_in_dim(decay_rates, head_of_chunk, 1)[0]
    blocks = jnp.arange(n, dtype=jnp.float32)
    gaps = blocks[:, None] - 1.0 - blocks[None, :]
    chain = jnp.where(
        gaps >= 0.0, jnp.exp(-rate * float(span) * jnp.maximum(gaps, 0.0)), 0.0
    )
    c_hi, c_lo = split_hi_lo(chain)
    g_hi, g_lo = split_hi_lo(gathered)
    spec = "ab,bxy->axy"
    before = (
        jnp.einsum(spec, c_hi, g_hi, preferred_element_type=jnp.float32)
        + jnp.einsum(spec, c_lo, g_hi, preferred_element_type=jnp.float32)
        + jnp.einsum(spec, c_hi, g_lo, preferred_element_type=jnp.float32)
    )
    incoming = lax.all_to_all(before, AXES, 0, 0, tiled=True).reshape(
        HEADS, HEAD_DIM, HEAD_DIM
    )

    gains = norm_gain.reshape(HEADS, HEAD_DIM)
    return block_output(decay_rates, queries, key_rows, value_rows, incoming, gains)


def solution(mesh):
    n = mesh.shape["seq"] * mesh.shape["head"]

    def run(queries, key_rows, value_rows, decay_rates, norm_gain):
        return body(n, queries, key_rows, value_rows, decay_rates, norm_gain)

    return jax.shard_map(
        run,
        mesh=mesh,
        in_specs=(
            P(AXES, None),
            P(AXES, None),
            P(AXES, None),
            P(),
            P(),
        ),
        out_specs=P(AXES, None),
        check_vma=False,
    )
```

time: 110 us -> 96.7 us (0.88)
  blocking collectives: 0 us -> 34.8 us
  waiting for transfers between devices: 52.4 us -> 29.5 us
  matrix products: 21.2 us -> 4.44 us
  Pallas kernels: 0 us -> 13.5 us
  local copies, waits for them, and re-layouts: 15.3 us -> 1.87 us
  starting transfers between devices: 16.9 us -> 11.5 us
  other arithmetic: 2.77 us -> 0.01 us
    all_to_all x0 -> x1, blocking collectives: none -> 34.8 us  [body(): lax.all_to_all(before, AXES, 0, 0, tiled=True)]
    all_to_all x1 -> x0, waiting for transfers between devices: 23.1 us -> none  [body(): lax.all_to_all(before, AXES, 0, 0, tiled=True)]
    dot_general x6 -> x3, matrix products: 21.2 us -> 4.44 us  [the longest x1 1.61 us: body(): jnp.einsum(spec, c_hi, g_lo, preferred_element_type=jnp.float32)]
    pallas_call x0 -> x2, Pallas kernels: none -> 13.5 us  [the longest x1 8.31 us: block_output(): pl.pallas_call(output_kernel, grid=(groups,), in_specs=[pl.BlockSpec(memo...]
    reshape x3 -> x0, local copies, waits for them, and re-layouts: 11 us -> none  [the longest x1 4.06 us: body(): k = key_rows.reshape(shaped)]
    all_to_all x1 -> x0, starting transfers between devices: 4.92 us -> none  [body(): lax.all_to_all(before, AXES, 0, 0, tiled=True)]
    dot_general x1 -> x0, local copies, waits for them, and re-layouts: 2.56 us -> none  [body(): jnp.einsum('ab,bxy->axy', chain, gathered, precision=lax.Precision.HIGHEST)]
    convert_element_type x1 -> x0, other arithmetic: 1.71 us -> none  [body(): (total * lax.rsqrt(mean_square + 1e-06) * gains).astype(jnp.bfloat16)]
  transfers between devices with their start and end apart: 2 -> 1, of which waited for: 2 -> 1; matrix products, arithmetic and copies ran while one was open for 7% -> 1% of each run, Pallas kernels for 0% -> 0%
where the time goes in v3:
time: 96.7 us; the launch traced here: 96.4 us
  blocking collectives  34.8 us (36%)
  waiting for transfers between devices  29.5 us (31%)
  Pallas kernels  13.5 us (14%)
  starting transfers between devices  11.5 us (12%)
  matrix products  4.44 us (5%)
  local copies, waits for them, and re-layouts  1.87 us (2%)
    all_to_all x1, blocking collectives, body(): lax.all_to_all(before, AXES, 0, 0, tiled=True)  34.8 us
    all_to_all x1, waiting for transfers between devices, body(): gathered = lax.all_to_all(chunks, AXES, 0, 0, tiled=True)  29.5 us
    all_to_all x1, starting transfers between devices, body(): gathered = lax.all_to_all(chunks, AXES, 0, 0, tiled=True)  11.5 us
    pallas_call x1, Pallas kernels, block_output(): pl.pallas_call(output_kernel, grid=(groups,), in_specs=[pl.BlockSpec(memo...  8.31 us
    pallas_call x1, Pallas kernels, block_state(): pl.pallas_call(state_kernel, grid=(groups,), in_specs=[pl.BlockSpec(memor...  5.19 us
  transfers between devices with their start and end apart: 1, of which 1 were waited for; matrix products, arithmetic and copies ran while one was open for 1% of the time, Pallas kernels for 0%

profile of v3, /device:TPU:1, one launch (start us, length us, event | category | flops | bytes accessed | tf_op | source)
XLA Modules:
  0.0 96.4 jit_solution(15206883409514345005)
XLA Ops:
  0.0 5.2 %shard_map.55 = f32[32,128,128]{2,1,0:T(8,128)} custom-call(f32[32]{0:T(128)} %rates_ref.3, bf16[256,4096]{1,0:T(8,128)(2,1)} %k_ref.3, bf16[256,4096]{1,0:T(8,128)(2,1)} %v_ref.3), custom_call_target="tpu_custom_call" | custom-call | flops 536870912 | bytes 6291456 | tf_op jit(solution)/shard_map/pallas_call | solution.py:45
  5.2 0.0 copy-start
  5.2 11.5 %all-to-all-start = ((f32[128,32,128]{2,1,0:T(8,128)}), f32[128,32,128]{2,1,0:T(8,128)S(1)}, u32[]{:S(2)}, u32[]{:S(2)}) async-start(f32[128,32,128]{2,1,0:T(8,128)} %bitcast.11), calls=%async_computation | async-start | bytes 4194304 | tf_op jit(solution)/shard_map/all_to_all | solution.py:127
  16.7 0.0 copy-done
  16.7 0.7 dynamic_slice.3
  18.0 29.5 %all-to-all-done = f32[128,32,128]{2,1,0:T(8,128)S(1)} async-done(((f32[128,32,128]{2,1,0:T(8,128)}), f32[128,32,128]{2,1,0:T(8,128)S(1)}, u32[]{:S(2)}, u32[]{:S(2)}) %all-to-all-start) | async-done | bytes 2097184 | tf_op jit(solution)/shard_map/all_to_all | solution.py:127
  47.5 1.4 %fusion.2 = f32[128,32,128]{2,0,1:T(8,128)S(1)} fusion(f32[128,32,128]{2,1,0:T(8,128)S(1)} %all-to-all-done, f32[]{:T(128)} %bitcast, f32[128]{0:T(128)S(1)} %iota_add_fusion), kind=kOutput, calls=%fused_computation.4 | convolution fusion | flops 135397376 | bytes 4194820 | tf_op jit(solution)/shard_map/ab,bxy->axy/dot_general | solution.py:140
  48.9 1.4 %fusion.3 = f32[128,32,128]{2,0,1:T(8,128)S(1)} fusion(f32[128,32,128]{2,1,0:T(8,128)S(1)} %all-to-all-done, f32[]{:T(128)} %bitcast, f32[128]{0:T(128)S(1)} %iota_add_fusion), kind=kOutput, calls=%fused_computation.5 | convolution fusion | flops 135380992 | bytes 4194820 | tf_op jit(solution)/shard_map/ab,bxy->axy/dot_general | solution.py:139
  50.4 1.6 %add_add_fusion = f32[128,32,128]{2,0,1:T(8,128)S(1)} fusion(f32[128,32,128]{2,0,1:T(8,128)S(1)} %fusion.3, f32[128,32,128]{2,0,1:T(8,128)S(1)} %fusion.2, f32[128,32,128]{2,1,0:T(8,128)S(1)} %all-to-all-done, f32[]{:T(128)} %bitcast, f32[128]{0:T(128)S(1)} %iota_add_fusion), kind=kOutput, calls=%fused_computation.3 | convolution fusion | flops 136953856 | bytes 8389124 | tf_op jit(solution)/shard_map/ab,bxy->axy/dot_general | solution.py:141
  52.0 1.2 %copy.10 = f32[128,32,128]{2,1,0:T(8,128)S(1)} copy(f32[128,32,128]{2,0,1:T(8,128)S(1)} %add_add_fusion) | data formatting | bytes 4194304 | tf_op jit(solution)/shard_map/add | solution.py:139
  53.2 34.8 %all_to_all.10 = f32[128,32,128]{2,1,0:T(8,128)} all-to-all(f32[128,32,128]{2,1,0:T(8,128)S(1)} %copy.10), channel_id=1, replica_groups=mesh['seq'=32,'head'=4] {'seq','head'}, dimensions={0} | all-to-all | bytes 4194304 | tf_op jit(solution)/shard_map/all_to_all | solution.py:143
  88.0 8.3 %shard_map.56 = bf16[256,4096]{1,0:T(8,128)(2,1)} custom-call(f32[32]{0:T(128)} %rates_ref.3, bf16[256,4096]{1,0:T(8,128)(2,1)} %q_ref.1, bf16[256,4096]{1,0:T(8,128)(2,1)} %k_ref.3, bf16[256,4096]{1,0:T(8,128)(2,1)} %v_ref.3, f32[32,128,128]{2,1,0:T(8,128)} %bitcast.12, f32[32,128]{1,0:T(8,128)} %bitcast.13), custom_call_target="tpu_custom_call" | custom-call | flops 1610612736 | bytes 10485760 | tf_op jit(solution)/shard_map/pallas_call | solution.py:98
  (1 shorter events, 0.0 us)
Async XLA Ops:
  5.2 11.5 %copy-start = (f32[32]{0:T(128)S(1)}, f32[32]{0:T(128)}, u32[]{:S(2)}) copy-start(f32[32]{0:T(128)} %rates_ref.3) | copy-start | bytes 388
  5.2 42.3 %all-to-all-start = ((f32[128,32,128]{2,1,0:T(8,128)}), f32[128,32,128]{2,1,0:T(8,128)S(1)}, u32[]{:S(2)}, u32[]{:S(2)}) async-start(f32[128,32,128]{2,1,0:T(8,128)} %bitcast.11), calls=%async_computation | async-start | bytes 4194304 | tf_op jit(solution)/shard_map/all_to_all | solution.py:127

commit v4 on v3

--- a/solution.py
+++ b/solution.py
@@ -10,6 +10,7 @@
 BLOCK = 256
 AXES = ("seq", "head")
 GROUP = 8
+CHAIN_BLOCKS = 128
 
 
 def split_hi_lo(x):
@@ -60,7 +61,7 @@
     )(decay_rates, k, v)
 
 
-def output_kernel(rates_ref, q_ref, k_ref, v_ref, s_ref, gain_ref, out_ref):
+def intra_kernel(rates_ref, q_ref, k_ref, v_ref, out_ref):
     g = pl.program_id(0)
     span = q_ref.shape[0]
     rows = lax.broadcasted_iota(jnp.int32, (span, span), 0).astype(jnp.float32)
@@ -68,30 +69,61 @@
     offsets = rows - cols_i
     causal = offsets >= 0.0
     gap = jnp.maximum(offsets, 0.0)
+    for hh in range(GROUP):
+        rate = rates_ref[g * GROUP + hh]
+        cols = slice(hh * HEAD_DIM, (hh + 1) * HEAD_DIM)
+        q = q_ref[:, cols]
+        k = k_ref[:, cols]
+        scores = lax.dot_general(
+            q, k, (((1,), (1,)), ((), ())), preferred_element_type=jnp.float32
+        )
+        within = jnp.where(causal, jnp.exp(-rate * gap), 0.0)
+        weights = (scores * within).astype(jnp.bfloat16)
+        out_ref[:, cols] = jnp.dot(weights, v_ref[:, cols], preferred_element_type=jnp.float32)
+
+
+def block_intra(decay_rates, q, k, v):
+    span = q.shape[0]
+    groups = HEADS // GROUP
+    width = GROUP * HEAD_DIM
+    return pl.pallas_call(
+        intra_kernel,
+        grid=(groups,),
+        in_specs=[
+            pl.BlockSpec(memory_space=pltpu.SMEM),
+            pl.BlockSpec((span, width), lambda g: (0, g)),
+            pl.BlockSpec((span, width), lambda g: (0, g)),
+            pl.BlockSpec((span, width), lambda g: (0, g)),
+        ],
+        out_specs=pl.BlockSpec((span, width), lambda g: (0, g)),
+        out_shape=jax.ShapeDtypeStruct((span, HEADS * HEAD_DIM), jnp.float32),
+        cost_estimate=pl.CostEstimate(
+            flops=HEADS * 4 * span * span * HEAD_DIM,
+            transcendentals=HEADS * span * span,
+            bytes_accessed=3 * 2 * span * HEADS * HEAD_DIM + 4 * span * HEADS * HEAD_DIM,
+        ),
+    )(decay_rates, q, k, v)
+
+
+def output_kernel(rates_ref, intra_ref, q_ref, s_ref, gain_ref, out_ref):
+    g = pl.program_id(0)
+    span = q_ref.shape[0]
     lead = lax.broadcasted_iota(jnp.int32, (span, 1), 0).astype(jnp.float32) + 1.0
     for hh in range(GROUP):
         rate = rates_ref[g * GROUP + hh]
         cols = slice(hh * HEAD_DIM, (hh + 1) * HEAD_DIM)
         q = q_ref[:, cols]
-        k = k_ref[:, cols]
-        v = v_ref[:, cols]
-        scores = lax.dot_general(
-            q, k, (((1,), (1,)), ((), ())), preferred_element_type=jnp.float32
-        )
-        within = jnp.where(causal, jnp.exp(-rate * gap), 0.0)
-        weights = (scores * within).astype(jnp.bfloat16)
-        intra = jnp.dot(weights, v, preferred_element_type=jnp.float32)
         hi, lo = kernel_split(s_ref[hh])
         inter = jnp.dot(q, hi, preferred_element_type=jnp.float32) + jnp.dot(
             q, lo, preferred_element_type=jnp.float32
         )
-        total = intra + inter * jnp.exp(-rate * lead)
+        total = intra_ref[:, cols] + inter * jnp.exp(-rate * lead)
         mean_square = jnp.mean(total * total, axis=-1, keepdims=True)
         normed = total * lax.rsqrt(mean_square + 1e-06) * gain_ref[hh : hh + 1, :]
         out_ref[:, cols] = normed.astype(out_ref.dtype)
 
 
-def block_output(decay_rates, q, k, v, incoming, gains):
+def block_output(decay_rates, intra, q, incoming, gains):
     span = q.shape[0]
     groups = HEADS // GROUP
     width = GROUP * HEAD_DIM
@@ -102,18 +134,56 @@
             pl.BlockSpec(memory_space=pltpu.SMEM),
             pl.BlockSpec((span, width), lambda g: (0, g)),
             pl.BlockSpec((span, width), lambda g: (0, g)),
-            pl.BlockSpec((span, width), lambda g: (0, g)),
             pl.BlockSpec((GROUP, HEAD_DIM, HEAD_DIM), lambda g: (g, 0, 0)),
             pl.BlockSpec((GROUP, HEAD_DIM), lambda g: (g, 0)),
         ],
         out_specs=pl.BlockSpec((span, width), lambda g: (0, g)),
         out_shape=jax.ShapeDtypeStruct((span, HEADS * HEAD_DIM), jnp.bfloat16),
         cost_estimate=pl.CostEstimate(
-            flops=HEADS * (4 * span * span * HEAD_DIM + 4 * span * HEAD_DIM * HEAD_DIM),
-            transcendentals=HEADS * span * span,
-            bytes_accessed=4 * 2 * span * HEADS * HEAD_DIM + 4 * HEADS * HEAD_DIM * HEAD_DIM,
-        ),
-    )(decay_rates, q, k, v, incoming, gains)
+            flops=HEADS * 4 * span * HEAD_DIM * HEAD_DIM,
+            transcendentals=HEADS * span,
+            bytes_accessed=8 * span * HEADS * HEAD_DIM + 4 * HEADS * HEAD_DIM * HEAD_DIM,
+        ),
+    )(decay_rates, intra, q, incoming, gains)
+
+
+def chain_kernel(scale_ref, g_ref, out_ref):
+    blocks = CHAIN_BLOCKS
+    parts = g_ref.shape[0] // blocks
+    scale = scale_ref[0]
+    a = lax.broadcasted_iota(jnp.int32, (blocks, blocks), 0).astype(jnp.float32)
+    b = lax.broadcasted_iota(jnp.int32, (blocks, blocks), 1).astype(jnp.float32)
+    gaps = a - 1.0 - b
+    chain = jnp.where(gaps >= 0.0, jnp.exp(-scale * jnp.maximum(gaps, 0.0)), 0.0)
+    c_hi, c_lo = kernel_split(chain)
+    for r in range(parts):
+        x = g_ref[pl.ds(r, blocks, stride=parts), :]
+        x_hi, x_lo = kernel_split(x)
+        y = (
+            jnp.dot(c_hi, x_hi, preferred_element_type=jnp.float32)
+            + jnp.dot(c_lo, x_hi, preferred_element_type=jnp.float32)
+            + jnp.dot(c_hi, x_lo, preferred_element_type=jnp.float32)
+        )
+        out_ref[pl.ds(r, blocks, stride=parts), :] = y
+
+
+def block_chain(scale, gathered2d):
+    blocks = CHAIN_BLOCKS
+    rows, width = gathered2d.shape
+    return pl.pallas_call(
+        chain_kernel,
+        in_specs=[
+            pl.BlockSpec(memory_space=pltpu.SMEM),
+            pl.BlockSpec((rows, width), lambda: (0, 0)),
+        ],
+        out_specs=pl.BlockSpec((rows, width), lambda: (0, 0)),
+        out_shape=jax.ShapeDtypeStruct((rows, width), jnp.float32),
+        cost_estimate=pl.CostEstimate(
+            flops=6 * blocks * rows * width,
+            transcendentals=blocks * blocks,
+            bytes_accessed=8 * rows * width,
+        ),
+    )(scale, gathered2d)
 
 
 def body(n, queries, key_rows, value_rows, decay_rates, norm_gain):
@@ -125,27 +195,15 @@
     rows = HEADS * HEAD_DIM // n
     chunks = local_state.reshape(n, rows, HEAD_DIM)
     gathered = lax.all_to_all(chunks, AXES, 0, 0, tiled=True)
+    intra = block_intra(decay_rates, queries, key_rows, value_rows)
     head_of_chunk = me // (n // HEADS)
-    rate = lax.dynamic_slice_in_dim(decay_rates, head_of_chunk, 1)[0]
-    blocks = jnp.arange(n, dtype=jnp.float32)
-    gaps = blocks[:, None] - 1.0 - blocks[None, :]
-    chain = jnp.where(
-        gaps >= 0.0, jnp.exp(-rate * float(span) * jnp.maximum(gaps, 0.0)), 0.0
-    )
-    c_hi, c_lo = split_hi_lo(chain)
-    g_hi, g_lo = split_hi_lo(gathered)
-    spec = "ab,bxy->axy"
-    before = (
-        jnp.einsum(spec, c_hi, g_hi, preferred_element_type=jnp.float32)
-        + jnp.einsum(spec, c_lo, g_hi, preferred_element_type=jnp.float32)
-        + jnp.einsum(spec, c_hi, g_lo, preferred_element_type=jnp.float32)
-    )
-    incoming = lax.all_to_all(before, AXES, 0, 0, tiled=True).reshape(
-        HEADS, HEAD_DIM, HEAD_DIM
-    )
+    rate = lax.dynamic_slice_in_dim(decay_rates, head_of_chunk, 1)
+    before = block_chain(rate * float(span), gathered.reshape(n * rows, HEAD_DIM))
+    incoming = lax.all_to_all(before.reshape(n, rows, HEAD_DIM), AXES, 0, 0, tiled=True)
+    incoming = incoming.reshape(HEADS, HEAD_DIM, HEAD_DIM)
 
     gains = norm_gain.reshape(HEADS, HEAD_DIM)
-    return block_output(decay_rates, queries, key_rows, value_rows, incoming, gains)
+    return block_output(decay_rates, intra, queries, incoming, gains)
 
 
 def solution(mesh):

time: 96.7 us -> 97.6 us (level)
  blocking collectives: 34.8 us -> 0 us
  waiting for transfers between devices: 29.5 us -> 53.3 us
  Pallas kernels: 13.5 us -> 24.5 us
  matrix products: 4.44 us -> 0 us
  starting transfers between devices: 11.5 us -> 15.3 us
  local copies, waits for them, and re-layouts: 1.87 us -> 3.3 us
    all_to_all x1 -> x0, blocking collectives: 34.8 us -> none  [body(): lax.all_to_all(before, AXES, 0, 0, tiled=True)]
    all_to_all x0 -> x1, waiting for transfers between devices: none -> 23.8 us  [body(): lax.all_to_all(before.reshape(n, rows, HEAD_DIM), AXES, 0, 0, tiled=True)]
    pallas_call x0 -> x2, Pallas kernels: none -> 13 us  [the longest x1 7.14 us: block_intra(): pl.pallas_call(intra_kernel, grid=(groups,), in_specs=[pl.BlockSpec(memor...]
    dot_general x3 -> x0, matrix products: 4.44 us -> none  [the longest x1 1.61 us: body(): jnp.einsum(spec, c_hi, g_lo, preferred_element_type=jnp.float32)]
    all_to_all x0 -> x1, starting transfers between devices: none -> 3.84 us  [body(): lax.all_to_all(before.reshape(n, rows, HEAD_DIM), AXES, 0, 0, tiled=True)]
    unnamed x2 -> x6, local copies, waits for them, and re-layouts: 0.01 us -> 2.64 us
    pallas_call x1, Pallas kernels: 8.31 us -> 6.35 us  [block_output(): pl.pallas_call(output_kernel, grid=(groups,), in_specs=[pl.BlockSpec(memo...]
    add x1 -> x0, local copies, waits for them, and re-layouts: 1.22 us -> none  [body(): jnp.einsum(spec, c_hi, g_hi, preferred_element_type=jnp.float32)]
  transfers between devices with their start and end apart: 1 -> 2, of which waited for: 1 -> 2; matrix products, arithmetic and copies ran while one was open for 1% -> 1% of each run, Pallas kernels for 0% -> 7%
where the time goes in v4:
time: 97.6 us; the launch traced here: 97.1 us
  waiting for transfers between devices  53.3 us (55%)
  Pallas kernels  24.5 us (25%)
  starting transfers between devices  15.3 us (16%)
  local copies, waits for them, and re-layouts  3.3 us (3%)
    all_to_all x1, waiting for transfers between devices, body(): gathered = lax.all_to_all(chunks, AXES, 0, 0, tiled=True)  29.4 us
    all_to_all x1, waiting for transfers between devices, body(): lax.all_to_all(before.reshape(n, rows, HEAD_DIM), AXES, 0, 0, tiled=True)  23.8 us
    all_to_all x1, starting transfers between devices, body(): gathered = lax.all_to_all(chunks, AXES, 0, 0, tiled=True)  11.5 us
    pallas_call x1, Pallas kernels, block_intra(): pl.pallas_call(intra_kernel, grid=(groups,), in_specs=[pl.BlockSpec(memor...  7.14 us
    pallas_call x1, Pallas kernels, block_output(): pl.pallas_call(output_kernel, grid=(groups,), in_specs=[pl.BlockSpec(memo...  6.35 us
    pallas_call x1, Pallas kernels, block_chain(): pl.pallas_call(chain_kernel, in_specs=[pl.BlockSpec(memory_space=pltpu.SM...  5.82 us
    pallas_call x1, Pallas kernels, block_state(): pl.pallas_call(state_kernel, grid=(groups,), in_specs=[pl.BlockSpec(memor...  5.19 us
    all_to_all x1, starting transfers between devices, body(): lax.all_to_all(before.reshape(n, rows, HEAD_DIM), AXES, 0, 0, tiled=True)  3.84 us
  transfers between devices with their start and end apart: 2, of which 2 were waited for; matrix products, arithmetic and copies ran while one was open for 1% of the time, Pallas kernels for 7%

profile of v4, /device:TPU:1, one launch (start us, length us, event | category | flops | bytes accessed | tf_op | source)
XLA Modules:
  0.0 97.1 jit_solution(16716305347372844575)
XLA Ops:
  0.0 5.2 %shard_map.56 = f32[32,128,128]{2,1,0:T(8,128)} custom-call(f32[32]{0:T(128)} %rates_ref.5, bf16[256,4096]{1,0:T(8,128)(2,1)} %k_ref.3, bf16[256,4096]{1,0:T(8,128)(2,1)} %v_ref.3), custom_call_target="tpu_custom_call" | custom-call | flops 536870912 | bytes 6291456 | tf_op jit(solution)/shard_map/pallas_call | solution.py:46
  5.2 0.0 copy-start.2
  5.2 11.5 %all-to-all-start = ((f32[128,32,128]{2,1,0:T(8,128)}), f32[128,32,128]{2,1,0:T(8,128)S(1)}, u32[]{:S(2)}, u32[]{:S(2)}) async-start(f32[128,32,128]{2,1,0:T(8,128)} %bitcast.5), calls=%async_computation | async-start | bytes 4194304 | tf_op jit(solution)/shard_map/all_to_all | solution.py:197
  16.7 0.0 copy-done.2
  16.7 0.7 dynamic_slice.3
  18.1 29.4 %all-to-all-done = f32[128,32,128]{2,1,0:T(8,128)S(1)} async-done(((f32[128,32,128]{2,1,0:T(8,128)}), f32[128,32,128]{2,1,0:T(8,128)S(1)}, u32[]{:S(2)}, u32[]{:S(2)}) %all-to-all-start) | async-done | bytes 2097184 | tf_op jit(solution)/shard_map/all_to_all | solution.py:197
  47.5 0.0 copy-start
  47.5 1.3 %copy-done = f32[128,32,128]{2,1,0:T(8,128)} copy-done((f32[128,32,128]{2,1,0:T(8,128)}, f32[128,32,128]{2,1,0:T(8,128)S(1)}, u32[]{:S(2)}) %copy-start) | copy-done | bytes 2097176
  48.8 5.8 %shard_map.57 = f32[4096,128]{1,0:T(8,128)} custom-call(f32[1]{0:T(128)S(6)} %mul.7.scale_ref, f32[4096,128]{1,0:T(8,128)} %bitcast.6), custom_call_target="tpu_custom_call" | custom-call | flops 402653184 | bytes 4194304 | tf_op jit(solution)/shard_map/pallas_call | solution.py:173
  54.7 3.8 %all-to-all-start.1 = ((f32[128,32,128]{2,1,0:T(8,128)}), f32[128,32,128]{2,1,0:T(8,128)S(1)}, u32[]{:S(2)}, u32[]{:S(2)}) async-start(f32[128,32,128]{2,1,0:T(8,128)} %bitcast.7), calls=%async_computation.1 | async-start | bytes 4194304 | tf_op jit(solution)/shard_map/all_to_all | solution.py:202
  58.5 7.1 %shard_map.55.intra_ref = f32[256,4096]{1,0:T(8,128)} custom-call(f32[32]{0:T(128)} %rates_ref.5, bf16[256,4096]{1,0:T(8,128)(2,1)} %q_ref.3, bf16[256,4096]{1,0:T(8,128)(2,1)} %k_ref.3, bf16[256,4096]{1,0:T(8,128)(2,1)} %v_ref.3), custom_call_target="tpu_custom_call" | custom-call | flops 1073741824 | bytes 10485760 | tf_op jit(solution)/shard_map/pallas_call | solution.py:89
  65.6 23.8 %all-to-all-done.1 = f32[128,32,128]{2,1,0:T(8,128)S(1)} async-done(((f32[128,32,128]{2,1,0:T(8,128)}), f32[128,32,128]{2,1,0:T(8,128)S(1)}, u32[]{:S(2)}, u32[]{:S(2)}) %all-to-all-start.1) | async-done | bytes 2097184 | tf_op jit(solution)/shard_map/all_to_all | solution.py:202
  89.5 0.0 copy-start.1
  89.5 1.3 %copy-done.1 = f32[128,32,128]{2,1,0:T(8,128)} copy-done((f32[128,32,128]{2,1,0:T(8,128)}, f32[128,32,128]{2,1,0:T(8,128)S(1)}, u32[]{:S(2)}) %copy-start.1) | copy-done | bytes 2097176
  90.8 6.3 %shard_map.58 = bf16[256,4096]{1,0:T(8,128)(2,1)} custom-call(f32[32]{0:T(128)} %rates_ref.5, f32[256,4096]{1,0:T(8,128)} %shard_map.55.intra_ref, bf16[256,4096]{1,0:T(8,128)(2,1)} %q_ref.3, f32[32,128,128]{2,1,0:T(8,128)} %bitcast.8, f32[32,128]{1,0:T(8,128)} %bitcast.9), custom_call_target="tpu_custom_call" | custom-call | flops 536870912 | bytes 10485760 | tf_op jit(solution)/shard_map/pallas_call | solution.py:130
Async XLA Ops:
  5.2 11.5 %copy-start.2 = (f32[32]{0:T(128)S(1)}, f32[32]{0:T(128)}, u32[]{:S(2)}) copy-start(f32[32]{0:T(128)} %rates_ref.5) | copy-start | bytes 388
  5.2 42.3 %all-to-all-start = ((f32[128,32,128]{2,1,0:T(8,128)}), f32[128,32,128]{2,1,0:T(8,128)S(1)}, u32[]{:S(2)}, u32[]{:S(2)}) async-start(f32[128,32,128]{2,1,0:T(8,128)} %bitcast.5), calls=%async_computation | async-start | bytes 4194304 | tf_op jit(solution)/shard_map/all_to_all | solution.py:197
  47.5 1.3 %copy-start = (f32[128,32,128]{2,1,0:T(8,128)}, f32[128,32,128]{2,1,0:T(8,128)S(1)}, u32[]{:S(2)}) copy-start(f32[128,32,128]{2,1,0:T(8,128)S(1)} %all-to-all-done) | copy-start | bytes 6291460
  54.7 34.8 %all-to-all-start.1 = ((f32[128,32,128]{2,1,0:T(8,128)}), f32[128,32,128]{2,1,0:T(8,128)S(1)}, u32[]{:S(2)}, u32[]{:S(2)}) async-start(f32[128,32,128]{2,1,0:T(8,128)} %bitcast.7), calls=%async_computation.1 | async-start | bytes 4194304 | tf_op jit(solution)/shard_map/all_to_all | solution.py:202
  89.5 1.3 %copy-start.1 = (f32[128,32,128]{2,1,0:T(8,128)}, f32[128,32,128]{2,1,0:T(8,128)S(1)}, u32[]{:S(2)}) copy-start(f32[128,32,128]{2,1,0:T(8,128)S(1)} %all-to-all-done.1) | copy-start | bytes 6291460

commit v5 on v4

--- a/solution.py
+++ b/solution.py
@@ -10,7 +10,6 @@
 BLOCK = 256
 AXES = ("seq", "head")
 GROUP = 8
-CHAIN_BLOCKS = 128
 
 
 def split_hi_lo(x):
@@ -113,7 +112,7 @@
         rate = rates_ref[g * GROUP + hh]
         cols = slice(hh * HEAD_DIM, (hh + 1) * HEAD_DIM)
         q = q_ref[:, cols]
-        hi, lo = kernel_split(s_ref[hh])
+        hi, lo = kernel_split(s_ref[g * GROUP + hh])
         inter = jnp.dot(q, hi, preferred_element_type=jnp.float32) + jnp.dot(
             q, lo, preferred_element_type=jnp.float32
         )
@@ -134,7 +133,7 @@
             pl.BlockSpec(memory_space=pltpu.SMEM),
             pl.BlockSpec((span, width), lambda g: (0, g)),
             pl.BlockSpec((span, width), lambda g: (0, g)),
-            pl.BlockSpec((GROUP, HEAD_DIM, HEAD_DIM), lambda g: (g, 0, 0)),
+            pl.BlockSpec(memory_space=pltpu.VMEM),
             pl.BlockSpec((GROUP, HEAD_DIM), lambda g: (g, 0)),
         ],
         out_specs=pl.BlockSpec((span, width), lambda g: (0, g)),
@@ -147,43 +146,35 @@
     )(decay_rates, intra, q, incoming, gains)
 
 
-def chain_kernel(scale_ref, g_ref, out_ref):
-    blocks = CHAIN_BLOCKS
-    parts = g_ref.shape[0] // blocks
-    scale = scale_ref[0]
-    a = lax.broadcasted_iota(jnp.int32, (blocks, blocks), 0).astype(jnp.float32)
-    b = lax.broadcasted_iota(jnp.int32, (blocks, blocks), 1).astype(jnp.float32)
-    gaps = a - 1.0 - b
-    chain = jnp.where(gaps >= 0.0, jnp.exp(-scale * jnp.maximum(gaps, 0.0)), 0.0)
-    c_hi, c_lo = kernel_split(chain)
-    for r in range(parts):
-        x = g_ref[pl.ds(r, blocks, stride=parts), :]
-        x_hi, x_lo = kernel_split(x)
-        y = (
-            jnp.dot(c_hi, x_hi, preferred_element_type=jnp.float32)
-            + jnp.dot(c_lo, x_hi, preferred_element_type=jnp.float32)
-            + jnp.dot(c_hi, x_lo, preferred_element_type=jnp.float32)
-        )
-        out_ref[pl.ds(r, blocks, stride=parts), :] = y
-
-
-def block_chain(scale, gathered2d):
-    blocks = CHAIN_BLOCKS
-    rows, width = gathered2d.shape
+def chain_kernel(carry_ref, g_ref, out_ref):
+    carry = carry_ref[0]
+    state = jnp.zeros(out_ref.shape[1:], jnp.float32)
+    out_ref[0] = state
+
+    def step(b, state):
+        state = carry * state + g_ref[b - 1]
+        out_ref[b] = state
+        return state
+
+    lax.fori_loop(1, out_ref.shape[0], step, state, unroll=8)
+
+
+def block_chain(carry, gathered):
+    blocks, rows, width = gathered.shape
     return pl.pallas_call(
         chain_kernel,
         in_specs=[
             pl.BlockSpec(memory_space=pltpu.SMEM),
-            pl.BlockSpec((rows, width), lambda: (0, 0)),
-        ],
-        out_specs=pl.BlockSpec((rows, width), lambda: (0, 0)),
-        out_shape=jax.ShapeDtypeStruct((rows, width), jnp.float32),
-        cost_estimate=pl.CostEstimate(
-            flops=6 * blocks * rows * width,
-            transcendentals=blocks * blocks,
-            bytes_accessed=8 * rows * width,
-        ),
-    )(scale, gathered2d)
+            pl.BlockSpec(memory_space=pltpu.VMEM),
+        ],
+        out_specs=pl.BlockSpec(memory_space=pltpu.VMEM),
+        out_shape=jax.ShapeDtypeStruct((blocks, rows, width), jnp.float32),
+        cost_estimate=pl.CostEstimate(
+            flops=2 * blocks * rows * width,
+            transcendentals=0,
+            bytes_accessed=8 * blocks * rows * width,
+        ),
+    )(carry, gathered)
 
 
 def body(n, queries, key_rows, value_rows, decay_rates, norm_gain):
@@ -198,8 +189,8 @@
     intra = block_intra(decay_rates, queries, key_rows, value_rows)
     head_of_chunk = me // (n // HEADS)
     rate = lax.dynamic_slice_in_dim(decay_rates, head_of_chunk, 1)
-    before = block_chain(rate * float(span), gathered.reshape(n * rows, HEAD_DIM))
-    incoming = lax.all_to_all(before.reshape(n, rows, HEAD_DIM), AXES, 0, 0, tiled=True)
+    before = block_chain(jnp.exp(-rate * float(span)), gathered)
+    incoming = lax.all_to_all(before, AXES, 0, 0, tiled=True)
     incoming = incoming.reshape(HEADS, HEAD_DIM, HEAD_DIM)
 
     gains = norm_gain.reshape(HEADS, HEAD_DIM)

time: 97.6 us -> 95.5 us (0.978)
  Pallas kernels: 24.5 us -> 22.4 us
    pallas_call x1, Pallas kernels: 5.82 us -> 3.24 us  [block_chain(): pl.pallas_call(chain_kernel, in_specs=[pl.BlockSpec(memory_space=pltpu.SM...]
  transfers between devices with their start and end apart: 2 -> 2, of which waited for: 2 -> 2; matrix products, arithmetic and copies ran while one was open for 1% -> 1% of each run, Pallas kernels for 7% -> 8%
where the time goes in v5:
time: 95.5 us; the launch traced here: 95 us
  waiting for transfers between devices  53.2 us (56%)
  Pallas kernels  22.4 us (23%)
  starting transfers between devices  15.3 us (16%)
  local copies, waits for them, and re-layouts  3.3 us (3%)
    all_to_all x1, waiting for transfers between devices, body(): gathered = lax.all_to_all(chunks, AXES, 0, 0, tiled=True)  29.4 us
    all_to_all x1, waiting for transfers between devices, body(): incoming = lax.all_to_all(before, AXES, 0, 0, tiled=True)  23.8 us
    all_to_all x1, starting transfers between devices, body(): gathered = lax.all_to_all(chunks, AXES, 0, 0, tiled=True)  11.5 us
    pallas_call x1, Pallas kernels, block_intra(): pl.pallas_call(intra_kernel, grid=(groups,), in_specs=[pl.BlockSpec(memor...  7.14 us
    pallas_call x1, Pallas kernels, block_output(): pl.pallas_call(output_kernel, grid=(groups,), in_specs=[pl.BlockSpec(memo...  6.83 us
    pallas_call x1, Pallas kernels, block_state(): pl.pallas_call(state_kernel, grid=(groups,), in_specs=[pl.BlockSpec(memor...  5.19 us
    all_to_all x1, starting transfers between devices, body(): incoming = lax.all_to_all(before, AXES, 0, 0, tiled=True)  3.84 us
    pallas_call x1, Pallas kernels, block_chain(): pl.pallas_call(chain_kernel, in_specs=[pl.BlockSpec(memory_space=pltpu.SM...  3.24 us
  transfers between devices with their start and end apart: 2, of which 2 were waited for; matrix products, arithmetic and copies ran while one was open for 1% of the time, Pallas kernels for 8%

profile of v5, /device:TPU:1, one launch (start us, length us, event | category | flops | bytes accessed | tf_op | source)
XLA Modules:
  0.0 95.0 jit_solution(7433423236216446789)
XLA Ops:
  0.0 5.2 %shard_map.56 = f32[32,128,128]{2,1,0:T(8,128)} custom-call(f32[32]{0:T(128)} %rates_ref.5, bf16[256,4096]{1,0:T(8,128)(2,1)} %k_ref.3, bf16[256,4096]{1,0:T(8,128)(2,1)} %v_ref.3), custom_call_target="tpu_custom_call" | custom-call | flops 536870912 | bytes 6291456 | tf_op jit(solution)/shard_map/pallas_call | solution.py:45
  5.2 0.0 copy-start.2
  5.2 11.5 %all-to-all-start = ((f32[128,32,128]{2,1,0:T(8,128)}), f32[128,32,128]{2,1,0:T(8,128)S(1)}, u32[]{:S(2)}, u32[]{:S(2)}) async-start(f32[128,32,128]{2,1,0:T(8,128)} %bitcast.3), calls=%async_computation | async-start | bytes 4194304 | tf_op jit(solution)/shard_map/all_to_all | solution.py:188
  16.7 0.0 copy-done.2
  16.7 0.7 dynamic_slice.3
  18.1 29.4 %all-to-all-done.g_ref = f32[128,32,128]{2,1,0:T(8,128)S(1)} async-done(((f32[128,32,128]{2,1,0:T(8,128)}), f32[128,32,128]{2,1,0:T(8,128)S(1)}, u32[]{:S(2)}, u32[]{:S(2)}) %all-to-all-start) | async-done | bytes 2097184 | tf_op jit(solution)/shard_map/all_to_all | solution.py:188
  47.5 0.0 copy-start
  47.5 1.3 %copy-done = f32[128,32,128]{2,1,0:T(8,128)} copy-done((f32[128,32,128]{2,1,0:T(8,128)}, f32[128,32,128]{2,1,0:T(8,128)S(1)}, u32[]{:S(2)}) %copy-start) | copy-done | bytes 2097176
  48.8 3.2 %shard_map.57 = f32[128,32,128]{2,1,0:T(8,128)} custom-call(f32[1]{0:T(128)S(6)} %exp.3.carry_ref, f32[128,32,128]{2,1,0:T(8,128)} %copy-done), custom_call_target="tpu_custom_call" | custom-call | flops 1048576 | bytes 4194304 | tf_op jit(solution)/shard_map/pallas_call | solution.py:164
  52.1 3.8 %all-to-all-start.1 = ((f32[128,32,128]{2,1,0:T(8,128)}), f32[128,32,128]{2,1,0:T(8,128)S(1)}, u32[]{:S(2)}, u32[]{:S(2)}) async-start(f32[128,32,128]{2,1,0:T(8,128)} %shard_map.57), calls=%async_computation.1 | async-start | bytes 4194304 | tf_op jit(solution)/shard_map/all_to_all | solution.py:193
  55.9 7.1 %shard_map.55.intra_ref = f32[256,4096]{1,0:T(8,128)} custom-call(f32[32]{0:T(128)} %rates_ref.5, bf16[256,4096]{1,0:T(8,128)(2,1)} %q_ref.3, bf16[256,4096]{1,0:T(8,128)(2,1)} %k_ref.3, bf16[256,4096]{1,0:T(8,128)(2,1)} %v_ref.3), custom_call_target="tpu_custom_call" | custom-call | flops 1073741824 | bytes 10485760 | tf_op jit(solution)/shard_map/pallas_call | solution.py:88
  63.1 23.8 %all-to-all-done.1 = f32[128,32,128]{2,1,0:T(8,128)S(1)} async-done(((f32[128,32,128]{2,1,0:T(8,128)}), f32[128,32,128]{2,1,0:T(8,128)S(1)}, u32[]{:S(2)}, u32[]{:S(2)}) %all-to-all-start.1) | async-done | bytes 2097184 | tf_op jit(solution)/shard_map/all_to_all | solution.py:193
  86.9 0.0 copy-start.1
  86.9 1.3 %copy-done.1 = f32[128,32,128]{2,1,0:T(8,128)} copy-done((f32[128,32,128]{2,1,0:T(8,128)}, f32[128,32,128]{2,1,0:T(8,128)S(1)}, u32[]{:S(2)}) %copy-start.1) | copy-done | bytes 2097176
  88.2 6.8 %shard_map.58 = bf16[256,4096]{1,0:T(8,128)(2,1)} custom-call(f32[32]{0:T(128)} %rates_ref.5, f32[256,4096]{1,0:T(8,128)} %shard_map.55.intra_ref, bf16[256,4096]{1,0:T(8,128)(2,1)} %q_ref.3, f32[32,128,128]{2,1,0:T(8,128)} %bitcast.4, f32[32,128]{1,0:T(8,128)} %bitcast.5), custom_call_target="tpu_custom_call" | custom-call | flops 536870912 | bytes 10485760 | tf_op jit(solution)/shard_map/pallas_call | solution.py:129
Async XLA Ops:
  5.2 11.5 %copy-start.2 = (f32[32]{0:T(128)S(1)}, f32[32]{0:T(128)}, u32[]{:S(2)}) copy-start(f32[32]{0:T(128)} %rates_ref.5) | copy-start | bytes 388
  5.2 42.3 %all-to-all-start = ((f32[128,32,128]{2,1,0:T(8,128)}), f32[128,32,128]{2,1,0:T(8,128)S(1)}, u32[]{:S(2)}, u32[]{:S(2)}) async-start(f32[128,32,128]{2,1,0:T(8,128)} %bitcast.3), calls=%async_computation | async-start | bytes 4194304 | tf_op jit(solution)/shard_map/all_to_all | solution.py:188
  47.5 1.3 %copy-start = (f32[128,32,128]{2,1,0:T(8,128)}, f32[128,32,128]{2,1,0:T(8,128)S(1)}, u32[]{:S(2)}) copy-start(f32[128,32,128]{2,1,0:T(8,128)S(1)} %all-to-all-done.g_ref) | copy-start | bytes 6291460
  52.1 34.8 %all-to-all-start.1 = ((f32[128,32,128]{2,1,0:T(8,128)}), f32[128,32,128]{2,1,0:T(8,128)S(1)}, u32[]{:S(2)}, u32[]{:S(2)}) async-start(f32[128,32,128]{2,1,0:T(8,128)} %shard_map.57), calls=%async_computation.1 | async-start | bytes 4194304 | tf_op jit(solution)/shard_map/all_to_all | solution.py:193
  86.9 1.3 %copy-start.1 = (f32[128,32,128]{2,1,0:T(8,128)}, f32[128,32,128]{2,1,0:T(8,128)S(1)}, u32[]{:S(2)}) copy-start(f32[128,32,128]{2,1,0:T(8,128)S(1)} %all-to-all-done.1) | copy-start | bytes 6291460

commit v6 on v5

--- a/solution.py
+++ b/solution.py
@@ -10,6 +10,7 @@
 BLOCK = 256
 AXES = ("seq", "head")
 GROUP = 8
+PIECE = 64
 
 
 def split_hi_lo(x):
@@ -25,17 +26,26 @@
 def state_kernel(rates_ref, k_ref, v_ref, out_ref):
     g = pl.program_id(0)
     span = k_ref.shape[0]
-    tail = (span - 1.0) - lax.broadcasted_iota(jnp.int32, (span, 1), 0).astype(jnp.float32)
-    for hh in range(GROUP):
+    dims = (((0,), (0,)), ((), ()))
+
+    def head(hh, carry):
         rate = rates_ref[g * GROUP + hh]
-        cols = slice(hh * HEAD_DIM, (hh + 1) * HEAD_DIM)
-        kd = k_ref[:, cols].astype(jnp.float32) * jnp.exp(-rate * tail)
-        hi, lo = kernel_split(kd)
-        v = v_ref[:, cols]
-        dims = (((0,), (0,)), ((), ()))
-        out_ref[hh] = lax.dot_general(
-            hi, v, dims, preferred_element_type=jnp.float32
-        ) + lax.dot_general(lo, v, dims, preferred_element_type=jnp.float32)
+        cols = pl.ds(pl.multiple_of(hh * HEAD_DIM, HEAD_DIM), HEAD_DIM)
+        acc = jnp.zeros((HEAD_DIM, HEAD_DIM), jnp.float32)
+        for p in range(span // PIECE):
+            rows = pl.ds(p * PIECE, PIECE)
+            tail = (span - 1.0 - p * PIECE) - lax.broadcasted_iota(
+                jnp.int32, (PIECE, HEAD_DIM), 0
+            ).astype(jnp.float32)
+            kd = k_ref[rows, cols].astype(jnp.float32) * jnp.exp(-rate * tail)
+            hi, lo = kernel_split(kd)
+            v = v_ref[rows, cols]
+            acc = acc + lax.dot_general(hi, v, dims, preferred_element_type=jnp.float32)
+            acc = acc + lax.dot_general(lo, v, dims, preferred_element_type=jnp.float32)
+        out_ref[hh] = acc
+        return carry
+
+    lax.fori_loop(0, GROUP, head, 0)
 
 
 def block_state(decay_rates, k, v):
@@ -107,19 +117,28 @@
 def output_kernel(rates_ref, intra_ref, q_ref, s_ref, gain_ref, out_ref):
     g = pl.program_id(0)
     span = q_ref.shape[0]
-    lead = lax.broadcasted_iota(jnp.int32, (span, 1), 0).astype(jnp.float32) + 1.0
-    for hh in range(GROUP):
+
+    def head(hh, carry):
         rate = rates_ref[g * GROUP + hh]
-        cols = slice(hh * HEAD_DIM, (hh + 1) * HEAD_DIM)
-        q = q_ref[:, cols]
-        hi, lo = kernel_split(s_ref[g * GROUP + hh])
-        inter = jnp.dot(q, hi, preferred_element_type=jnp.float32) + jnp.dot(
-            q, lo, preferred_element_type=jnp.float32
-        )
-        total = intra_ref[:, cols] + inter * jnp.exp(-rate * lead)
-        mean_square = jnp.mean(total * total, axis=-1, keepdims=True)
-        normed = total * lax.rsqrt(mean_square + 1e-06) * gain_ref[hh : hh + 1, :]
-        out_ref[:, cols] = normed.astype(out_ref.dtype)
+        cols = pl.ds(pl.multiple_of(hh * HEAD_DIM, HEAD_DIM), HEAD_DIM)
+        hi, lo = kernel_split(s_ref[hh])
+        gain = gain_ref[pl.ds(hh, 1), :]
+        for p in range(span // PIECE):
+            rows = pl.ds(p * PIECE, PIECE)
+            q = q_ref[rows, cols]
+            inter = jnp.dot(q, hi, preferred_element_type=jnp.float32) + jnp.dot(
+                q, lo, preferred_element_type=jnp.float32
+            )
+            lead = lax.broadcasted_iota(jnp.int32, (PIECE, HEAD_DIM), 0).astype(
+                jnp.float32
+            ) + (p * PIECE + 1.0)
+            total = intra_ref[rows, cols] + inter * jnp.exp(-rate * lead)
+            mean_square = jnp.mean(total * total, axis=-1, keepdims=True)
+            normed = total * lax.rsqrt(mean_square + 1e-06) * gain
+            out_ref[rows, cols] = normed.astype(out_ref.dtype)
+        return carry
+
+    lax.fori_loop(0, GROUP, head, 0)
 
 
 def block_output(decay_rates, intra, q, incoming, gains):
@@ -133,7 +152,7 @@
             pl.BlockSpec(memory_space=pltpu.SMEM),
             pl.BlockSpec((span, width), lambda g: (0, g)),
             pl.BlockSpec((span, width), lambda g: (0, g)),
-            pl.BlockSpec(memory_space=pltpu.VMEM),
+            pl.BlockSpec((GROUP, HEAD_DIM, HEAD_DIM), lambda g: (g, 0, 0)),
             pl.BlockSpec((GROUP, HEAD_DIM), lambda g: (g, 0)),
         ],
         out_specs=pl.BlockSpec((span, width), lambda g: (0, g)),

time: 95.5 us -> 107 us (1.12)
  Pallas kernels: 22.4 us -> 34.1 us
    pallas_call x1, Pallas kernels: 5.19 us -> 11.3 us  [block_state(): pl.pallas_call(state_kernel, grid=(groups,), in_specs=[pl.BlockSpec(memor...]
    pallas_call x1, Pallas kernels: 6.83 us -> 12.4 us  [block_output(): pl.pallas_call(output_kernel, grid=(groups,), in_specs=[pl.BlockSpec(memo...]
  transfers between devices with their start and end apart: 2 -> 2, of which waited for: 2 -> 2; matrix products, arithmetic and copies ran while one was open for 1% -> 1% of each run, Pallas kernels for 8% -> 7%
where the time goes in v6:
time: 107 us
  waiting for transfers between devices  53.2 us (50%)
  Pallas kernels  34.1 us (32%)
  starting transfers between devices  15.3 us (14%)
  local copies, waits for them, and re-layouts  3.3 us (3%)
    all_to_all x1, waiting for transfers between devices, body(): gathered = lax.all_to_all(chunks, AXES, 0, 0, tiled=True)  29.4 us
    all_to_all x1, waiting for transfers between devices, body(): incoming = lax.all_to_all(before, AXES, 0, 0, tiled=True)  23.8 us
    pallas_call x1, Pallas kernels, block_output(): pl.pallas_call(output_kernel, grid=(groups,), in_specs=[pl.BlockSpec(memo...  12.4 us
    all_to_all x1, starting transfers between devices, body(): gathered = lax.all_to_all(chunks, AXES, 0, 0, tiled=True)  11.5 us
    pallas_call x1, Pallas kernels, block_state(): pl.pallas_call(state_kernel, grid=(groups,), in_specs=[pl.BlockSpec(memor...  11.3 us
    pallas_call x1, Pallas kernels, block_intra(): pl.pallas_call(intra_kernel, grid=(groups,), in_specs=[pl.BlockSpec(memor...  7.14 us
    all_to_all x1, starting transfers between devices, body(): incoming = lax.all_to_all(before, AXES, 0, 0, tiled=True)  3.84 us
    pallas_call x1, Pallas kernels, block_chain(): pl.pallas_call(chain_kernel, in_specs=[pl.BlockSpec(memory_space=pltpu.SM...  3.24 us
  transfers between devices with their start and end apart: 2, of which 2 were waited for; matrix products, arithmetic and copies ran while one was open for 1% of the time, Pallas kernels for 7%

profile of v6, /device:TPU:1, one launch (start us, length us, event | category | flops | bytes accessed | tf_op | source)
XLA Modules:
  0.0 106.7 jit_solution(11841925696561500288)
XLA Ops:
  0.0 11.3 %shard_map.56 = f32[32,128,128]{2,1,0:T(8,128)} custom-call(f32[32]{0:T(128)} %rates_ref.5, bf16[256,4096]{1,0:T(8,128)(2,1)} %k_ref.3, bf16[256,4096]{1,0:T(8,128)(2,1)} %v_ref.3), custom_call_target="tpu_custom_call" | custom-call | flops 536870912 | bytes 6291456 | tf_op jit(solution)/shard_map/pallas_call | solution.py:55
  11.3 0.0 copy-start.2
  11.3 11.5 %all-to-all-start = ((f32[128,32,128]{2,1,0:T(8,128)}), f32[128,32,128]{2,1,0:T(8,128)S(1)}, u32[]{:S(2)}, u32[]{:S(2)}) async-start(f32[128,32,128]{2,1,0:T(8,128)} %bitcast.3), calls=%async_computation | async-start | bytes 4194304 | tf_op jit(solution)/shard_map/all_to_all | solution.py:207
  22.8 0.0 copy-done.2
  22.8 0.7 dynamic_slice.3
  24.2 29.4 %all-to-all-done.g_ref = f32[128,32,128]{2,1,0:T(8,128)S(1)} async-done(((f32[128,32,128]{2,1,0:T(8,128)}), f32[128,32,128]{2,1,0:T(8,128)S(1)}, u32[]{:S(2)}, u32[]{:S(2)}) %all-to-all-start) | async-done | bytes 2097184 | tf_op jit(solution)/shard_map/all_to_all | solution.py:207
  53.6 0.0 copy-start
  53.6 1.3 %copy-done = f32[128,32,128]{2,1,0:T(8,128)} copy-done((f32[128,32,128]{2,1,0:T(8,128)}, f32[128,32,128]{2,1,0:T(8,128)S(1)}, u32[]{:S(2)}) %copy-start) | copy-done | bytes 2097176
  55.0 3.2 %shard_map.57 = f32[128,32,128]{2,1,0:T(8,128)} custom-call(f32[1]{0:T(128)S(6)} %exp.3.carry_ref, f32[128,32,128]{2,1,0:T(8,128)} %copy-done), custom_call_target="tpu_custom_call" | custom-call | flops 1048576 | bytes 4194304 | tf_op jit(solution)/shard_map/pallas_call | solution.py:183
  58.2 3.8 %all-to-all-start.1 = ((f32[128,32,128]{2,1,0:T(8,128)}), f32[128,32,128]{2,1,0:T(8,128)S(1)}, u32[]{:S(2)}, u32[]{:S(2)}) async-start(f32[128,32,128]{2,1,0:T(8,128)} %shard_map.57), calls=%async_computation.1 | async-start | bytes 4194304 | tf_op jit(solution)/shard_map/all_to_all | solution.py:212
  62.0 7.1 %shard_map.55.intra_ref = f32[256,4096]{1,0:T(8,128)} custom-call(f32[32]{0:T(128)} %rates_ref.5, bf16[256,4096]{1,0:T(8,128)(2,1)} %q_ref.3, bf16[256,4096]{1,0:T(8,128)(2,1)} %k_ref.3, bf16[256,4096]{1,0:T(8,128)(2,1)} %v_ref.3), custom_call_target="tpu_custom_call" | custom-call | flops 1073741824 | bytes 10485760 | tf_op jit(solution)/shard_map/pallas_call | solution.py:98
  69.2 23.8 %all-to-all-done.1 = f32[128,32,128]{2,1,0:T(8,128)S(1)} async-done(((f32[128,32,128]{2,1,0:T(8,128)}), f32[128,32,128]{2,1,0:T(8,128)S(1)}, u32[]{:S(2)}, u32[]{:S(2)}) %all-to-all-start.1) | async-done | bytes 2097184 | tf_op jit(solution)/shard_map/all_to_all | solution.py:212
  93.0 0.0 copy-start.1
  93.0 1.3 %copy-done.1 = f32[128,32,128]{2,1,0:T(8,128)} copy-done((f32[128,32,128]{2,1,0:T(8,128)}, f32[128,32,128]{2,1,0:T(8,128)S(1)}, u32[]{:S(2)}) %copy-start.1) | copy-done | bytes 2097176
  94.3 12.4 %shard_map.58 = bf16[256,4096]{1,0:T(8,128)(2,1)} custom-call(f32[32]{0:T(128)} %rates_ref.5, f32[256,4096]{1,0:T(8,128)} %shard_map.55.intra_ref, bf16[256,4096]{1,0:T(8,128)(2,1)} %q_ref.3, f32[32,128,128]{2,1,0:T(8,128)} %bitcast.4, f32[32,128]{1,0:T(8,128)} %bitcast.5), custom_call_target="tpu_custom_call" | custom-call | flops 536870912 | bytes 10485760 | tf_op jit(solution)/shard_map/pallas_call | solution.py:148
Async XLA Ops:
  11.3 11.5 %copy-start.2 = (f32[32]{0:T(128)S(1)}, f32[32]{0:T(128)}, u32[]{:S(2)}) copy-start(f32[32]{0:T(128)} %rates_ref.5) | copy-start | bytes 388
  11.3 42.3 %all-to-all-start = ((f32[128,32,128]{2,1,0:T(8,128)}), f32[128,32,128]{2,1,0:T(8,128)S(1)}, u32[]{:S(2)}, u32[]{:S(2)}) async-start(f32[128,32,128]{2,1,0:T(8,128)} %bitcast.3), calls=%async_computation | async-start | bytes 4194304 | tf_op jit(solution)/shard_map/all_to_all | solution.py:207
  53.6 1.3 %copy-start = (f32[128,32,128]{2,1,0:T(8,128)}, f32[128,32,128]{2,1,0:T(8,128)S(1)}, u32[]{:S(2)}) copy-start(f32[128,32,128]{2,1,0:T(8,128)S(1)} %all-to-all-done.g_ref) | copy-start | bytes 6291460
  58.2 34.8 %all-to-all-start.1 = ((f32[128,32,128]{2,1,0:T(8,128)}), f32[128,32,128]{2,1,0:T(8,128)S(1)}, u32[]{:S(2)}, u32[]{:S(2)}) async-start(f32[128,32,128]{2,1,0:T(8,128)} %shard_map.57), calls=%async_computation.1 | async-start | bytes 4194304 | tf_op jit(solution)/shard_map/all_to_all | solution.py:212
  93.0 1.3 %copy-start.1 = (f32[128,32,128]{2,1,0:T(8,128)}, f32[128,32,128]{2,1,0:T(8,128)S(1)}, u32[]{:S(2)}) copy-start(f32[128,32,128]{2,1,0:T(8,128)S(1)} %all-to-all-done.1) | copy-start | bytes 6291460

commit v7 on v5

--- a/solution.py
+++ b/solution.py
@@ -10,6 +10,7 @@
 BLOCK = 256
 AXES = ("seq", "head")
 GROUP = 8
+STREAMS = 4
 
 
 def split_hi_lo(x):
@@ -112,7 +113,7 @@
         rate = rates_ref[g * GROUP + hh]
         cols = slice(hh * HEAD_DIM, (hh + 1) * HEAD_DIM)
         q = q_ref[:, cols]
-        hi, lo = kernel_split(s_ref[g * GROUP + hh])
+        hi, lo = kernel_split(s_ref[hh])
         inter = jnp.dot(q, hi, preferred_element_type=jnp.float32) + jnp.dot(
             q, lo, preferred_element_type=jnp.float32
         )
@@ -133,7 +134,7 @@
             pl.BlockSpec(memory_space=pltpu.SMEM),
             pl.BlockSpec((span, width), lambda g: (0, g)),
             pl.BlockSpec((span, width), lambda g: (0, g)),
-            pl.BlockSpec(memory_space=pltpu.VMEM),
+            pl.BlockSpec((GROUP, HEAD_DIM, HEAD_DIM), lambda g: (g, 0, 0)),
             pl.BlockSpec((GROUP, HEAD_DIM), lambda g: (g, 0)),
         ],
         out_specs=pl.BlockSpec((span, width), lambda g: (0, g)),
@@ -146,17 +147,39 @@
     )(decay_rates, intra, q, incoming, gains)
 
 
-def chain_kernel(carry_ref, g_ref, out_ref):
+def chain_kernel(carry_ref, g_hbm, out_hbm, g_vmem, out_vmem, in_sems, out_sems):
+    blocks = g_vmem.shape[0]
+    size = blocks // STREAMS
+    loads = [
+        pltpu.make_async_copy(
+            g_hbm.at[pl.ds(p * size, size)], g_vmem.at[pl.ds(p * size, size)], in_sems.at[p]
+        )
+        for p in range(STREAMS)
+    ]
+    stores = [
+        pltpu.make_async_copy(
+            out_vmem.at[pl.ds(p * size, size)], out_hbm.at[pl.ds(p * size, size)], out_sems.at[p]
+        )
+        for p in range(STREAMS)
+    ]
+    for copy in loads:
+        copy.start()
     carry = carry_ref[0]
-    state = jnp.zeros(out_ref.shape[1:], jnp.float32)
-    out_ref[0] = state
+    state = jnp.zeros(g_vmem.shape[1:], jnp.float32)
+    out_vmem[0] = state
 
     def step(b, state):
-        state = carry * state + g_ref[b - 1]
-        out_ref[b] = state
+        state = carry * state + g_vmem[b - 1]
+        out_vmem[b] = state
         return state
 
-    lax.fori_loop(1, out_ref.shape[0], step, state, unroll=8)
+    for p in range(STREAMS):
+        loads[p].wait()
+        first = 1 if p == 0 else p * size
+        state = lax.fori_loop(first, (p + 1) * size, step, state, unroll=8)
+        stores[p].start()
+    for copy in stores:
+        copy.wait()
 
 
 def block_chain(carry, gathered):
@@ -165,10 +188,16 @@
         chain_kernel,
         in_specs=[
             pl.BlockSpec(memory_space=pltpu.SMEM),
-            pl.BlockSpec(memory_space=pltpu.VMEM),
-        ],
-        out_specs=pl.BlockSpec(memory_space=pltpu.VMEM),
+            pl.BlockSpec(memory_space=pl.ANY),
+        ],
+        out_specs=pl.BlockSpec(memory_space=pl.ANY),
         out_shape=jax.ShapeDtypeStruct((blocks, rows, width), jnp.float32),
+        scratch_shapes=[
+            pltpu.VMEM((blocks, rows, width), jnp.float32),
+            pltpu.VMEM((blocks, rows, width), jnp.float32),
+            pltpu.SemaphoreType.DMA((STREAMS,)),
+            pltpu.SemaphoreType.DMA((STREAMS,)),
+        ],
         cost_estimate=pl.CostEstimate(
             flops=2 * blocks * rows * width,
             transcendentals=0,

time: 95.5 us -> 94.4 us (0.988)
  Pallas kernels: 22.4 us -> 21.2 us
where the time goes in v7:
time: 94.4 us; the launch traced here: 93.9 us
  waiting for transfers between devices  53.2 us (56%)
  Pallas kernels  21.2 us (22%)
  starting transfers between devices  15.3 us (16%)
  local copies, waits for them, and re-layouts  3.3 us (3%)
    all_to_all x1, waiting for transfers between devices, body(): gathered = lax.all_to_all(chunks, AXES, 0, 0, tiled=True)  29.4 us
    all_to_all x1, waiting for transfers between devices, body(): incoming = lax.all_to_all(before, AXES, 0, 0, tiled=True)  23.8 us
    all_to_all x1, starting transfers between devices, body(): gathered = lax.all_to_all(chunks, AXES, 0, 0, tiled=True)  11.5 us
    pallas_call x1, Pallas kernels, block_intra(): pl.pallas_call(intra_kernel, grid=(groups,), in_specs=[pl.BlockSpec(memor...  7.14 us
    pallas_call x1, Pallas kernels, block_output(): pl.pallas_call(output_kernel, grid=(groups,), in_specs=[pl.BlockSpec(memo...  6.35 us
    pallas_call x1, Pallas kernels, block_state(): pl.pallas_call(state_kernel, grid=(groups,), in_specs=[pl.BlockSpec(memor...  5.19 us
    all_to_all x1, starting transfers between devices, body(): incoming = lax.all_to_all(before, AXES, 0, 0, tiled=True)  3.85 us
    unnamed x6, local copies, waits for them, and re-layouts  2.64 us
  transfers between devices with their start and end apart: 2, of which 2 were waited for; matrix products, arithmetic and copies ran while one was open for 1% of the time, Pallas kernels for 8%

profile of v7, /device:TPU:1, one launch (start us, length us, event | category | flops | bytes accessed | tf_op | source)
XLA Modules:
  0.0 93.9 jit_solution(9391571057645983739)
XLA Ops:
  0.0 5.2 %shard_map.56 = f32[32,128,128]{2,1,0:T(8,128)} custom-call(f32[32]{0:T(128)} %rates_ref.5, bf16[256,4096]{1,0:T(8,128)(2,1)} %k_ref.3, bf16[256,4096]{1,0:T(8,128)(2,1)} %v_ref.3), custom_call_target="tpu_custom_call" | custom-call | flops 536870912 | bytes 6291456 | tf_op jit(solution)/shard_map/pallas_call | solution.py:46
  5.2 0.0 copy-start.2
  5.2 11.5 %all-to-all-start = ((f32[128,32,128]{2,1,0:T(8,128)}), f32[128,32,128]{2,1,0:T(8,128)S(1)}, u32[]{:S(2)}, u32[]{:S(2)}) async-start(f32[128,32,128]{2,1,0:T(8,128)} %bitcast.3), calls=%async_computation | async-start | bytes 4194304 | tf_op jit(solution)/shard_map/all_to_all | solution.py:217
  16.7 0.0 copy-done.2
  16.7 0.7 dynamic_slice.3
  18.1 29.4 %all-to-all-done.g_hbm = f32[128,32,128]{2,1,0:T(8,128)S(1)} async-done(((f32[128,32,128]{2,1,0:T(8,128)}), f32[128,32,128]{2,1,0:T(8,128)S(1)}, u32[]{:S(2)}, u32[]{:S(2)}) %all-to-all-start) | async-done | bytes 2097184 | tf_op jit(solution)/shard_map/all_to_all | solution.py:217
  47.5 0.0 copy-start
  47.5 1.3 %copy-done = f32[128,32,128]{2,1,0:T(8,128)} copy-done((f32[128,32,128]{2,1,0:T(8,128)}, f32[128,32,128]{2,1,0:T(8,128)S(1)}, u32[]{:S(2)}) %copy-start) | copy-done | bytes 2097176
  48.8 2.5 %shard_map.57 = f32[128,32,128]{2,1,0:T(8,128)} custom-call(f32[1]{0:T(128)S(6)} %exp.3.carry_ref, f32[128,32,128]{2,1,0:T(8,128)} %copy-done), custom_call_target="tpu_custom_call" | custom-call | flops 1048576 | bytes 4194304 | tf_op jit(solution)/shard_map/pallas_call | solution.py:187
  51.4 3.9 %all-to-all-start.1 = ((f32[128,32,128]{2,1,0:T(8,128)}), f32[128,32,128]{2,1,0:T(8,128)S(1)}, u32[]{:S(2)}, u32[]{:S(2)}) async-start(f32[128,32,128]{2,1,0:T(8,128)} %shard_map.57), calls=%async_computation.1 | async-start | bytes 4194304 | tf_op jit(solution)/shard_map/all_to_all | solution.py:222
  55.2 7.1 %shard_map.55.intra_ref = f32[256,4096]{1,0:T(8,128)} custom-call(f32[32]{0:T(128)} %rates_ref.5, bf16[256,4096]{1,0:T(8,128)(2,1)} %q_ref.3, bf16[256,4096]{1,0:T(8,128)(2,1)} %k_ref.3, bf16[256,4096]{1,0:T(8,128)(2,1)} %v_ref.3), custom_call_target="tpu_custom_call" | custom-call | flops 1073741824 | bytes 10485760 | tf_op jit(solution)/shard_map/pallas_call | solution.py:89
  62.4 23.8 %all-to-all-done.1 = f32[128,32,128]{2,1,0:T(8,128)S(1)} async-done(((f32[128,32,128]{2,1,0:T(8,128)}), f32[128,32,128]{2,1,0:T(8,128)S(1)}, u32[]{:S(2)}, u32[]{:S(2)}) %all-to-all-start.1) | async-done | bytes 2097184 | tf_op jit(solution)/shard_map/all_to_all | solution.py:222
  86.2 0.0 copy-start.1
  86.2 1.3 %copy-done.1 = f32[128,32,128]{2,1,0:T(8,128)} copy-done((f32[128,32,128]{2,1,0:T(8,128)}, f32[128,32,128]{2,1,0:T(8,128)S(1)}, u32[]{:S(2)}) %copy-start.1) | copy-done | bytes 2097176
  87.5 6.3 %shard_map.58 = bf16[256,4096]{1,0:T(8,128)(2,1)} custom-call(f32[32]{0:T(128)} %rates_ref.5, f32[256,4096]{1,0:T(8,128)} %shard_map.55.intra_ref, bf16[256,4096]{1,0:T(8,128)(2,1)} %q_ref.3, f32[32,128,128]{2,1,0:T(8,128)} %bitcast.4, f32[32,128]{1,0:T(8,128)} %bitcast.5), custom_call_target="tpu_custom_call" | custom-call | flops 536870912 | bytes 10485760 | tf_op jit(solution)/shard_map/pallas_call | solution.py:130
Async XLA Ops:
  5.2 11.5 %copy-start.2 = (f32[32]{0:T(128)S(1)}, f32[32]{0:T(128)}, u32[]{:S(2)}) copy-start(f32[32]{0:T(128)} %rates_ref.5) | copy-start | bytes 388
  5.2 42.3 %all-to-all-start = ((f32[128,32,128]{2,1,0:T(8,128)}), f32[128,32,128]{2,1,0:T(8,128)S(1)}, u32[]{:S(2)}, u32[]{:S(2)}) async-start(f32[128,32,128]{2,1,0:T(8,128)} %bitcast.3), calls=%async_computation | async-start | bytes 4194304 | tf_op jit(solution)/shard_map/all_to_all | solution.py:217
  47.5 1.3 %copy-start = (f32[128,32,128]{2,1,0:T(8,128)}, f32[128,32,128]{2,1,0:T(8,128)S(1)}, u32[]{:S(2)}) copy-start(f32[128,32,128]{2,1,0:T(8,128)S(1)} %all-to-all-done.g_hbm) | copy-start | bytes 6291460
  51.4 34.8 %all-to-all-start.1 = ((f32[128,32,128]{2,1,0:T(8,128)}), f32[128,32,128]{2,1,0:T(8,128)S(1)}, u32[]{:S(2)}, u32[]{:S(2)}) async-start(f32[128,32,128]{2,1,0:T(8,128)} %shard_map.57), calls=%async_computation.1 | async-start | bytes 4194304 | tf_op jit(solution)/shard_map/all_to_all | solution.py:222
  86.2 1.3 %copy-start.1 = (f32[128,32,128]{2,1,0:T(8,128)}, f32[128,32,128]{2,1,0:T(8,128)S(1)}, u32[]{:S(2)}) copy-start(f32[128,32,128]{2,1,0:T(8,128)S(1)} %all-to-all-done.1) | copy-start | bytes 6291460

commit v8 on v7

--- a/solution.py
+++ b/solution.py
@@ -61,7 +61,7 @@
     )(decay_rates, k, v)
 
 
-def intra_kernel(rates_ref, q_ref, k_ref, v_ref, out_ref):
+def intra_kernel(rates_ref, q_ref, k_ref, v_ref, out_ref, qhi_ref, qlo_ref):
     g = pl.program_id(0)
     span = q_ref.shape[0]
     rows = lax.broadcasted_iota(jnp.int32, (span, span), 0).astype(jnp.float32)
@@ -69,6 +69,7 @@
     offsets = rows - cols_i
     causal = offsets >= 0.0
     gap = jnp.maximum(offsets, 0.0)
+    lead = lax.broadcasted_iota(jnp.int32, (span, HEAD_DIM), 0).astype(jnp.float32) + 1.0
     for hh in range(GROUP):
         rate = rates_ref[g * GROUP + hh]
         cols = slice(hh * HEAD_DIM, (hh + 1) * HEAD_DIM)
@@ -80,71 +81,73 @@
         within = jnp.where(causal, jnp.exp(-rate * gap), 0.0)
         weights = (scores * within).astype(jnp.bfloat16)
         out_ref[:, cols] = jnp.dot(weights, v_ref[:, cols], preferred_element_type=jnp.float32)
+        q_hi, q_lo = kernel_split(q.astype(jnp.float32) * jnp.exp(-rate * lead))
+        qhi_ref[:, cols] = q_hi
+        qlo_ref[:, cols] = q_lo
 
 
 def block_intra(decay_rates, q, k, v):
     span = q.shape[0]
     groups = HEADS // GROUP
     width = GROUP * HEAD_DIM
+    tile = pl.BlockSpec((span, width), lambda g: (0, g))
     return pl.pallas_call(
         intra_kernel,
         grid=(groups,),
-        in_specs=[
-            pl.BlockSpec(memory_space=pltpu.SMEM),
-            pl.BlockSpec((span, width), lambda g: (0, g)),
-            pl.BlockSpec((span, width), lambda g: (0, g)),
-            pl.BlockSpec((span, width), lambda g: (0, g)),
-        ],
-        out_specs=pl.BlockSpec((span, width), lambda g: (0, g)),
-        out_shape=jax.ShapeDtypeStruct((span, HEADS * HEAD_DIM), jnp.float32),
+        in_specs=[pl.BlockSpec(memory_space=pltpu.SMEM), tile, tile, tile],
+        out_specs=[tile, tile, tile],
+        out_shape=[
+            jax.ShapeDtypeStruct((span, HEADS * HEAD_DIM), jnp.float32),
+            jax.ShapeDtypeStruct((span, HEADS * HEAD_DIM), jnp.bfloat16),
+            jax.ShapeDtypeStruct((span, HEADS * HEAD_DIM), jnp.bfloat16),
+        ],
         cost_estimate=pl.CostEstimate(
             flops=HEADS * 4 * span * span * HEAD_DIM,
             transcendentals=HEADS * span * span,
-            bytes_accessed=3 * 2 * span * HEADS * HEAD_DIM + 4 * span * HEADS * HEAD_DIM,
+            bytes_accessed=5 * 2 * span * HEADS * HEAD_DIM + 4 * span * HEADS * HEAD_DIM,
         ),
     )(decay_rates, q, k, v)
 
 
-def output_kernel(rates_ref, intra_ref, q_ref, s_ref, gain_ref, out_ref):
-    g = pl.program_id(0)
-    span = q_ref.shape[0]
-    lead = lax.broadcasted_iota(jnp.int32, (span, 1), 0).astype(jnp.float32) + 1.0
+def output_kernel(intra_ref, qhi_ref, qlo_ref, s_ref, gain_ref, out_ref):
     for hh in range(GROUP):
-        rate = rates_ref[g * GROUP + hh]
         cols = slice(hh * HEAD_DIM, (hh + 1) * HEAD_DIM)
-        q = q_ref[:, cols]
-        hi, lo = kernel_split(s_ref[hh])
-        inter = jnp.dot(q, hi, preferred_element_type=jnp.float32) + jnp.dot(
-            q, lo, preferred_element_type=jnp.float32
-        )
-        total = intra_ref[:, cols] + inter * jnp.exp(-rate * lead)
+        s_hi, s_lo = kernel_split(s_ref[hh])
+        q_hi = qhi_ref[:, cols]
+        inter = (
+            jnp.dot(q_hi, s_hi, preferred_element_type=jnp.float32)
+            + jnp.dot(qlo_ref[:, cols], s_hi, preferred_element_type=jnp.float32)
+            + jnp.dot(q_hi, s_lo, preferred_element_type=jnp.float32)
+        )
+        total = intra_ref[:, cols] + inter
         mean_square = jnp.mean(total * total, axis=-1, keepdims=True)
         normed = total * lax.rsqrt(mean_square + 1e-06) * gain_ref[hh : hh + 1, :]
         out_ref[:, cols] = normed.astype(out_ref.dtype)
 
 
-def block_output(decay_rates, intra, q, incoming, gains):
-    span = q.shape[0]
+def block_output(intra, q_hi, q_lo, incoming, gains):
+    span = q_hi.shape[0]
     groups = HEADS // GROUP
     width = GROUP * HEAD_DIM
+    tile = pl.BlockSpec((span, width), lambda g: (0, g))
     return pl.pallas_call(
         output_kernel,
         grid=(groups,),
         in_specs=[
-            pl.BlockSpec(memory_space=pltpu.SMEM),
-            pl.BlockSpec((span, width), lambda g: (0, g)),
-            pl.BlockSpec((span, width), lambda g: (0, g)),
+            tile,
+            tile,
+            tile,
             pl.BlockSpec((GROUP, HEAD_DIM, HEAD_DIM), lambda g: (g, 0, 0)),
             pl.BlockSpec((GROUP, HEAD_DIM), lambda g: (g, 0)),
         ],
-        out_specs=pl.BlockSpec((span, width), lambda g: (0, g)),
+        out_specs=tile,
         out_shape=jax.ShapeDtypeStruct((span, HEADS * HEAD_DIM), jnp.bfloat16),
         cost_estimate=pl.CostEstimate(
-            flops=HEADS * 4 * span * HEAD_DIM * HEAD_DIM,
+            flops=HEADS * 6 * span * HEAD_DIM * HEAD_DIM,
             transcendentals=HEADS * span,
-            bytes_accessed=8 * span * HEADS * HEAD_DIM + 4 * HEADS * HEAD_DIM * HEAD_DIM,
-        ),
-    )(decay_rates, intra, q, incoming, gains)
+            bytes_accessed=10 * span * HEADS * HEAD_DIM + 4 * HEADS * HEAD_DIM * HEAD_DIM,
+        ),
+    )(intra, q_hi, q_lo, incoming, gains)
 
 
 def chain_kernel(carry_ref, g_hbm, out_hbm, g_vmem, out_vmem, in_sems, out_sems):
@@ -215,7 +218,7 @@
     rows = HEADS * HEAD_DIM // n
     chunks = local_state.reshape(n, rows, HEAD_DIM)
     gathered = lax.all_to_all(chunks, AXES, 0, 0, tiled=True)
-    intra = block_intra(decay_rates, queries, key_rows, value_rows)
+    intra, q_hi, q_lo = block_intra(decay_rates, queries, key_rows, value_rows)
     head_of_chunk = me // (n // HEADS)
     rate = lax.dynamic_slice_in_dim(decay_rates, head_of_chunk, 1)
     before = block_chain(jnp.exp(-rate * float(span)), gathered)
@@ -223,7 +226,7 @@
     incoming = incoming.reshape(HEADS, HEAD_DIM, HEAD_DIM)
 
     gains = norm_gain.reshape(HEADS, HEAD_DIM)
-    return block_output(decay_rates, intra, queries, incoming, gains)
+    return block_output(intra, q_hi, q_lo, incoming, gains)
 
 
 def solution(mesh):

time: 94.4 us -> 95 us (level)
  Pallas kernels: 21.2 us -> 22.6 us
where the time goes in v8:
time: 95 us; the launch traced here: 94.5 us
  waiting for transfers between devices  52.6 us (55%)
  Pallas kernels  22.6 us (24%)
  starting transfers between devices  15.3 us (16%)
  local copies, waits for them, and re-layouts  3.26 us (3%)
    all_to_all x1, waiting for transfers between devices, body(): gathered = lax.all_to_all(chunks, AXES, 0, 0, tiled=True)  29.6 us
    all_to_all x1, waiting for transfers between devices, body(): incoming = lax.all_to_all(before, AXES, 0, 0, tiled=True)  23 us
    all_to_all x1, starting transfers between devices, body(): gathered = lax.all_to_all(chunks, AXES, 0, 0, tiled=True)  11.5 us
    pallas_call x1, Pallas kernels, block_intra(): pl.pallas_call(intra_kernel, grid=(groups,), in_specs=[pl.BlockSpec(memor...  7.94 us
    pallas_call x1, Pallas kernels, block_output(): pl.pallas_call(output_kernel, grid=(groups,), in_specs=[tile, tile, tile,...  6.89 us
    pallas_call x1, Pallas kernels, block_state(): pl.pallas_call(state_kernel, grid=(groups,), in_specs=[pl.BlockSpec(memor...  5.19 us
    all_to_all x1, starting transfers between devices, body(): incoming = lax.all_to_all(before, AXES, 0, 0, tiled=True)  3.85 us
    unnamed x6, local copies, waits for them, and re-layouts  2.68 us
  transfers between devices with their start and end apart: 2, of which 2 were waited for; matrix products, arithmetic and copies ran while one was open for 1% of the time, Pallas kernels for 8%

profile of v8, /device:TPU:1, one launch (start us, length us, event | category | flops | bytes accessed | tf_op | source)
XLA Modules:
  0.0 94.5 jit_solution(3276125286862116815)
XLA Ops:
  0.0 5.2 %shard_map.56 = f32[32,128,128]{2,1,0:T(8,128)} custom-call(f32[32]{0:T(128)} %rates_ref.3, bf16[256,4096]{1,0:T(8,128)(2,1)} %k_ref.3, bf16[256,4096]{1,0:T(8,128)(2,1)} %v_ref.3), custom_call_target="tpu_custom_call" | custom-call | flops 536870912 | bytes 6291456 | tf_op jit(solution)/shard_map/pallas_call | solution.py:46
  5.2 0.0 copy-start.2
  5.2 11.5 %all-to-all-start = ((f32[128,32,128]{2,1,0:T(8,128)}), f32[128,32,128]{2,1,0:T(8,128)S(1)}, u32[]{:S(2)}, u32[]{:S(2)}) async-start(f32[128,32,128]{2,1,0:T(8,128)} %bitcast.3), calls=%async_computation | async-start | bytes 4194304 | tf_op jit(solution)/shard_map/all_to_all | solution.py:220
  16.7 0.0 copy-done.2
  16.7 0.6 dynamic_slice.3
  17.9 29.6 %all-to-all-done.g_hbm = f32[128,32,128]{2,1,0:T(8,128)S(1)} async-done(((f32[128,32,128]{2,1,0:T(8,128)}), f32[128,32,128]{2,1,0:T(8,128)S(1)}, u32[]{:S(2)}, u32[]{:S(2)}) %all-to-all-start) | async-done | bytes 2097184 | tf_op jit(solution)/shard_map/all_to_all | solution.py:220
  47.5 0.0 copy-start
  47.5 1.3 %copy-done = f32[128,32,128]{2,1,0:T(8,128)} copy-done((f32[128,32,128]{2,1,0:T(8,128)}, f32[128,32,128]{2,1,0:T(8,128)S(1)}, u32[]{:S(2)}) %copy-start) | copy-done | bytes 2097176
  48.8 2.6 %shard_map.57 = f32[128,32,128]{2,1,0:T(8,128)} custom-call(f32[1]{0:T(128)S(6)} %exp.3.carry_ref, f32[128,32,128]{2,1,0:T(8,128)} %copy-done), custom_call_target="tpu_custom_call" | custom-call | flops 1048576 | bytes 4194304 | tf_op jit(solution)/shard_map/pallas_call | solution.py:190
  51.4 3.9 %all-to-all-start.1 = ((f32[128,32,128]{2,1,0:T(8,128)}), f32[128,32,128]{2,1,0:T(8,128)S(1)}, u32[]{:S(2)}, u32[]{:S(2)}) async-start(f32[128,32,128]{2,1,0:T(8,128)} %shard_map.57), calls=%async_computation.1 | async-start | bytes 4194304 | tf_op jit(solution)/shard_map/all_to_all | solution.py:225
  55.3 7.9 %shard_map.55 = (f32[256,4096]{1,0:T(8,128)}, bf16[256,4096]{1,0:T(8,128)(2,1)}, bf16[256,4096]{1,0:T(8,128)(2,1)}) custom-call(f32[32]{0:T(128)} %rates_ref.3, bf16[256,4096]{1,0:T(8,128)(2,1)} %q_ref.1, bf16[256,4096]{1,0:T(8,128)(2,1)} %k_ref.3, bf16[256,4096]{1,0:T(8,128)(2,1)} %v_ref.3), custom_call_target="tpu_custom_call" | custom-call | flops 1073741824 | bytes 14680064 | tf_op jit(solution)/shard_map/pallas_call | solution.py:94
  63.2 23.0 %all-to-all-done.1 = f32[128,32,128]{2,1,0:T(8,128)S(1)} async-done(((f32[128,32,128]{2,1,0:T(8,128)}), f32[128,32,128]{2,1,0:T(8,128)S(1)}, u32[]{:S(2)}, u32[]{:S(2)}) %all-to-all-start.1) | async-done | bytes 2097184 | tf_op jit(solution)/shard_map/all_to_all | solution.py:225
  86.2 0.0 copy-start.1
  86.2 1.4 %copy-done.1 = f32[128,32,128]{2,1,0:T(8,128)} copy-done((f32[128,32,128]{2,1,0:T(8,128)}, f32[128,32,128]{2,1,0:T(8,128)S(1)}, u32[]{:S(2)}) %copy-start.1) | copy-done | bytes 2097176
  87.6 6.9 %shard_map.58 = bf16[256,4096]{1,0:T(8,128)(2,1)} custom-call(f32[256,4096]{1,0:T(8,128)} %get-tuple-element.8.intra_ref, bf16[256,4096]{1,0:T(8,128)(2,1)} %get-tuple-element.9.qhi_ref, bf16[256,4096]{1,0:T(8,128)(2,1)} %get-tuple-element.10.qlo_ref, f32[32,128,128]{2,1,0:T(8,128)} %bitcast.4, f32[32,128]{1,0:T(8,128)} %bitcast.5), custom_call_target="tpu_custom_call" | custom-call | flops 805306368 | bytes 12582912 | tf_op jit(solution)/shard_map/pallas_call | solution.py:133
Async XLA Ops:
  5.2 11.5 %copy-start.2 = (f32[32]{0:T(128)S(1)}, f32[32]{0:T(128)}, u32[]{:S(2)}) copy-start(f32[32]{0:T(128)} %rates_ref.3) | copy-start | bytes 388
  5.2 42.3 %all-to-all-start = ((f32[128,32,128]{2,1,0:T(8,128)}), f32[128,32,128]{2,1,0:T(8,128)S(1)}, u32[]{:S(2)}, u32[]{:S(2)}) async-start(f32[128,32,128]{2,1,0:T(8,128)} %bitcast.3), calls=%async_computation | async-start | bytes 4194304 | tf_op jit(solution)/shard_map/all_to_all | solution.py:220
  47.5 1.3 %copy-start = (f32[128,32,128]{2,1,0:T(8,128)}, f32[128,32,128]{2,1,0:T(8,128)S(1)}, u32[]{:S(2)}) copy-start(f32[128,32,128]{2,1,0:T(8,128)S(1)} %all-to-all-done.g_hbm) | copy-start | bytes 6291460
  51.4 34.8 %all-to-all-start.1 = ((f32[128,32,128]{2,1,0:T(8,128)}), f32[128,32,128]{2,1,0:T(8,128)S(1)}, u32[]{:S(2)}, u32[]{:S(2)}) async-start(f32[128,32,128]{2,1,0:T(8,128)} %shard_map.57), calls=%async_computation.1 | async-start | bytes 4194304 | tf_op jit(solution)/shard_map/all_to_all | solution.py:225
  86.2 1.4 %copy-start.1 = (f32[128,32,128]{2,1,0:T(8,128)}, f32[128,32,128]{2,1,0:T(8,128)S(1)}, u32[]{:S(2)}) copy-start(f32[128,32,128]{2,1,0:T(8,128)S(1)} %all-to-all-done.1) | copy-start | bytes 6291460

commit v9 on v5

--- a/solution.py
+++ b/solution.py
@@ -143,7 +143,7 @@
             transcendentals=HEADS * span,
             bytes_accessed=8 * span * HEADS * HEAD_DIM + 4 * HEADS * HEAD_DIM * HEAD_DIM,
         ),
-    )(decay_rates, intra, q, incoming, gains)
+    )(decay_rates, intra, q, pltpu.with_memory_space_constraint(incoming, pltpu.VMEM), gains)
 
 
 def chain_kernel(carry_ref, g_ref, out_ref):
@@ -174,7 +174,7 @@
             transcendentals=0,
             bytes_accessed=8 * blocks * rows * width,
         ),
-    )(carry, gathered)
+    )(carry, pltpu.with_memory_space_constraint(gathered, pltpu.VMEM))
 
 
 def body(n, queries, key_rows, value_rows, decay_rates, norm_gain):

time: 95.5 us -> 90.4 us (0.947)
  local copies, waits for them, and re-layouts: 3.3 us -> 0.6 us
  Pallas kernels: 22.4 us -> 19.9 us
    unnamed x6 -> x2, local copies, waits for them, and re-layouts: 2.64 us -> 0.01 us
    pallas_call x1, Pallas kernels: 3.24 us -> 1.65 us  [block_chain(): pl.pallas_call(chain_kernel, in_specs=[pl.BlockSpec(memory_space=pltpu.SM...]
where the time goes in v9:
time: 90.4 us; the launch traced here: 89.9 us
  waiting for transfers between devices  53.4 us (59%)
  Pallas kernels  19.9 us (22%)
  starting transfers between devices  15.3 us (17%)
    all_to_all x1, waiting for transfers between devices, body(): gathered = lax.all_to_all(chunks, AXES, 0, 0, tiled=True)  29.5 us
    all_to_all x1, waiting for transfers between devices, body(): incoming = lax.all_to_all(before, AXES, 0, 0, tiled=True)  23.8 us
    all_to_all x1, starting transfers between devices, body(): gathered = lax.all_to_all(chunks, AXES, 0, 0, tiled=True)  11.5 us
    pallas_call x1, Pallas kernels, block_intra(): pl.pallas_call(intra_kernel, grid=(groups,), in_specs=[pl.BlockSpec(memor...  7.13 us
    pallas_call x1, Pallas kernels, block_output(): pl.pallas_call(output_kernel, grid=(groups,), in_specs=[pl.BlockSpec(memo...  5.95 us
    pallas_call x1, Pallas kernels, block_state(): pl.pallas_call(state_kernel, grid=(groups,), in_specs=[pl.BlockSpec(memor...  5.19 us
    all_to_all x1, starting transfers between devices, body(): incoming = lax.all_to_all(before, AXES, 0, 0, tiled=True)  3.84 us
  transfers between devices with their start and end apart: 2, of which 2 were waited for; matrix products, arithmetic and copies ran while one was open for 1% of the time, Pallas kernels for 8%

profile of v9, /device:TPU:1, one launch (start us, length us, event | category | flops | bytes accessed | tf_op | source)
XLA Modules:
  0.0 89.9 jit_solution(7783363692924583499)
XLA Ops:
  0.0 5.2 %shard_map.56 = f32[32,128,128]{2,1,0:T(8,128)} custom-call(f32[32]{0:T(128)} %rates_ref.5, bf16[256,4096]{1,0:T(8,128)(2,1)} %k_ref.3, bf16[256,4096]{1,0:T(8,128)(2,1)} %v_ref.3), custom_call_target="tpu_custom_call" | custom-call | flops 536870912 | bytes 6291456 | tf_op jit(solution)/shard_map/pallas_call | solution.py:45
  5.2 0.0 copy-start
  5.2 11.5 %all-to-all-start = ((f32[128,32,128]{2,1,0:T(8,128)}), f32[128,32,128]{2,1,0:T(8,128)S(1)}, u32[]{:S(2)}, u32[]{:S(2)}) async-start(f32[128,32,128]{2,1,0:T(8,128)} %bitcast.4), calls=%async_computation | async-start | bytes 4194304 | tf_op jit(solution)/shard_map/all_to_all | solution.py:188
  16.7 0.0 copy-done
  16.7 0.6 dynamic_slice.3
  18.0 29.5 %all-to-all-done.g_ref = f32[128,32,128]{2,1,0:T(8,128)S(1)} async-done(((f32[128,32,128]{2,1,0:T(8,128)}), f32[128,32,128]{2,1,0:T(8,128)S(1)}, u32[]{:S(2)}, u32[]{:S(2)}) %all-to-all-start) | async-done | bytes 2097184 | tf_op jit(solution)/shard_map/all_to_all | solution.py:188
  47.5 1.7 %shard_map.57 = f32[128,32,128]{2,1,0:T(8,128)} custom-call(f32[1]{0:T(128)S(6)} %exp.3.carry_ref, f32[128,32,128]{2,1,0:T(8,128)S(1)} %all-to-all-done.g_ref), custom_call_target="tpu_custom_call" | custom-call | flops 1048576 | bytes 4194304 | tf_op jit(solution)/shard_map/pallas_call | solution.py:164
  49.2 3.8 %all-to-all-start.1 = ((f32[128,32,128]{2,1,0:T(8,128)}), f32[128,32,128]{2,1,0:T(8,128)S(1)}, u32[]{:S(2)}, u32[]{:S(2)}) async-start(f32[128,32,128]{2,1,0:T(8,128)} %shard_map.57), calls=%async_computation.1 | async-start | bytes 4194304 | tf_op jit(solution)/shard_map/all_to_all | solution.py:193
  53.0 7.1 %shard_map.55.intra_ref = f32[256,4096]{1,0:T(8,128)} custom-call(f32[32]{0:T(128)} %rates_ref.5, bf16[256,4096]{1,0:T(8,128)(2,1)} %q_ref.3, bf16[256,4096]{1,0:T(8,128)(2,1)} %k_ref.3, bf16[256,4096]{1,0:T(8,128)(2,1)} %v_ref.3), custom_call_target="tpu_custom_call" | custom-call | flops 1073741824 | bytes 10485760 | tf_op jit(solution)/shard_map/pallas_call | solution.py:88
  60.2 23.8 %all-to-all-done.1 = f32[128,32,128]{2,1,0:T(8,128)S(1)} async-done(((f32[128,32,128]{2,1,0:T(8,128)}), f32[128,32,128]{2,1,0:T(8,128)S(1)}, u32[]{:S(2)}, u32[]{:S(2)}) %all-to-all-start.1) | async-done | bytes 2097184 | tf_op jit(solution)/shard_map/all_to_all | solution.py:193
  84.0 5.9 %shard_map.58 = bf16[256,4096]{1,0:T(8,128)(2,1)} custom-call(f32[32]{0:T(128)} %rates_ref.5, f32[256,4096]{1,0:T(8,128)} %shard_map.55.intra_ref, bf16[256,4096]{1,0:T(8,128)(2,1)} %q_ref.3, f32[32,128,128]{2,1,0:T(8,128)S(1)} %bitcast.3, f32[32,128]{1,0:T(8,128)} %bitcast.5), custom_call_target="tpu_custom_call" | custom-call | flops 536870912 | bytes 10485760 | tf_op jit(solution)/shard_map/pallas_call | solution.py:129
Async XLA Ops:
  5.2 11.5 %copy-start = (f32[32]{0:T(128)S(1)}, f32[32]{0:T(128)}, u32[]{:S(2)}) copy-start(f32[32]{0:T(128)} %rates_ref.5) | copy-start | bytes 388
  5.2 42.3 %all-to-all-start = ((f32[128,32,128]{2,1,0:T(8,128)}), f32[128,32,128]{2,1,0:T(8,128)S(1)}, u32[]{:S(2)}, u32[]{:S(2)}) async-start(f32[128,32,128]{2,1,0:T(8,128)} %bitcast.4), calls=%async_computation | async-start | bytes 4194304 | tf_op jit(solution)/shard_map/all_to_all | solution.py:188
  49.2 34.8 %all-to-all-start.1 = ((f32[128,32,128]{2,1,0:T(8,128)}), f32[128,32,128]{2,1,0:T(8,128)S(1)}, u32[]{:S(2)}, u32[]{:S(2)}) async-start(f32[128,32,128]{2,1,0:T(8,128)} %shard_map.57), calls=%async_computation.1 | async-start | bytes 4194304 | tf_op jit(solution)/shard_map/all_to_all | solution.py:193

commit v10 on v9

--- a/solution.py
+++ b/solution.py
@@ -9,7 +9,7 @@
 HEAD_DIM = 128
 BLOCK = 256
 AXES = ("seq", "head")
-GROUP = 8
+GROUP = 4
 
 
 def split_hi_lo(x):
@@ -118,7 +118,7 @@
         )
         total = intra_ref[:, cols] + inter * jnp.exp(-rate * lead)
         mean_square = jnp.mean(total * total, axis=-1, keepdims=True)
-        normed = total * lax.rsqrt(mean_square + 1e-06) * gain_ref[hh : hh + 1, :]
+        normed = total * lax.rsqrt(mean_square + 1e-06) * gain_ref[pl.ds(g * GROUP + hh, 1), :]
         out_ref[:, cols] = normed.astype(out_ref.dtype)
 
 
@@ -134,7 +134,7 @@
             pl.BlockSpec((span, width), lambda g: (0, g)),
             pl.BlockSpec((span, width), lambda g: (0, g)),
             pl.BlockSpec(memory_space=pltpu.VMEM),
-            pl.BlockSpec((GROUP, HEAD_DIM), lambda g: (g, 0)),
+            pl.BlockSpec(memory_space=pltpu.VMEM),
         ],
         out_specs=pl.BlockSpec((span, width), lambda g: (0, g)),
         out_shape=jax.ShapeDtypeStruct((span, HEADS * HEAD_DIM), jnp.bfloat16),

time: 90.4 us -> 94.9 us (1.050)
  Pallas kernels: 19.9 us -> 26.4 us
  waiting for transfers between devices: 53.4 us -> 51.1 us
    all_to_all x1, waiting for transfers between devices: 23.8 us -> 21.5 us  [body(): incoming = lax.all_to_all(before, AXES, 0, 0, tiled=True)]
    pallas_call x1, Pallas kernels: 7.13 us -> 9.45 us  [block_intra(): pl.pallas_call(intra_kernel, grid=(groups,), in_specs=[pl.BlockSpec(memor...]
    pallas_call x1, Pallas kernels: 5.19 us -> 7.38 us  [block_state(): pl.pallas_call(state_kernel, grid=(groups,), in_specs=[pl.BlockSpec(memor...]
    pallas_call x1, Pallas kernels: 5.95 us -> 7.97 us  [block_output(): pl.pallas_call(output_kernel, grid=(groups,), in_specs=[pl.BlockSpec(memo...]
  transfers between devices with their start and end apart: 2 -> 2, of which waited for: 2 -> 2; matrix products, arithmetic and copies ran while one was open for 1% -> 1% of each run, Pallas kernels for 8% -> 10%
where the time goes in v10:
time: 94.9 us; the launch traced here: 94.2 us
  waiting for transfers between devices  51.1 us (54%)
  Pallas kernels  26.4 us (28%)
  starting transfers between devices  15.3 us (16%)
    all_to_all x1, waiting for transfers between devices, body(): gathered = lax.all_to_all(chunks, AXES, 0, 0, tiled=True)  29.5 us
    all_to_all x1, waiting for transfers between devices, body(): incoming = lax.all_to_all(before, AXES, 0, 0, tiled=True)  21.5 us
    all_to_all x1, starting transfers between devices, body(): gathered = lax.all_to_all(chunks, AXES, 0, 0, tiled=True)  11.5 us
    pallas_call x1, Pallas kernels, block_intra(): pl.pallas_call(intra_kernel, grid=(groups,), in_specs=[pl.BlockSpec(memor...  9.45 us
    pallas_call x1, Pallas kernels, block_output(): pl.pallas_call(output_kernel, grid=(groups,), in_specs=[pl.BlockSpec(memo...  7.97 us
    pallas_call x1, Pallas kernels, block_state(): pl.pallas_call(state_kernel, grid=(groups,), in_specs=[pl.BlockSpec(memor...  7.38 us
    all_to_all x1, starting transfers between devices, body(): incoming = lax.all_to_all(before, AXES, 0, 0, tiled=True)  3.84 us
  transfers between devices with their start and end apart: 2, of which 2 were waited for; matrix products, arithmetic and copies ran while one was open for 1% of the time, Pallas kernels for 10%

profile of v10, /device:TPU:1, one launch (start us, length us, event | category | flops | bytes accessed | tf_op | source)
XLA Modules:
  0.0 94.2 jit_solution(2621733092411746003)
XLA Ops:
  0.0 7.4 %shard_map.56 = f32[32,128,128]{2,1,0:T(8,128)} custom-call(f32[32]{0:T(128)} %rates_ref.5, bf16[256,4096]{1,0:T(8,128)(2,1)} %k_ref.3, bf16[256,4096]{1,0:T(8,128)(2,1)} %v_ref.3), custom_call_target="tpu_custom_call" | custom-call | flops 536870912 | bytes 6291456 | tf_op jit(solution)/shard_map/pallas_call | solution.py:45
  7.4 0.0 copy-start
  7.4 11.5 %all-to-all-start = ((f32[128,32,128]{2,1,0:T(8,128)}), f32[128,32,128]{2,1,0:T(8,128)S(1)}, u32[]{:S(2)}, u32[]{:S(2)}) async-start(f32[128,32,128]{2,1,0:T(8,128)} %bitcast.4), calls=%async_computation | async-start | bytes 4194304 | tf_op jit(solution)/shard_map/all_to_all | solution.py:188
  18.9 0.0 copy-done
  18.9 0.6 dynamic_slice.3
  20.2 29.5 %all-to-all-done.g_ref = f32[128,32,128]{2,1,0:T(8,128)S(1)} async-done(((f32[128,32,128]{2,1,0:T(8,128)}), f32[128,32,128]{2,1,0:T(8,128)S(1)}, u32[]{:S(2)}, u32[]{:S(2)}) %all-to-all-start) | async-done | bytes 2097184 | tf_op jit(solution)/shard_map/all_to_all | solution.py:188
  49.7 1.7 %shard_map.57 = f32[128,32,128]{2,1,0:T(8,128)} custom-call(f32[1]{0:T(128)S(6)} %exp.3.carry_ref, f32[128,32,128]{2,1,0:T(8,128)S(1)} %all-to-all-done.g_ref), custom_call_target="tpu_custom_call" | custom-call | flops 1048576 | bytes 4194304 | tf_op jit(solution)/shard_map/pallas_call | solution.py:164
  51.4 3.8 %all-to-all-start.1 = ((f32[128,32,128]{2,1,0:T(8,128)}), f32[128,32,128]{2,1,0:T(8,128)S(1)}, u32[]{:S(2)}, u32[]{:S(2)}) async-start(f32[128,32,128]{2,1,0:T(8,128)} %shard_map.57), calls=%async_computation.1 | async-start | bytes 4194304 | tf_op jit(solution)/shard_map/all_to_all | solution.py:193
  55.2 9.5 %shard_map.55.intra_ref = f32[256,4096]{1,0:T(8,128)} custom-call(f32[32]{0:T(128)} %rates_ref.5, bf16[256,4096]{1,0:T(8,128)(2,1)} %q_ref.3, bf16[256,4096]{1,0:T(8,128)(2,1)} %k_ref.3, bf16[256,4096]{1,0:T(8,128)(2,1)} %v_ref.3), custom_call_target="tpu_custom_call" | custom-call | flops 1073741824 | bytes 10485760 | tf_op jit(solution)/shard_map/pallas_call | solution.py:88
  64.7 21.5 %all-to-all-done.1 = f32[128,32,128]{2,1,0:T(8,128)S(1)} async-done(((f32[128,32,128]{2,1,0:T(8,128)}), f32[128,32,128]{2,1,0:T(8,128)S(1)}, u32[]{:S(2)}, u32[]{:S(2)}) %all-to-all-start.1) | async-done | bytes 2097184 | tf_op jit(solution)/shard_map/all_to_all | solution.py:193
  86.2 8.0 %shard_map.58 = bf16[256,4096]{1,0:T(8,128)(2,1)} custom-call(f32[32]{0:T(128)} %rates_ref.5, f32[256,4096]{1,0:T(8,128)} %shard_map.55.intra_ref, bf16[256,4096]{1,0:T(8,128)(2,1)} %q_ref.3, f32[32,128,128]{2,1,0:T(8,128)S(1)} %bitcast.3, f32[32,128]{1,0:T(8,128)} %bitcast.5), custom_call_target="tpu_custom_call" | custom-call | flops 536870912 | bytes 10485760 | tf_op jit(solution)/shard_map/pallas_call | solution.py:129
Async XLA Ops:
  7.4 11.5 %copy-start = (f32[32]{0:T(128)S(1)}, f32[32]{0:T(128)}, u32[]{:S(2)}) copy-start(f32[32]{0:T(128)} %rates_ref.5) | copy-start | bytes 388
  7.4 42.3 %all-to-all-start = ((f32[128,32,128]{2,1,0:T(8,128)}), f32[128,32,128]{2,1,0:T(8,128)S(1)}, u32[]{:S(2)}, u32[]{:S(2)}) async-start(f32[128,32,128]{2,1,0:T(8,128)} %bitcast.4), calls=%async_computation | async-start | bytes 4194304 | tf_op jit(solution)/shard_map/all_to_all | solution.py:188
  51.4 34.8 %all-to-all-start.1 = ((f32[128,32,128]{2,1,0:T(8,128)}), f32[128,32,128]{2,1,0:T(8,128)S(1)}, u32[]{:S(2)}, u32[]{:S(2)}) async-start(f32[128,32,128]{2,1,0:T(8,128)} %shard_map.57), calls=%async_computation.1 | async-start | bytes 4194304 | tf_op jit(solution)/shard_map/all_to_all | solution.py:193

commit v11 on v10

--- a/solution.py
+++ b/solution.py
@@ -9,7 +9,7 @@
 HEAD_DIM = 128
 BLOCK = 256
 AXES = ("seq", "head")
-GROUP = 4
+GROUP = 16
 
 
 def split_hi_lo(x):

time: 94.9 us -> 88.9 us (0.937)
  Pallas kernels: 26.4 us -> 17.7 us
  waiting for transfers between devices: 51.1 us -> 54.2 us
    all_to_all x1, waiting for transfers between devices: 21.5 us -> 24.7 us  [body(): incoming = lax.all_to_all(before, AXES, 0, 0, tiled=True)]
    pallas_call x1, Pallas kernels: 9.45 us -> 6.28 us  [block_intra(): pl.pallas_call(intra_kernel, grid=(groups,), in_specs=[pl.BlockSpec(memor...]
    pallas_call x1, Pallas kernels: 7.38 us -> 4.42 us  [block_state(): pl.pallas_call(state_kernel, grid=(groups,), in_specs=[pl.BlockSpec(memor...]
    pallas_call x1, Pallas kernels: 7.97 us -> 5.39 us  [block_output(): pl.pallas_call(output_kernel, grid=(groups,), in_specs=[pl.BlockSpec(memo...]
  transfers between devices with their start and end apart: 2 -> 2, of which waited for: 2 -> 2; matrix products, arithmetic and copies ran while one was open for 1% -> 1% of each run, Pallas kernels for 10% -> 7%
where the time goes in v11:
time: 88.9 us; the launch traced here: 88.6 us
  waiting for transfers between devices  54.2 us (61%)
  Pallas kernels  17.7 us (20%)
  starting transfers between devices  15.3 us (17%)
    all_to_all x1, waiting for transfers between devices, body(): gathered = lax.all_to_all(chunks, AXES, 0, 0, tiled=True)  29.5 us
    all_to_all x1, waiting for transfers between devices, body(): incoming = lax.all_to_all(before, AXES, 0, 0, tiled=True)  24.7 us
    all_to_all x1, starting transfers between devices, body(): gathered = lax.all_to_all(chunks, AXES, 0, 0, tiled=True)  11.5 us
    pallas_call x1, Pallas kernels, block_intra(): pl.pallas_call(intra_kernel, grid=(groups,), in_specs=[pl.BlockSpec(memor...  6.28 us
    pallas_call x1, Pallas kernels, block_output(): pl.pallas_call(output_kernel, grid=(groups,), in_specs=[pl.BlockSpec(memo...  5.39 us
    pallas_call x1, Pallas kernels, block_state(): pl.pallas_call(state_kernel, grid=(groups,), in_specs=[pl.BlockSpec(memor...  4.42 us
    all_to_all x1, starting transfers between devices, body(): incoming = lax.all_to_all(before, AXES, 0, 0, tiled=True)  3.84 us
  transfers between devices with their start and end apart: 2, of which 2 were waited for; matrix products, arithmetic and copies ran while one was open for 1% of the time, Pallas kernels for 7%

profile of v11, /device:TPU:1, one launch (start us, length us, event | category | flops | bytes accessed | tf_op | source)
XLA Modules:
  0.0 88.6 jit_solution(5322406933651131166)
XLA Ops:
  0.0 4.4 %shard_map.56 = f32[32,128,128]{2,1,0:T(8,128)} custom-call(f32[32]{0:T(128)} %rates_ref.5, bf16[256,4096]{1,0:T(8,128)(2,1)} %k_ref.3, bf16[256,4096]{1,0:T(8,128)(2,1)} %v_ref.3), custom_call_target="tpu_custom_call" | custom-call | flops 536870912 | bytes 6291456 | tf_op jit(solution)/shard_map/pallas_call | solution.py:45
  4.4 0.0 copy-start
  4.4 11.5 %all-to-all-start = ((f32[128,32,128]{2,1,0:T(8,128)}), f32[128,32,128]{2,1,0:T(8,128)S(1)}, u32[]{:S(2)}, u32[]{:S(2)}) async-start(f32[128,32,128]{2,1,0:T(8,128)} %bitcast.4), calls=%async_computation | async-start | bytes 4194304 | tf_op jit(solution)/shard_map/all_to_all | solution.py:188
  15.9 0.0 copy-done
  16.0 0.6 dynamic_slice.3
  17.2 29.5 %all-to-all-done.g_ref = f32[128,32,128]{2,1,0:T(8,128)S(1)} async-done(((f32[128,32,128]{2,1,0:T(8,128)}), f32[128,32,128]{2,1,0:T(8,128)S(1)}, u32[]{:S(2)}, u32[]{:S(2)}) %all-to-all-start) | async-done | bytes 2097184 | tf_op jit(solution)/shard_map/all_to_all | solution.py:188
  46.8 1.7 %shard_map.57 = f32[128,32,128]{2,1,0:T(8,128)} custom-call(f32[1]{0:T(128)S(6)} %exp.3.carry_ref, f32[128,32,128]{2,1,0:T(8,128)S(1)} %all-to-all-done.g_ref), custom_call_target="tpu_custom_call" | custom-call | flops 1048576 | bytes 4194304 | tf_op jit(solution)/shard_map/pallas_call | solution.py:164
  48.4 3.8 %all-to-all-start.1 = ((f32[128,32,128]{2,1,0:T(8,128)}), f32[128,32,128]{2,1,0:T(8,128)S(1)}, u32[]{:S(2)}, u32[]{:S(2)}) async-start(f32[128,32,128]{2,1,0:T(8,128)} %shard_map.57), calls=%async_computation.1 | async-start | bytes 4194304 | tf_op jit(solution)/shard_map/all_to_all | solution.py:193
  52.3 6.3 %shard_map.55.intra_ref = f32[256,4096]{1,0:T(8,128)} custom-call(f32[32]{0:T(128)} %rates_ref.5, bf16[256,4096]{1,0:T(8,128)(2,1)} %q_ref.3, bf16[256,4096]{1,0:T(8,128)(2,1)} %k_ref.3, bf16[256,4096]{1,0:T(8,128)(2,1)} %v_ref.3), custom_call_target="tpu_custom_call" | custom-call | flops 1073741824 | bytes 10485760 | tf_op jit(solution)/shard_map/pallas_call | solution.py:88
  58.5 24.7 %all-to-all-done.1 = f32[128,32,128]{2,1,0:T(8,128)S(1)} async-done(((f32[128,32,128]{2,1,0:T(8,128)}), f32[128,32,128]{2,1,0:T(8,128)S(1)}, u32[]{:S(2)}, u32[]{:S(2)}) %all-to-all-start.1) | async-done | bytes 2097184 | tf_op jit(solution)/shard_map/all_to_all | solution.py:193
  83.2 5.4 %shard_map.58 = bf16[256,4096]{1,0:T(8,128)(2,1)} custom-call(f32[32]{0:T(128)} %rates_ref.5, f32[256,4096]{1,0:T(8,128)} %shard_map.55.intra_ref, bf16[256,4096]{1,0:T(8,128)(2,1)} %q_ref.3, f32[32,128,128]{2,1,0:T(8,128)S(1)} %bitcast.3, f32[32,128]{1,0:T(8,128)} %bitcast.5), custom_call_target="tpu_custom_call" | custom-call | flops 536870912 | bytes 10485760 | tf_op jit(solution)/shard_map/pallas_call | solution.py:129
Async XLA Ops:
  4.4 11.5 %copy-start = (f32[32]{0:T(128)S(1)}, f32[32]{0:T(128)}, u32[]{:S(2)}) copy-start(f32[32]{0:T(128)} %rates_ref.5) | copy-start | bytes 388
  4.4 42.3 %all-to-all-start = ((f32[128,32,128]{2,1,0:T(8,128)}), f32[128,32,128]{2,1,0:T(8,128)S(1)}, u32[]{:S(2)}, u32[]{:S(2)}) async-start(f32[128,32,128]{2,1,0:T(8,128)} %bitcast.4), calls=%async_computation | async-start | bytes 4194304 | tf_op jit(solution)/shard_map/all_to_all | solution.py:188
  48.4 34.8 %all-to-all-start.1 = ((f32[128,32,128]{2,1,0:T(8,128)}), f32[128,32,128]{2,1,0:T(8,128)S(1)}, u32[]{:S(2)}, u32[]{:S(2)}) async-start(f32[128,32,128]{2,1,0:T(8,128)} %shard_map.57), calls=%async_computation.1 | async-start | bytes 4194304 | tf_op jit(solution)/shard_map/all_to_all | solution.py:193

commit v12 on v11

--- a/solution.py
+++ b/solution.py
@@ -10,6 +10,7 @@
 BLOCK = 256
 AXES = ("seq", "head")
 GROUP = 16
+PIECE = 4
 
 
 def split_hi_lo(x):
@@ -22,36 +23,68 @@
     return hi, (x - hi.astype(jnp.float32)).astype(jnp.bfloat16)
 
 
-def state_kernel(rates_ref, k_ref, v_ref, out_ref):
-    g = pl.program_id(0)
-    span = k_ref.shape[0]
+def column_copies(src, dst, sems, width):
+    return [
+        pltpu.make_async_copy(
+            src.at[:, pl.ds(p * width, width)], dst.at[:, pl.ds(p * width, width)], sems.at[p]
+        )
+        for p in range(HEADS // PIECE)
+    ]
+
+
+def state_kernel(rates_ref, k_hbm, v_hbm, out_hbm, k_vmem, v_vmem, out_vmem, k_sems, v_sems, out_sems):
+    span = k_vmem.shape[0]
+    width = PIECE * HEAD_DIM
+    k_loads = column_copies(k_hbm, k_vmem, k_sems, width)
+    v_loads = column_copies(v_hbm, v_vmem, v_sems, width)
+    stores = [
+        pltpu.make_async_copy(
+            out_vmem.at[pl.ds(p * PIECE, PIECE)], out_hbm.at[pl.ds(p * PIECE, PIECE)], out_sems.at[p]
+        )
+        for p in range(HEADS // PIECE)
+    ]
+    for p in range(HEADS // PIECE):
+        k_loads[p].start()
+        v_loads[p].start()
     tail = (span - 1.0) - lax.broadcasted_iota(jnp.int32, (span, 1), 0).astype(jnp.float32)
-    for hh in range(GROUP):
-        rate = rates_ref[g * GROUP + hh]
-        cols = slice(hh * HEAD_DIM, (hh + 1) * HEAD_DIM)
-        kd = k_ref[:, cols].astype(jnp.float32) * jnp.exp(-rate * tail)
-        hi, lo = kernel_split(kd)
-        v = v_ref[:, cols]
-        dims = (((0,), (0,)), ((), ()))
-        out_ref[hh] = lax.dot_general(
-            hi, v, dims, preferred_element_type=jnp.float32
-        ) + lax.dot_general(lo, v, dims, preferred_element_type=jnp.float32)
+    dims = (((0,), (0,)), ((), ()))
+    for p in range(HEADS // PIECE):
+        k_loads[p].wait()
+        v_loads[p].wait()
+        for h in range(p * PIECE, (p + 1) * PIECE):
+            rate = rates_ref[h]
+            cols = slice(h * HEAD_DIM, (h + 1) * HEAD_DIM)
+            kd = k_vmem[:, cols].astype(jnp.float32) * jnp.exp(-rate * tail)
+            hi, lo = kernel_split(kd)
+            v = v_vmem[:, cols]
+            out_vmem[h] = lax.dot_general(
+                hi, v, dims, preferred_element_type=jnp.float32
+            ) + lax.dot_general(lo, v, dims, preferred_element_type=jnp.float32)
+        stores[p].start()
+    for copy in stores:
+        copy.wait()
 
 
 def block_state(decay_rates, k, v):
     span = k.shape[0]
-    groups = HEADS // GROUP
-    width = GROUP * HEAD_DIM
+    pieces = HEADS // PIECE
     return pl.pallas_call(
         state_kernel,
-        grid=(groups,),
-        in_specs=[
-            pl.BlockSpec(memory_space=pltpu.SMEM),
-            pl.BlockSpec((span, width), lambda g: (0, g)),
-            pl.BlockSpec((span, width), lambda g: (0, g)),
-        ],
-        out_specs=pl.BlockSpec((GROUP, HEAD_DIM, HEAD_DIM), lambda g: (g, 0, 0)),
+        in_specs=[
+            pl.BlockSpec(memory_space=pltpu.SMEM),
+            pl.BlockSpec(memory_space=pl.ANY),
+            pl.BlockSpec(memory_space=pl.ANY),
+        ],
+        out_specs=pl.BlockSpec(memory_space=pl.ANY),
         out_shape=jax.ShapeDtypeStruct((HEADS, HEAD_DIM, HEAD_DIM), jnp.float32),
+        scratch_shapes=[
+            pltpu.VMEM(k.shape, k.dtype),
+            pltpu.VMEM(v.shape, v.dtype),
+            pltpu.VMEM((HEADS, HEAD_DIM, HEAD_DIM), jnp.float32),
+            pltpu.SemaphoreType.DMA((pieces,)),
+            pltpu.SemaphoreType.DMA((pieces,)),
+            pltpu.SemaphoreType.DMA((pieces,)),
+        ],
         cost_estimate=pl.CostEstimate(
             flops=4 * span * HEADS * HEAD_DIM * HEAD_DIM,
             transcendentals=span * HEADS * HEAD_DIM,
@@ -104,40 +137,60 @@
     )(decay_rates, q, k, v)
 
 
-def output_kernel(rates_ref, intra_ref, q_ref, s_ref, gain_ref, out_ref):
-    g = pl.program_id(0)
-    span = q_ref.shape[0]
+def output_kernel(
+    rates_ref, intra_hbm, q_hbm, s_ref, gain_ref, out_hbm, intra_vmem, q_vmem, out_vmem, i_sems, q_sems, o_sems
+):
+    span = q_vmem.shape[0]
+    width = PIECE * HEAD_DIM
+    i_loads = column_copies(intra_hbm, intra_vmem, i_sems, width)
+    q_loads = column_copies(q_hbm, q_vmem, q_sems, width)
+    stores = column_copies(out_vmem, out_hbm, o_sems, width)
+    for p in range(HEADS // PIECE):
+        i_loads[p].start()
+        q_loads[p].start()
     lead = lax.broadcasted_iota(jnp.int32, (span, 1), 0).astype(jnp.float32) + 1.0
-    for hh in range(GROUP):
-        rate = rates_ref[g * GROUP + hh]
-        cols = slice(hh * HEAD_DIM, (hh + 1) * HEAD_DIM)
-        q = q_ref[:, cols]
-        hi, lo = kernel_split(s_ref[g * GROUP + hh])
-        inter = jnp.dot(q, hi, preferred_element_type=jnp.float32) + jnp.dot(
-            q, lo, preferred_element_type=jnp.float32
-        )
-        total = intra_ref[:, cols] + inter * jnp.exp(-rate * lead)
-        mean_square = jnp.mean(total * total, axis=-1, keepdims=True)
-        normed = total * lax.rsqrt(mean_square + 1e-06) * gain_ref[pl.ds(g * GROUP + hh, 1), :]
-        out_ref[:, cols] = normed.astype(out_ref.dtype)
+    for p in range(HEADS // PIECE):
+        i_loads[p].wait()
+        q_loads[p].wait()
+        for h in range(p * PIECE, (p + 1) * PIECE):
+            rate = rates_ref[h]
+            cols = slice(h * HEAD_DIM, (h + 1) * HEAD_DIM)
+            q = q_vmem[:, cols]
+            hi, lo = kernel_split(s_ref[h])
+            inter = jnp.dot(q, hi, preferred_element_type=jnp.float32) + jnp.dot(
+                q, lo, preferred_element_type=jnp.float32
+            )
+            total = intra_vmem[:, cols] + inter * jnp.exp(-rate * lead)
+            mean_square = jnp.mean(total * total, axis=-1, keepdims=True)
+            normed = total * lax.rsqrt(mean_square + 1e-06) * gain_ref[h : h + 1, :]
+            out_vmem[:, cols] = normed.astype(out_vmem.dtype)
+        stores[p].start()
+    for copy in stores:
+        copy.wait()
 
 
 def block_output(decay_rates, intra, q, incoming, gains):
     span = q.shape[0]
-    groups = HEADS // GROUP
-    width = GROUP * HEAD_DIM
+    pieces = HEADS // PIECE
     return pl.pallas_call(
         output_kernel,
-        grid=(groups,),
-        in_specs=[
-            pl.BlockSpec(memory_space=pltpu.SMEM),
-            pl.BlockSpec((span, width), lambda g: (0, g)),
-            pl.BlockSpec((span, width), lambda g: (0, g)),
+        in_specs=[
+            pl.BlockSpec(memory_space=pltpu.SMEM),
+            pl.BlockSpec(memory_space=pl.ANY),
+            pl.BlockSpec(memory_space=pl.ANY),
             pl.BlockSpec(memory_space=pltpu.VMEM),
             pl.BlockSpec(memory_space=pltpu.VMEM),
         ],
-        out_specs=pl.BlockSpec((span, width), lambda g: (0, g)),
+        out_specs=pl.BlockSpec(memory_space=pl.ANY),
         out_shape=jax.ShapeDtypeStruct((span, HEADS * HEAD_DIM), jnp.bfloat16),
+        scratch_shapes=[
+            pltpu.VMEM(intra.shape, intra.dtype),
+            pltpu.VMEM(q.shape, q.dtype),
+            pltpu.VMEM((span, HEADS * HEAD_DIM), jnp.bfloat16),
+            pltpu.SemaphoreType.DMA((pieces,)),
+            pltpu.SemaphoreType.DMA((pieces,)),
+            pltpu.SemaphoreType.DMA((pieces,)),
+        ],
         cost_estimate=pl.CostEstimate(
             flops=HEADS * 4 * span * HEAD_DIM * HEAD_DIM,
             transcendentals=HEADS * span,

time: 88.9 us -> 91.1 us (1.025)
  Pallas kernels: 17.7 us -> 19.7 us
    pallas_call x2, Pallas kernels: 9.81 us -> 11.8 us  [the longest x1 6.16 us: block_output(): pl.pallas_call(output_kernel, in_specs=[pl.BlockSpec(memory_space=pltpu.S...]
where the time goes in v12:
time: 91.1 us; the launch traced here: 90.6 us
  waiting for transfers between devices  54.2 us (59%)
  Pallas kernels  19.7 us (22%)
  starting transfers between devices  15.3 us (17%)
    all_to_all x1, waiting for transfers between devices, body(): gathered = lax.all_to_all(chunks, AXES, 0, 0, tiled=True)  29.5 us
    all_to_all x1, waiting for transfers between devices, body(): incoming = lax.all_to_all(before, AXES, 0, 0, tiled=True)  24.7 us
    all_to_all x1, starting transfers between devices, body(): gathered = lax.all_to_all(chunks, AXES, 0, 0, tiled=True)  11.5 us
    pallas_call x1, Pallas kernels, block_intra(): pl.pallas_call(intra_kernel, grid=(groups,), in_specs=[pl.BlockSpec(memor...  6.28 us
    pallas_call x1, Pallas kernels, block_output(): pl.pallas_call(output_kernel, in_specs=[pl.BlockSpec(memory_space=pltpu.S...  6.16 us
    pallas_call x1, Pallas kernels, block_state(): pl.pallas_call(state_kernel, in_specs=[pl.BlockSpec(memory_space=pltpu.SM...  5.63 us
    all_to_all x1, starting transfers between devices, body(): incoming = lax.all_to_all(before, AXES, 0, 0, tiled=True)  3.84 us
  transfers between devices with their start and end apart: 2, of which 2 were waited for; matrix products, arithmetic and copies ran while one was open for 1% of the time, Pallas kernels for 7%

profile of v12, /device:TPU:1, one launch (start us, length us, event | category | flops | bytes accessed | tf_op | source)
XLA Modules:
  0.0 90.6 jit_solution(4337013184607471896)
XLA Ops:
  0.0 5.6 %shard_map.56 = f32[32,128,128]{2,1,0:T(8,128)} custom-call(f32[32]{0:T(128)} %rates_ref.5, bf16[256,4096]{1,0:T(8,128)(2,1)} %k_hbm.1, bf16[256,4096]{1,0:T(8,128)(2,1)} %v_hbm.1), custom_call_target="tpu_custom_call" | custom-call | flops 536870912 | bytes 6291456 | tf_op jit(solution)/shard_map/pallas_call | solution.py:71
  5.6 0.0 copy-start
  5.7 11.5 %all-to-all-start = ((f32[128,32,128]{2,1,0:T(8,128)}), f32[128,32,128]{2,1,0:T(8,128)S(1)}, u32[]{:S(2)}, u32[]{:S(2)}) async-start(f32[128,32,128]{2,1,0:T(8,128)} %bitcast.4), calls=%async_computation | async-start | bytes 4194304 | tf_op jit(solution)/shard_map/all_to_all | solution.py:241
  17.2 0.0 copy-done
  17.2 0.6 dynamic_slice.3
  18.4 29.5 %all-to-all-done.g_ref = f32[128,32,128]{2,1,0:T(8,128)S(1)} async-done(((f32[128,32,128]{2,1,0:T(8,128)}), f32[128,32,128]{2,1,0:T(8,128)S(1)}, u32[]{:S(2)}, u32[]{:S(2)}) %all-to-all-start) | async-done | bytes 2097184 | tf_op jit(solution)/shard_map/all_to_all | solution.py:241
  48.0 1.7 %shard_map.57 = f32[128,32,128]{2,1,0:T(8,128)} custom-call(f32[1]{0:T(128)S(6)} %exp.3.carry_ref, f32[128,32,128]{2,1,0:T(8,128)S(1)} %all-to-all-done.g_ref), custom_call_target="tpu_custom_call" | custom-call | flops 1048576 | bytes 4194304 | tf_op jit(solution)/shard_map/pallas_call | solution.py:217
  49.6 3.8 %all-to-all-start.1 = ((f32[128,32,128]{2,1,0:T(8,128)}), f32[128,32,128]{2,1,0:T(8,128)S(1)}, u32[]{:S(2)}, u32[]{:S(2)}) async-start(f32[128,32,128]{2,1,0:T(8,128)} %shard_map.57), calls=%async_computation.1 | async-start | bytes 4194304 | tf_op jit(solution)/shard_map/all_to_all | solution.py:246
  53.5 6.3 %shard_map.55.intra_hbm = f32[256,4096]{1,0:T(8,128)} custom-call(f32[32]{0:T(128)} %rates_ref.5, bf16[256,4096]{1,0:T(8,128)(2,1)} %q_hbm.1, bf16[256,4096]{1,0:T(8,128)(2,1)} %k_hbm.1, bf16[256,4096]{1,0:T(8,128)(2,1)} %v_hbm.1), custom_call_target="tpu_custom_call" | custom-call | flops 1073741824 | bytes 10485760 | tf_op jit(solution)/shard_map/pallas_call | solution.py:121
  59.8 24.7 %all-to-all-done.1 = f32[128,32,128]{2,1,0:T(8,128)S(1)} async-done(((f32[128,32,128]{2,1,0:T(8,128)}), f32[128,32,128]{2,1,0:T(8,128)S(1)}, u32[]{:S(2)}, u32[]{:S(2)}) %all-to-all-start.1) | async-done | bytes 2097184 | tf_op jit(solution)/shard_map/all_to_all | solution.py:246
  84.5 6.2 %shard_map.58 = bf16[256,4096]{1,0:T(8,128)(2,1)} custom-call(f32[32]{0:T(128)} %rates_ref.5, f32[256,4096]{1,0:T(8,128)} %shard_map.55.intra_hbm, bf16[256,4096]{1,0:T(8,128)(2,1)} %q_hbm.1, f32[32,128,128]{2,1,0:T(8,128)S(1)} %bitcast.3, f32[32,128]{1,0:T(8,128)} %bitcast.5), custom_call_target="tpu_custom_call" | custom-call | flops 536870912 | bytes 10485760 | tf_op jit(solution)/shard_map/pallas_call | solution.py:175
Async XLA Ops:
  5.6 11.5 %copy-start = (f32[32]{0:T(128)S(1)}, f32[32]{0:T(128)}, u32[]{:S(2)}) copy-start(f32[32]{0:T(128)} %rates_ref.5) | copy-start | bytes 388
  5.7 42.3 %all-to-all-start = ((f32[128,32,128]{2,1,0:T(8,128)}), f32[128,32,128]{2,1,0:T(8,128)S(1)}, u32[]{:S(2)}, u32[]{:S(2)}) async-start(f32[128,32,128]{2,1,0:T(8,128)} %bitcast.4), calls=%async_computation | async-start | bytes 4194304 | tf_op jit(solution)/shard_map/all_to_all | solution.py:241
  49.6 34.8 %all-to-all-start.1 = ((f32[128,32,128]{2,1,0:T(8,128)}), f32[128,32,128]{2,1,0:T(8,128)S(1)}, u32[]{:S(2)}, u32[]{:S(2)}) async-start(f32[128,32,128]{2,1,0:T(8,128)} %shard_map.57), calls=%async_computation.1 | async-start | bytes 4194304 | tf_op jit(solution)/shard_map/all_to_all | solution.py:246

commit v13 on v11

--- a/solution.py
+++ b/solution.py
@@ -10,6 +10,7 @@
 BLOCK = 256
 AXES = ("seq", "head")
 GROUP = 16
+STREAMS = 4
 
 
 def split_hi_lo(x):
@@ -146,17 +147,30 @@
     )(decay_rates, intra, q, pltpu.with_memory_space_constraint(incoming, pltpu.VMEM), gains)
 
 
-def chain_kernel(carry_ref, g_ref, out_ref):
+def chain_kernel(carry_ref, g_ref, out_hbm, out_vmem, out_sems):
+    blocks = g_ref.shape[0]
+    size = blocks // STREAMS
+    stores = [
+        pltpu.make_async_copy(
+            out_vmem.at[pl.ds(p * size, size)], out_hbm.at[pl.ds(p * size, size)], out_sems.at[p]
+        )
+        for p in range(STREAMS)
+    ]
     carry = carry_ref[0]
-    state = jnp.zeros(out_ref.shape[1:], jnp.float32)
-    out_ref[0] = state
+    state = jnp.zeros(g_ref.shape[1:], jnp.float32)
+    out_vmem[0] = state
 
     def step(b, state):
         state = carry * state + g_ref[b - 1]
-        out_ref[b] = state
+        out_vmem[b] = state
         return state
 
-    lax.fori_loop(1, out_ref.shape[0], step, state, unroll=8)
+    for p in range(STREAMS):
+        first = 1 if p == 0 else p * size
+        state = lax.fori_loop(first, (p + 1) * size, step, state, unroll=8)
+        stores[p].start()
+    for copy in stores:
+        copy.wait()
 
 
 def block_chain(carry, gathered):
@@ -167,8 +181,12 @@
             pl.BlockSpec(memory_space=pltpu.SMEM),
             pl.BlockSpec(memory_space=pltpu.VMEM),
         ],
-        out_specs=pl.BlockSpec(memory_space=pltpu.VMEM),
+        out_specs=pl.BlockSpec(memory_space=pl.ANY),
         out_shape=jax.ShapeDtypeStruct((blocks, rows, width), jnp.float32),
+        scratch_shapes=[
+            pltpu.VMEM((blocks, rows, width), jnp.float32),
+            pltpu.SemaphoreType.DMA((STREAMS,)),
+        ],
         cost_estimate=pl.CostEstimate(
             flops=2 * blocks * rows * width,
             transcendentals=0,

time: 88.9 us -> 88.8 us (level)
  no operation moved by 1% of the time
where the time goes in v13:
time: 88.8 us; the launch traced here: 88.4 us
  waiting for transfers between devices  54.2 us (61%)
  Pallas kernels  17.5 us (20%)
  starting transfers between devices  15.4 us (17%)
    all_to_all x1, waiting for transfers between devices, body(): gathered = lax.all_to_all(chunks, AXES, 0, 0, tiled=True)  29.5 us
    all_to_all x1, waiting for transfers between devices, body(): incoming = lax.all_to_all(before, AXES, 0, 0, tiled=True)  24.7 us
    all_to_all x1, starting transfers between devices, body(): gathered = lax.all_to_all(chunks, AXES, 0, 0, tiled=True)  11.5 us
    pallas_call x1, Pallas kernels, block_intra(): pl.pallas_call(intra_kernel, grid=(groups,), in_specs=[pl.BlockSpec(memor...  6.28 us
    pallas_call x1, Pallas kernels, block_output(): pl.pallas_call(output_kernel, grid=(groups,), in_specs=[pl.BlockSpec(memo...  5.4 us
    pallas_call x1, Pallas kernels, block_state(): pl.pallas_call(state_kernel, grid=(groups,), in_specs=[pl.BlockSpec(memor...  4.42 us
    all_to_all x1, starting transfers between devices, body(): incoming = lax.all_to_all(before, AXES, 0, 0, tiled=True)  3.86 us
  transfers between devices with their start and end apart: 2, of which 2 were waited for; matrix products, arithmetic and copies ran while one was open for 1% of the time, Pallas kernels for 7%

profile of v13, /device:TPU:1, one launch (start us, length us, event | category | flops | bytes accessed | tf_op | source)
XLA Modules:
  0.0 88.4 jit_solution(17713439972373749184)
XLA Ops:
  0.0 4.4 %shard_map.56 = f32[32,128,128]{2,1,0:T(8,128)} custom-call(f32[32]{0:T(128)} %rates_ref.5, bf16[256,4096]{1,0:T(8,128)(2,1)} %k_ref.3, bf16[256,4096]{1,0:T(8,128)(2,1)} %v_ref.3), custom_call_target="tpu_custom_call" | custom-call | flops 536870912 | bytes 6291456 | tf_op jit(solution)/shard_map/pallas_call | solution.py:46
  4.4 0.0 copy-start
  4.4 11.5 %all-to-all-start = ((f32[128,32,128]{2,1,0:T(8,128)}), f32[128,32,128]{2,1,0:T(8,128)S(1)}, u32[]{:S(2)}, u32[]{:S(2)}) async-start(f32[128,32,128]{2,1,0:T(8,128)} %bitcast.4), calls=%async_computation | async-start | bytes 4194304 | tf_op jit(solution)/shard_map/all_to_all | solution.py:206
  15.9 0.0 copy-done
  16.0 0.6 dynamic_slice.3
  17.2 29.5 %all-to-all-done.g_ref = f32[128,32,128]{2,1,0:T(8,128)S(1)} async-done(((f32[128,32,128]{2,1,0:T(8,128)}), f32[128,32,128]{2,1,0:T(8,128)S(1)}, u32[]{:S(2)}, u32[]{:S(2)}) %all-to-all-start) | async-done | bytes 2097184 | tf_op jit(solution)/shard_map/all_to_all | solution.py:206
  46.8 1.4 %shard_map.57 = f32[128,32,128]{2,1,0:T(8,128)} custom-call(f32[1]{0:T(128)S(6)} %exp.3.carry_ref, f32[128,32,128]{2,1,0:T(8,128)S(1)} %all-to-all-done.g_ref), custom_call_target="tpu_custom_call" | custom-call | flops 1048576 | bytes 4194304 | tf_op jit(solution)/shard_map/pallas_call | solution.py:178
  48.2 3.9 %all-to-all-start.1 = ((f32[128,32,128]{2,1,0:T(8,128)}), f32[128,32,128]{2,1,0:T(8,128)S(1)}, u32[]{:S(2)}, u32[]{:S(2)}) async-start(f32[128,32,128]{2,1,0:T(8,128)} %shard_map.57), calls=%async_computation.1 | async-start | bytes 4194304 | tf_op jit(solution)/shard_map/all_to_all | solution.py:211
  52.1 6.3 %shard_map.55.intra_ref = f32[256,4096]{1,0:T(8,128)} custom-call(f32[32]{0:T(128)} %rates_ref.5, bf16[256,4096]{1,0:T(8,128)(2,1)} %q_ref.3, bf16[256,4096]{1,0:T(8,128)(2,1)} %k_ref.3, bf16[256,4096]{1,0:T(8,128)(2,1)} %v_ref.3), custom_call_target="tpu_custom_call" | custom-call | flops 1073741824 | bytes 10485760 | tf_op jit(solution)/shard_map/pallas_call | solution.py:89
  58.4 24.7 %all-to-all-done.1 = f32[128,32,128]{2,1,0:T(8,128)S(1)} async-done(((f32[128,32,128]{2,1,0:T(8,128)}), f32[128,32,128]{2,1,0:T(8,128)S(1)}, u32[]{:S(2)}, u32[]{:S(2)}) %all-to-all-start.1) | async-done | bytes 2097184 | tf_op jit(solution)/shard_map/all_to_all | solution.py:211
  83.0 5.4 %shard_map.58 = bf16[256,4096]{1,0:T(8,128)(2,1)} custom-call(f32[32]{0:T(128)} %rates_ref.5, f32[256,4096]{1,0:T(8,128)} %shard_map.55.intra_ref, bf16[256,4096]{1,0:T(8,128)(2,1)} %q_ref.3, f32[32,128,128]{2,1,0:T(8,128)S(1)} %bitcast.3, f32[32,128]{1,0:T(8,128)} %bitcast.5), custom_call_target="tpu_custom_call" | custom-call | flops 536870912 | bytes 10485760 | tf_op jit(solution)/shard_map/pallas_call | solution.py:130
Async XLA Ops:
  4.4 11.5 %copy-start = (f32[32]{0:T(128)S(1)}, f32[32]{0:T(128)}, u32[]{:S(2)}) copy-start(f32[32]{0:T(128)} %rates_ref.5) | copy-start | bytes 388
  4.4 42.3 %all-to-all-start = ((f32[128,32,128]{2,1,0:T(8,128)}), f32[128,32,128]{2,1,0:T(8,128)S(1)}, u32[]{:S(2)}, u32[]{:S(2)}) async-start(f32[128,32,128]{2,1,0:T(8,128)} %bitcast.4), calls=%async_computation | async-start | bytes 4194304 | tf_op jit(solution)/shard_map/all_to_all | solution.py:206
  48.2 34.8 %all-to-all-start.1 = ((f32[128,32,128]{2,1,0:T(8,128)}), f32[128,32,128]{2,1,0:T(8,128)S(1)}, u32[]{:S(2)}, u32[]{:S(2)}) async-start(f32[128,32,128]{2,1,0:T(8,128)} %shard_map.57), calls=%async_computation.1 | async-start | bytes 4194304 | tf_op jit(solution)/shard_map/all_to_all | solution.py:211

commit v14 on v12

--- a/solution.py
+++ b/solution.py
@@ -10,7 +10,8 @@
 BLOCK = 256
 AXES = ("seq", "head")
 GROUP = 16
-PIECE = 4
+PIECE = 16
+STREAMS = 4
 
 
 def split_hi_lo(x):
@@ -199,17 +200,30 @@
     )(decay_rates, intra, q, pltpu.with_memory_space_constraint(incoming, pltpu.VMEM), gains)
 
 
-def chain_kernel(carry_ref, g_ref, out_ref):
+def chain_kernel(carry_ref, g_ref, out_hbm, out_vmem, out_sems):
+    blocks = g_ref.shape[0]
+    size = blocks // STREAMS
+    stores = [
+        pltpu.make_async_copy(
+            out_vmem.at[pl.ds(p * size, size)], out_hbm.at[pl.ds(p * size, size)], out_sems.at[p]
+        )
+        for p in range(STREAMS)
+    ]
     carry = carry_ref[0]
-    state = jnp.zeros(out_ref.shape[1:], jnp.float32)
-    out_ref[0] = state
+    state = jnp.zeros(g_ref.shape[1:], jnp.float32)
+    out_vmem[0] = state
 
     def step(b, state):
         state = carry * state + g_ref[b - 1]
-        out_ref[b] = state
+        out_vmem[b] = state
         return state
 
-    lax.fori_loop(1, out_ref.shape[0], step, state, unroll=8)
+    for p in range(STREAMS):
+        first = 1 if p == 0 else p * size
+        state = lax.fori_loop(first, (p + 1) * size, step, state, unroll=8)
+        stores[p].start()
+    for copy in stores:
+        copy.wait()
 
 
 def block_chain(carry, gathered):
@@ -220,8 +234,12 @@
             pl.BlockSpec(memory_space=pltpu.SMEM),
             pl.BlockSpec(memory_space=pltpu.VMEM),
         ],
-        out_specs=pl.BlockSpec(memory_space=pltpu.VMEM),
+        out_specs=pl.BlockSpec(memory_space=pl.ANY),
         out_shape=jax.ShapeDtypeStruct((blocks, rows, width), jnp.float32),
+        scratch_shapes=[
+            pltpu.VMEM((blocks, rows, width), jnp.float32),
+            pltpu.SemaphoreType.DMA((STREAMS,)),
+        ],
         cost_estimate=pl.CostEstimate(
             flops=2 * blocks * rows * width,
             transcendentals=0,

time: 91.1 us -> 90.3 us (level)
  no operation moved by 1% of the time
where the time goes in v14:
time: 90.3 us; the launch traced here: 89.8 us
  waiting for transfers between devices  54.2 us (60%)
  Pallas kernels  18.9 us (21%)
  starting transfers between devices  15.4 us (17%)
    all_to_all x1, waiting for transfers between devices, body(): gathered = lax.all_to_all(chunks, AXES, 0, 0, tiled=True)  29.5 us
    all_to_all x1, waiting for transfers between devices, body(): incoming = lax.all_to_all(before, AXES, 0, 0, tiled=True)  24.7 us
    all_to_all x1, starting transfers between devices, body(): gathered = lax.all_to_all(chunks, AXES, 0, 0, tiled=True)  11.5 us
    pallas_call x1, Pallas kernels, block_intra(): pl.pallas_call(intra_kernel, grid=(groups,), in_specs=[pl.BlockSpec(memor...  6.28 us
    pallas_call x1, Pallas kernels, block_output(): pl.pallas_call(output_kernel, in_specs=[pl.BlockSpec(memory_space=pltpu.S...  6.13 us
    pallas_call x1, Pallas kernels, block_state(): pl.pallas_call(state_kernel, in_specs=[pl.BlockSpec(memory_space=pltpu.SM...  5.05 us
    all_to_all x1, starting transfers between devices, body(): incoming = lax.all_to_all(before, AXES, 0, 0, tiled=True)  3.86 us
  transfers between devices with their start and end apart: 2, of which 2 were waited for; matrix products, arithmetic and copies ran while one was open for 1% of the time, Pallas kernels for 7%

profile of v14, /device:TPU:1, one launch (start us, length us, event | category | flops | bytes accessed | tf_op | source)
XLA Modules:
  0.0 89.8 jit_solution(12817586508692680383)
XLA Ops:
  0.0 5.0 %shard_map.56 = f32[32,128,128]{2,1,0:T(8,128)} custom-call(f32[32]{0:T(128)} %rates_ref.5, bf16[256,4096]{1,0:T(8,128)(2,1)} %k_hbm.1, bf16[256,4096]{1,0:T(8,128)(2,1)} %v_hbm.1), custom_call_target="tpu_custom_call" | custom-call | flops 536870912 | bytes 6291456 | tf_op jit(solution)/shard_map/pallas_call | solution.py:72
  5.1 0.0 copy-start
  5.1 11.5 %all-to-all-start = ((f32[128,32,128]{2,1,0:T(8,128)}), f32[128,32,128]{2,1,0:T(8,128)S(1)}, u32[]{:S(2)}, u32[]{:S(2)}) async-start(f32[128,32,128]{2,1,0:T(8,128)} %bitcast.4), calls=%async_computation | async-start | bytes 4194304 | tf_op jit(solution)/shard_map/all_to_all | solution.py:259
  16.6 0.0 copy-done
  16.6 0.6 dynamic_slice.3
  17.9 29.5 %all-to-all-done.g_ref = f32[128,32,128]{2,1,0:T(8,128)S(1)} async-done(((f32[128,32,128]{2,1,0:T(8,128)}), f32[128,32,128]{2,1,0:T(8,128)S(1)}, u32[]{:S(2)}, u32[]{:S(2)}) %all-to-all-start) | async-done | bytes 2097184 | tf_op jit(solution)/shard_map/all_to_all | solution.py:259
  47.4 1.4 %shard_map.57 = f32[128,32,128]{2,1,0:T(8,128)} custom-call(f32[1]{0:T(128)S(6)} %exp.3.carry_ref, f32[128,32,128]{2,1,0:T(8,128)S(1)} %all-to-all-done.g_ref), custom_call_target="tpu_custom_call" | custom-call | flops 1048576 | bytes 4194304 | tf_op jit(solution)/shard_map/pallas_call | solution.py:231
  48.9 3.9 %all-to-all-start.1 = ((f32[128,32,128]{2,1,0:T(8,128)}), f32[128,32,128]{2,1,0:T(8,128)S(1)}, u32[]{:S(2)}, u32[]{:S(2)}) async-start(f32[128,32,128]{2,1,0:T(8,128)} %shard_map.57), calls=%async_computation.1 | async-start | bytes 4194304 | tf_op jit(solution)/shard_map/all_to_all | solution.py:264
  52.7 6.3 %shard_map.55.intra_hbm = f32[256,4096]{1,0:T(8,128)} custom-call(f32[32]{0:T(128)} %rates_ref.5, bf16[256,4096]{1,0:T(8,128)(2,1)} %q_hbm.1, bf16[256,4096]{1,0:T(8,128)(2,1)} %k_hbm.1, bf16[256,4096]{1,0:T(8,128)(2,1)} %v_hbm.1), custom_call_target="tpu_custom_call" | custom-call | flops 1073741824 | bytes 10485760 | tf_op jit(solution)/shard_map/pallas_call | solution.py:122
  59.0 24.7 %all-to-all-done.1 = f32[128,32,128]{2,1,0:T(8,128)S(1)} async-done(((f32[128,32,128]{2,1,0:T(8,128)}), f32[128,32,128]{2,1,0:T(8,128)S(1)}, u32[]{:S(2)}, u32[]{:S(2)}) %all-to-all-start.1) | async-done | bytes 2097184 | tf_op jit(solution)/shard_map/all_to_all | solution.py:264
  83.7 6.1 %shard_map.58 = bf16[256,4096]{1,0:T(8,128)(2,1)} custom-call(f32[32]{0:T(128)} %rates_ref.5, f32[256,4096]{1,0:T(8,128)} %shard_map.55.intra_hbm, bf16[256,4096]{1,0:T(8,128)(2,1)} %q_hbm.1, f32[32,128,128]{2,1,0:T(8,128)S(1)} %bitcast.3, f32[32,128]{1,0:T(8,128)} %bitcast.5), custom_call_target="tpu_custom_call" | custom-call | flops 536870912 | bytes 10485760 | tf_op jit(solution)/shard_map/pallas_call | solution.py:176
Async XLA Ops:
  5.1 11.5 %copy-start = (f32[32]{0:T(128)S(1)}, f32[32]{0:T(128)}, u32[]{:S(2)}) copy-start(f32[32]{0:T(128)} %rates_ref.5) | copy-start | bytes 388
  5.1 42.3 %all-to-all-start = ((f32[128,32,128]{2,1,0:T(8,128)}), f32[128,32,128]{2,1,0:T(8,128)S(1)}, u32[]{:S(2)}, u32[]{:S(2)}) async-start(f32[128,32,128]{2,1,0:T(8,128)} %bitcast.4), calls=%async_computation | async-start | bytes 4194304 | tf_op jit(solution)/shard_map/all_to_all | solution.py:259
  48.9 34.8 %all-to-all-start.1 = ((f32[128,32,128]{2,1,0:T(8,128)}), f32[128,32,128]{2,1,0:T(8,128)S(1)}, u32[]{:S(2)}, u32[]{:S(2)}) async-start(f32[128,32,128]{2,1,0:T(8,128)} %shard_map.57), calls=%async_computation.1 | async-start | bytes 4194304 | tf_op jit(solution)/shard_map/all_to_all | solution.py:264

commit v15 on v13

--- a/solution.py
+++ b/solution.py
@@ -32,11 +32,13 @@
         cols = slice(hh * HEAD_DIM, (hh + 1) * HEAD_DIM)
         kd = k_ref[:, cols].astype(jnp.float32) * jnp.exp(-rate * tail)
         hi, lo = kernel_split(kd)
-        v = v_ref[:, cols]
-        dims = (((0,), (0,)), ((), ()))
-        out_ref[hh] = lax.dot_general(
-            hi, v, dims, preferred_element_type=jnp.float32
-        ) + lax.dot_general(lo, v, dims, preferred_element_type=jnp.float32)
+        both = lax.dot_general(
+            v_ref[:, cols],
+            jnp.concatenate([hi, lo], axis=1),
+            (((0,), (0,)), ((), ())),
+            preferred_element_type=jnp.float32,
+        )
+        out_ref[hh] = both[:, :HEAD_DIM] + both[:, HEAD_DIM:]
 
 
 def block_state(decay_rates, k, v):
@@ -114,8 +116,9 @@
         cols = slice(hh * HEAD_DIM, (hh + 1) * HEAD_DIM)
         q = q_ref[:, cols]
         hi, lo = kernel_split(s_ref[g * GROUP + hh])
-        inter = jnp.dot(q, hi, preferred_element_type=jnp.float32) + jnp.dot(
-            q, lo, preferred_element_type=jnp.float32
+        nt = (((1,), (1,)), ((), ()))
+        inter = lax.dot_general(q, hi, nt, preferred_element_type=jnp.float32) + lax.dot_general(
+            q, lo, nt, preferred_element_type=jnp.float32
         )
         total = intra_ref[:, cols] + inter * jnp.exp(-rate * lead)
         mean_square = jnp.mean(total * total, axis=-1, keepdims=True)

time: 88.8 us -> 88.8 us (level)
  no operation moved by 1% of the time
where the time goes in v15:
time: 88.8 us; the launch traced here: 88.5 us
  waiting for transfers between devices  54.2 us (61%)
  Pallas kernels  17.6 us (20%)
  starting transfers between devices  15.4 us (17%)
    all_to_all x1, waiting for transfers between devices, body(): gathered = lax.all_to_all(chunks, AXES, 0, 0, tiled=True)  29.5 us
    all_to_all x1, waiting for transfers between devices, body(): incoming = lax.all_to_all(before, AXES, 0, 0, tiled=True)  24.7 us
    all_to_all x1, starting transfers between devices, body(): gathered = lax.all_to_all(chunks, AXES, 0, 0, tiled=True)  11.5 us
    pallas_call x1, Pallas kernels, block_intra(): pl.pallas_call(intra_kernel, grid=(groups,), in_specs=[pl.BlockSpec(memor...  6.28 us
    pallas_call x1, Pallas kernels, block_output(): pl.pallas_call(output_kernel, grid=(groups,), in_specs=[pl.BlockSpec(memo...  5.41 us
    pallas_call x1, Pallas kernels, block_state(): pl.pallas_call(state_kernel, grid=(groups,), in_specs=[pl.BlockSpec(memor...  4.42 us
    all_to_all x1, starting transfers between devices, body(): incoming = lax.all_to_all(before, AXES, 0, 0, tiled=True)  3.86 us
  transfers between devices with their start and end apart: 2, of which 2 were waited for; matrix products, arithmetic and copies ran while one was open for 1% of the time, Pallas kernels for 7%

profile of v15, /device:TPU:1, one launch (start us, length us, event | category | flops | bytes accessed | tf_op | source)
XLA Modules:
  0.0 88.5 jit_solution(4081162305733954652)
XLA Ops:
  0.0 4.4 %shard_map.56 = f32[32,128,128]{2,1,0:T(8,128)} custom-call(f32[32]{0:T(128)} %rates_ref.5, bf16[256,4096]{1,0:T(8,128)(2,1)} %k_ref.3, bf16[256,4096]{1,0:T(8,128)(2,1)} %v_ref.3), custom_call_target="tpu_custom_call" | custom-call | flops 536870912 | bytes 6291456 | tf_op jit(solution)/shard_map/pallas_call | solution.py:48
  4.4 0.0 copy-start
  4.4 11.5 %all-to-all-start = ((f32[128,32,128]{2,1,0:T(8,128)}), f32[128,32,128]{2,1,0:T(8,128)S(1)}, u32[]{:S(2)}, u32[]{:S(2)}) async-start(f32[128,32,128]{2,1,0:T(8,128)} %bitcast.4), calls=%async_computation | async-start | bytes 4194304 | tf_op jit(solution)/shard_map/all_to_all | solution.py:209
  15.9 0.0 copy-done
  16.0 0.6 dynamic_slice.3
  17.2 29.5 %all-to-all-done.g_ref = f32[128,32,128]{2,1,0:T(8,128)S(1)} async-done(((f32[128,32,128]{2,1,0:T(8,128)}), f32[128,32,128]{2,1,0:T(8,128)S(1)}, u32[]{:S(2)}, u32[]{:S(2)}) %all-to-all-start) | async-done | bytes 2097184 | tf_op jit(solution)/shard_map/all_to_all | solution.py:209
  46.8 1.4 %shard_map.57 = f32[128,32,128]{2,1,0:T(8,128)} custom-call(f32[1]{0:T(128)S(6)} %exp.3.carry_ref, f32[128,32,128]{2,1,0:T(8,128)S(1)} %all-to-all-done.g_ref), custom_call_target="tpu_custom_call" | custom-call | flops 1048576 | bytes 4194304 | tf_op jit(solution)/shard_map/pallas_call | solution.py:181
  48.2 3.9 %all-to-all-start.1 = ((f32[128,32,128]{2,1,0:T(8,128)}), f32[128,32,128]{2,1,0:T(8,128)S(1)}, u32[]{:S(2)}, u32[]{:S(2)}) async-start(f32[128,32,128]{2,1,0:T(8,128)} %shard_map.57), calls=%async_computation.1 | async-start | bytes 4194304 | tf_op jit(solution)/shard_map/all_to_all | solution.py:214
  52.1 6.3 %shard_map.55.intra_ref = f32[256,4096]{1,0:T(8,128)} custom-call(f32[32]{0:T(128)} %rates_ref.5, bf16[256,4096]{1,0:T(8,128)(2,1)} %q_ref.3, bf16[256,4096]{1,0:T(8,128)(2,1)} %k_ref.3, bf16[256,4096]{1,0:T(8,128)(2,1)} %v_ref.3), custom_call_target="tpu_custom_call" | custom-call | flops 1073741824 | bytes 10485760 | tf_op jit(solution)/shard_map/pallas_call | solution.py:91
  58.4 24.7 %all-to-all-done.1 = f32[128,32,128]{2,1,0:T(8,128)S(1)} async-done(((f32[128,32,128]{2,1,0:T(8,128)}), f32[128,32,128]{2,1,0:T(8,128)S(1)}, u32[]{:S(2)}, u32[]{:S(2)}) %all-to-all-start.1) | async-done | bytes 2097184 | tf_op jit(solution)/shard_map/all_to_all | solution.py:214
  83.0 5.4 %shard_map.58 = bf16[256,4096]{1,0:T(8,128)(2,1)} custom-call(f32[32]{0:T(128)} %rates_ref.5, f32[256,4096]{1,0:T(8,128)} %shard_map.55.intra_ref, bf16[256,4096]{1,0:T(8,128)(2,1)} %q_ref.3, f32[32,128,128]{2,1,0:T(8,128)S(1)} %bitcast.3, f32[32,128]{1,0:T(8,128)} %bitcast.5), custom_call_target="tpu_custom_call" | custom-call | flops 536870912 | bytes 10485760 | tf_op jit(solution)/shard_map/pallas_call | solution.py:133
Async XLA Ops:
  4.4 11.5 %copy-start = (f32[32]{0:T(128)S(1)}, f32[32]{0:T(128)}, u32[]{:S(2)}) copy-start(f32[32]{0:T(128)} %rates_ref.5) | copy-start | bytes 388
  4.4 42.3 %all-to-all-start = ((f32[128,32,128]{2,1,0:T(8,128)}), f32[128,32,128]{2,1,0:T(8,128)S(1)}, u32[]{:S(2)}, u32[]{:S(2)}) async-start(f32[128,32,128]{2,1,0:T(8,128)} %bitcast.4), calls=%async_computation | async-start | bytes 4194304 | tf_op jit(solution)/shard_map/all_to_all | solution.py:209
  48.2 34.8 %all-to-all-start.1 = ((f32[128,32,128]{2,1,0:T(8,128)}), f32[128,32,128]{2,1,0:T(8,128)S(1)}, u32[]{:S(2)}, u32[]{:S(2)}) async-start(f32[128,32,128]{2,1,0:T(8,128)} %shard_map.57), calls=%async_computation.1 | async-start | bytes 4194304 | tf_op jit(solution)/shard_map/all_to_all | solution.py:214

commit v16 on v13

--- a/solution.py
+++ b/solution.py
@@ -157,17 +157,25 @@
         for p in range(STREAMS)
     ]
     carry = carry_ref[0]
+    carry2 = carry * carry
     state = jnp.zeros(g_ref.shape[1:], jnp.float32)
     out_vmem[0] = state
 
-    def step(b, state):
-        state = carry * state + g_ref[b - 1]
-        out_vmem[b] = state
+    def pair(i, state):
+        b = 2 * i
+        a0 = g_ref[b]
+        a1 = g_ref[b + 1]
+        out_vmem[b + 1] = carry * state + a0
+        state = carry2 * state + (carry * a0 + a1)
+        out_vmem[b + 2] = state
         return state
 
     for p in range(STREAMS):
-        first = 1 if p == 0 else p * size
-        state = lax.fori_loop(first, (p + 1) * size, step, state, unroll=8)
+        first = p * size // 2
+        last = (p + 1) * size // 2 - (1 if p == STREAMS - 1 else 0)
+        state = lax.fori_loop(first, last, pair, state, unroll=4)
+        if p == STREAMS - 1:
+            out_vmem[blocks - 1] = carry * state + g_ref[blocks - 2]
         stores[p].start()
     for copy in stores:
         copy.wait()

time: 88.8 us -> 88.7 us (level)
  no operation moved by 1% of the time
where the time goes in v16:
time: 88.7 us; the launch traced here: 88.4 us
  waiting for transfers between devices  54.2 us (61%)
  Pallas kernels  17.5 us (20%)
  starting transfers between devices  15.4 us (17%)
    all_to_all x1, waiting for transfers between devices, body(): gathered = lax.all_to_all(chunks, AXES, 0, 0, tiled=True)  29.5 us
    all_to_all x1, waiting for transfers between devices, body(): incoming = lax.all_to_all(before, AXES, 0, 0, tiled=True)  24.7 us
    all_to_all x1, starting transfers between devices, body(): gathered = lax.all_to_all(chunks, AXES, 0, 0, tiled=True)  11.5 us
    pallas_call x1, Pallas kernels, block_intra(): pl.pallas_call(intra_kernel, grid=(groups,), in_specs=[pl.BlockSpec(memor...  6.28 us
    pallas_call x1, Pallas kernels, block_output(): pl.pallas_call(output_kernel, grid=(groups,), in_specs=[pl.BlockSpec(memo...  5.4 us
    pallas_call x1, Pallas kernels, block_state(): pl.pallas_call(state_kernel, grid=(groups,), in_specs=[pl.BlockSpec(memor...  4.42 us
    all_to_all x1, starting transfers between devices, body(): incoming = lax.all_to_all(before, AXES, 0, 0, tiled=True)  3.86 us
  transfers between devices with their start and end apart: 2, of which 2 were waited for; matrix products, arithmetic and copies ran while one was open for 1% of the time, Pallas kernels for 7%

profile of v16, /device:TPU:1, one launch (start us, length us, event | category | flops | bytes accessed | tf_op | source)
XLA Modules:
  0.0 88.4 jit_solution(7995170178376415954)
XLA Ops:
  0.0 4.4 %shard_map.56 = f32[32,128,128]{2,1,0:T(8,128)} custom-call(f32[32]{0:T(128)} %rates_ref.5, bf16[256,4096]{1,0:T(8,128)(2,1)} %k_ref.3, bf16[256,4096]{1,0:T(8,128)(2,1)} %v_ref.3), custom_call_target="tpu_custom_call" | custom-call | flops 536870912 | bytes 6291456 | tf_op jit(solution)/shard_map/pallas_call | solution.py:46
  4.4 0.0 copy-start
  4.4 11.5 %all-to-all-start = ((f32[128,32,128]{2,1,0:T(8,128)}), f32[128,32,128]{2,1,0:T(8,128)S(1)}, u32[]{:S(2)}, u32[]{:S(2)}) async-start(f32[128,32,128]{2,1,0:T(8,128)} %bitcast.4), calls=%async_computation | async-start | bytes 4194304 | tf_op jit(solution)/shard_map/all_to_all | solution.py:214
  15.9 0.0 copy-done
  16.0 0.6 dynamic_slice.3
  17.2 29.5 %all-to-all-done.g_ref = f32[128,32,128]{2,1,0:T(8,128)S(1)} async-done(((f32[128,32,128]{2,1,0:T(8,128)}), f32[128,32,128]{2,1,0:T(8,128)S(1)}, u32[]{:S(2)}, u32[]{:S(2)}) %all-to-all-start) | async-done | bytes 2097184 | tf_op jit(solution)/shard_map/all_to_all | solution.py:214
  46.8 1.4 %shard_map.57 = f32[128,32,128]{2,1,0:T(8,128)} custom-call(f32[1]{0:T(128)S(6)} %exp.3.carry_ref, f32[128,32,128]{2,1,0:T(8,128)S(1)} %all-to-all-done.g_ref), custom_call_target="tpu_custom_call" | custom-call | flops 1048576 | bytes 4194304 | tf_op jit(solution)/shard_map/pallas_call | solution.py:186
  48.2 3.9 %all-to-all-start.1 = ((f32[128,32,128]{2,1,0:T(8,128)}), f32[128,32,128]{2,1,0:T(8,128)S(1)}, u32[]{:S(2)}, u32[]{:S(2)}) async-start(f32[128,32,128]{2,1,0:T(8,128)} %shard_map.57), calls=%async_computation.1 | async-start | bytes 4194304 | tf_op jit(solution)/shard_map/all_to_all | solution.py:219
  52.0 6.3 %shard_map.55.intra_ref = f32[256,4096]{1,0:T(8,128)} custom-call(f32[32]{0:T(128)} %rates_ref.5, bf16[256,4096]{1,0:T(8,128)(2,1)} %q_ref.3, bf16[256,4096]{1,0:T(8,128)(2,1)} %k_ref.3, bf16[256,4096]{1,0:T(8,128)(2,1)} %v_ref.3), custom_call_target="tpu_custom_call" | custom-call | flops 1073741824 | bytes 10485760 | tf_op jit(solution)/shard_map/pallas_call | solution.py:89
  58.3 24.7 %all-to-all-done.1 = f32[128,32,128]{2,1,0:T(8,128)S(1)} async-done(((f32[128,32,128]{2,1,0:T(8,128)}), f32[128,32,128]{2,1,0:T(8,128)S(1)}, u32[]{:S(2)}, u32[]{:S(2)}) %all-to-all-start.1) | async-done | bytes 2097184 | tf_op jit(solution)/shard_map/all_to_all | solution.py:219
  83.0 5.4 %shard_map.58 = bf16[256,4096]{1,0:T(8,128)(2,1)} custom-call(f32[32]{0:T(128)} %rates_ref.5, f32[256,4096]{1,0:T(8,128)} %shard_map.55.intra_ref, bf16[256,4096]{1,0:T(8,128)(2,1)} %q_ref.3, f32[32,128,128]{2,1,0:T(8,128)S(1)} %bitcast.3, f32[32,128]{1,0:T(8,128)} %bitcast.5), custom_call_target="tpu_custom_call" | custom-call | flops 536870912 | bytes 10485760 | tf_op jit(solution)/shard_map/pallas_call | solution.py:130
Async XLA Ops:
  4.4 11.5 %copy-start = (f32[32]{0:T(128)S(1)}, f32[32]{0:T(128)}, u32[]{:S(2)}) copy-start(f32[32]{0:T(128)} %rates_ref.5) | copy-start | bytes 388
  4.4 42.3 %all-to-all-start = ((f32[128,32,128]{2,1,0:T(8,128)}), f32[128,32,128]{2,1,0:T(8,128)S(1)}, u32[]{:S(2)}, u32[]{:S(2)}) async-start(f32[128,32,128]{2,1,0:T(8,128)} %bitcast.4), calls=%async_computation | async-start | bytes 4194304 | tf_op jit(solution)/shard_map/all_to_all | solution.py:214
  48.2 34.8 %all-to-all-start.1 = ((f32[128,32,128]{2,1,0:T(8,128)}), f32[128,32,128]{2,1,0:T(8,128)S(1)}, u32[]{:S(2)}, u32[]{:S(2)}) async-start(f32[128,32,128]{2,1,0:T(8,128)} %shard_map.57), calls=%async_computation.1 | async-start | bytes 4194304 | tf_op jit(solution)/shard_map/all_to_all | solution.py:219

commit v17 on v13

--- a/solution.py
+++ b/solution.py
@@ -10,6 +10,7 @@
 BLOCK = 256
 AXES = ("seq", "head")
 GROUP = 16
+ROW_STEPS = 2
 STREAMS = 4
 
 
@@ -107,8 +108,11 @@
 
 def output_kernel(rates_ref, intra_ref, q_ref, s_ref, gain_ref, out_ref):
     g = pl.program_id(0)
-    span = q_ref.shape[0]
-    lead = lax.broadcasted_iota(jnp.int32, (span, 1), 0).astype(jnp.float32) + 1.0
+    r = pl.program_id(1)
+    rows = q_ref.shape[0]
+    lead = lax.broadcasted_iota(jnp.int32, (rows, 1), 0).astype(jnp.float32) + (
+        r * rows + 1
+    ).astype(jnp.float32)
     for hh in range(GROUP):
         rate = rates_ref[g * GROUP + hh]
         cols = slice(hh * HEAD_DIM, (hh + 1) * HEAD_DIM)
@@ -127,17 +131,19 @@
     span = q.shape[0]
     groups = HEADS // GROUP
     width = GROUP * HEAD_DIM
+    rows = span // ROW_STEPS
+    tile = pl.BlockSpec((rows, width), lambda g, r: (r, g))
     return pl.pallas_call(
         output_kernel,
-        grid=(groups,),
-        in_specs=[
-            pl.BlockSpec(memory_space=pltpu.SMEM),
-            pl.BlockSpec((span, width), lambda g: (0, g)),
-            pl.BlockSpec((span, width), lambda g: (0, g)),
+        grid=(groups, ROW_STEPS),
+        in_specs=[
+            pl.BlockSpec(memory_space=pltpu.SMEM),
+            tile,
+            tile,
             pl.BlockSpec(memory_space=pltpu.VMEM),
             pl.BlockSpec(memory_space=pltpu.VMEM),
         ],
-        out_specs=pl.BlockSpec((span, width), lambda g: (0, g)),
+        out_specs=tile,
         out_shape=jax.ShapeDtypeStruct((span, HEADS * HEAD_DIM), jnp.bfloat16),
         cost_estimate=pl.CostEstimate(
             flops=HEADS * 4 * span * HEAD_DIM * HEAD_DIM,

time: 88.8 us -> 89.2 us (level)
  no operation moved by 1% of the time
where the time goes in v17:
time: 89.2 us; the launch traced here: 88.9 us
  waiting for transfers between devices  54.2 us (61%)
  Pallas kernels  18 us (20%)
  starting transfers between devices  15.4 us (17%)
    all_to_all x1, waiting for transfers between devices, body(): gathered = lax.all_to_all(chunks, AXES, 0, 0, tiled=True)  29.5 us
    all_to_all x1, waiting for transfers between devices, body(): incoming = lax.all_to_all(before, AXES, 0, 0, tiled=True)  24.7 us
    all_to_all x1, starting transfers between devices, body(): gathered = lax.all_to_all(chunks, AXES, 0, 0, tiled=True)  11.5 us
    pallas_call x1, Pallas kernels, block_intra(): pl.pallas_call(intra_kernel, grid=(groups,), in_specs=[pl.BlockSpec(memor...  6.28 us
    pallas_call x1, Pallas kernels, block_output(): pl.pallas_call(output_kernel, grid=(groups, ROW_STEPS), in_specs=[pl.Bloc...  5.88 us
    pallas_call x1, Pallas kernels, block_state(): pl.pallas_call(state_kernel, grid=(groups,), in_specs=[pl.BlockSpec(memor...  4.42 us
    all_to_all x1, starting transfers between devices, body(): incoming = lax.all_to_all(before, AXES, 0, 0, tiled=True)  3.86 us
  transfers between devices with their start and end apart: 2, of which 2 were waited for; matrix products, arithmetic and copies ran while one was open for 1% of the time, Pallas kernels for 7%

profile of v17, /device:TPU:1, one launch (start us, length us, event | category | flops | bytes accessed | tf_op | source)
XLA Modules:
  0.0 88.9 jit_solution(9939739187764090051)
XLA Ops:
  0.0 4.4 %shard_map.56 = f32[32,128,128]{2,1,0:T(8,128)} custom-call(f32[32]{0:T(128)} %rates_ref.5, bf16[256,4096]{1,0:T(8,128)(2,1)} %k_ref.3, bf16[256,4096]{1,0:T(8,128)(2,1)} %v_ref.3), custom_call_target="tpu_custom_call" | custom-call | flops 536870912 | bytes 6291456 | tf_op jit(solution)/shard_map/pallas_call | solution.py:47
  4.4 0.0 copy-start
  4.4 11.5 %all-to-all-start = ((f32[128,32,128]{2,1,0:T(8,128)}), f32[128,32,128]{2,1,0:T(8,128)S(1)}, u32[]{:S(2)}, u32[]{:S(2)}) async-start(f32[128,32,128]{2,1,0:T(8,128)} %bitcast.4), calls=%async_computation | async-start | bytes 4194304 | tf_op jit(solution)/shard_map/all_to_all | solution.py:212
  15.9 0.0 copy-done
  16.0 0.6 dynamic_slice.3
  17.2 29.5 %all-to-all-done.g_ref = f32[128,32,128]{2,1,0:T(8,128)S(1)} async-done(((f32[128,32,128]{2,1,0:T(8,128)}), f32[128,32,128]{2,1,0:T(8,128)S(1)}, u32[]{:S(2)}, u32[]{:S(2)}) %all-to-all-start) | async-done | bytes 2097184 | tf_op jit(solution)/shard_map/all_to_all | solution.py:212
  46.8 1.4 %shard_map.57 = f32[128,32,128]{2,1,0:T(8,128)} custom-call(f32[1]{0:T(128)S(6)} %exp.3.carry_ref, f32[128,32,128]{2,1,0:T(8,128)S(1)} %all-to-all-done.g_ref), custom_call_target="tpu_custom_call" | custom-call | flops 1048576 | bytes 4194304 | tf_op jit(solution)/shard_map/pallas_call | solution.py:184
  48.2 3.9 %all-to-all-start.1 = ((f32[128,32,128]{2,1,0:T(8,128)}), f32[128,32,128]{2,1,0:T(8,128)S(1)}, u32[]{:S(2)}, u32[]{:S(2)}) async-start(f32[128,32,128]{2,1,0:T(8,128)} %shard_map.57), calls=%async_computation.1 | async-start | bytes 4194304 | tf_op jit(solution)/shard_map/all_to_all | solution.py:217
  52.1 6.3 %shard_map.55.intra_ref = f32[256,4096]{1,0:T(8,128)} custom-call(f32[32]{0:T(128)} %rates_ref.5, bf16[256,4096]{1,0:T(8,128)(2,1)} %q_ref.3, bf16[256,4096]{1,0:T(8,128)(2,1)} %k_ref.3, bf16[256,4096]{1,0:T(8,128)(2,1)} %v_ref.3), custom_call_target="tpu_custom_call" | custom-call | flops 1073741824 | bytes 10485760 | tf_op jit(solution)/shard_map/pallas_call | solution.py:90
  58.4 24.7 %all-to-all-done.1 = f32[128,32,128]{2,1,0:T(8,128)S(1)} async-done(((f32[128,32,128]{2,1,0:T(8,128)}), f32[128,32,128]{2,1,0:T(8,128)S(1)}, u32[]{:S(2)}, u32[]{:S(2)}) %all-to-all-start.1) | async-done | bytes 2097184 | tf_op jit(solution)/shard_map/all_to_all | solution.py:217
  83.0 5.9 %shard_map.58 = bf16[256,4096]{1,0:T(8,128)(2,1)} custom-call(f32[32]{0:T(128)} %rates_ref.5, f32[256,4096]{1,0:T(8,128)} %shard_map.55.intra_ref, bf16[256,4096]{1,0:T(8,128)(2,1)} %q_ref.3, f32[32,128,128]{2,1,0:T(8,128)S(1)} %bitcast.3, f32[32,128]{1,0:T(8,128)} %bitcast.5), custom_call_target="tpu_custom_call" | custom-call | flops 536870912 | bytes 10485760 | tf_op jit(solution)/shard_map/pallas_call | solution.py:136
Async XLA Ops:
  4.4 11.5 %copy-start = (f32[32]{0:T(128)S(1)}, f32[32]{0:T(128)}, u32[]{:S(2)}) copy-start(f32[32]{0:T(128)} %rates_ref.5) | copy-start | bytes 388
  4.4 42.3 %all-to-all-start = ((f32[128,32,128]{2,1,0:T(8,128)}), f32[128,32,128]{2,1,0:T(8,128)S(1)}, u32[]{:S(2)}, u32[]{:S(2)}) async-start(f32[128,32,128]{2,1,0:T(8,128)} %bitcast.4), calls=%async_computation | async-start | bytes 4194304 | tf_op jit(solution)/shard_map/all_to_all | solution.py:212
  48.2 34.8 %all-to-all-start.1 = ((f32[128,32,128]{2,1,0:T(8,128)}), f32[128,32,128]{2,1,0:T(8,128)S(1)}, u32[]{:S(2)}, u32[]{:S(2)}) async-start(f32[128,32,128]{2,1,0:T(8,128)} %shard_map.57), calls=%async_computation.1 | async-start | bytes 4194304 | tf_op jit(solution)/shard_map/all_to_all | solution.py:217

commit v18 on v13

--- a/solution.py
+++ b/solution.py
@@ -10,6 +10,7 @@
 BLOCK = 256
 AXES = ("seq", "head")
 GROUP = 16
+OUT_PARTS = 2
 STREAMS = 4
 
 
@@ -105,22 +106,34 @@
     )(decay_rates, q, k, v)
 
 
-def output_kernel(rates_ref, intra_ref, q_ref, s_ref, gain_ref, out_ref):
+def output_kernel(rates_ref, intra_ref, q_ref, s_ref, gain_ref, out_hbm, out_vmem, sems):
     g = pl.program_id(0)
     span = q_ref.shape[0]
     lead = lax.broadcasted_iota(jnp.int32, (span, 1), 0).astype(jnp.float32) + 1.0
-    for hh in range(GROUP):
-        rate = rates_ref[g * GROUP + hh]
-        cols = slice(hh * HEAD_DIM, (hh + 1) * HEAD_DIM)
-        q = q_ref[:, cols]
-        hi, lo = kernel_split(s_ref[g * GROUP + hh])
-        inter = jnp.dot(q, hi, preferred_element_type=jnp.float32) + jnp.dot(
-            q, lo, preferred_element_type=jnp.float32
+    part = GROUP // OUT_PARTS
+    width = part * HEAD_DIM
+    copies = []
+    for c in range(OUT_PARTS):
+        for hh in range(c * part, (c + 1) * part):
+            rate = rates_ref[g * GROUP + hh]
+            cols = slice(hh * HEAD_DIM, (hh + 1) * HEAD_DIM)
+            q = q_ref[:, cols]
+            hi, lo = kernel_split(s_ref[g * GROUP + hh])
+            inter = jnp.dot(q, hi, preferred_element_type=jnp.float32) + jnp.dot(
+                q, lo, preferred_element_type=jnp.float32
+            )
+            total = intra_ref[:, cols] + inter * jnp.exp(-rate * lead)
+            mean_square = jnp.mean(total * total, axis=-1, keepdims=True)
+            normed = total * lax.rsqrt(mean_square + 1e-06) * gain_ref[pl.ds(g * GROUP + hh, 1), :]
+            out_vmem[:, cols] = normed.astype(out_vmem.dtype)
+        start = pl.multiple_of((g * GROUP + c * part) * HEAD_DIM, width)
+        copy = pltpu.make_async_copy(
+            out_vmem.at[:, pl.ds(c * width, width)], out_hbm.at[:, pl.ds(start, width)], sems.at[c]
         )
-        total = intra_ref[:, cols] + inter * jnp.exp(-rate * lead)
-        mean_square = jnp.mean(total * total, axis=-1, keepdims=True)
-        normed = total * lax.rsqrt(mean_square + 1e-06) * gain_ref[pl.ds(g * GROUP + hh, 1), :]
-        out_ref[:, cols] = normed.astype(out_ref.dtype)
+        copy.start()
+        copies.append(copy)
+    for copy in copies:
+        copy.wait()
 
 
 def block_output(decay_rates, intra, q, incoming, gains):
@@ -137,8 +150,12 @@
             pl.BlockSpec(memory_space=pltpu.VMEM),
             pl.BlockSpec(memory_space=pltpu.VMEM),
         ],
-        out_specs=pl.BlockSpec((span, width), lambda g: (0, g)),
+        out_specs=pl.BlockSpec(memory_space=pl.ANY),
         out_shape=jax.ShapeDtypeStruct((span, HEADS * HEAD_DIM), jnp.bfloat16),
+        scratch_shapes=[
+            pltpu.VMEM((span, width), jnp.bfloat16),
+            pltpu.SemaphoreType.DMA((OUT_PARTS,)),
+        ],
         cost_estimate=pl.CostEstimate(
             flops=HEADS * 4 * span * HEAD_DIM * HEAD_DIM,
             transcendentals=HEADS * span,

time: 88.8 us -> 89.4 us (level)
  no operation moved by 1% of the time
where the time goes in v18:
time: 89.4 us; the launch traced here: 89 us
  waiting for transfers between devices  54.2 us (61%)
  Pallas kernels  18.1 us (20%)
  starting transfers between devices  15.4 us (17%)
    all_to_all x1, waiting for transfers between devices, body(): gathered = lax.all_to_all(chunks, AXES, 0, 0, tiled=True)  29.5 us
    all_to_all x1, waiting for transfers between devices, body(): incoming = lax.all_to_all(before, AXES, 0, 0, tiled=True)  24.7 us
    all_to_all x1, starting transfers between devices, body(): gathered = lax.all_to_all(chunks, AXES, 0, 0, tiled=True)  11.5 us
    pallas_call x1, Pallas kernels, block_intra(): pl.pallas_call(intra_kernel, grid=(groups,), in_specs=[pl.BlockSpec(memor...  6.28 us
    pallas_call x1, Pallas kernels, block_output(): pl.pallas_call(output_kernel, grid=(groups,), in_specs=[pl.BlockSpec(memo...  5.99 us
    pallas_call x1, Pallas kernels, block_state(): pl.pallas_call(state_kernel, grid=(groups,), in_specs=[pl.BlockSpec(memor...  4.42 us
    all_to_all x1, starting transfers between devices, body(): incoming = lax.all_to_all(before, AXES, 0, 0, tiled=True)  3.86 us
  transfers between devices with their start and end apart: 2, of which 2 were waited for; matrix products, arithmetic and copies ran while one was open for 1% of the time, Pallas kernels for 7%

profile of v18, /device:TPU:1, one launch (start us, length us, event | category | flops | bytes accessed | tf_op | source)
XLA Modules:
  0.0 89.0 jit_solution(15030459948035079945)
XLA Ops:
  0.0 4.4 %shard_map.56 = f32[32,128,128]{2,1,0:T(8,128)} custom-call(f32[32]{0:T(128)} %rates_ref.5, bf16[256,4096]{1,0:T(8,128)(2,1)} %k_ref.3, bf16[256,4096]{1,0:T(8,128)(2,1)} %v_ref.3), custom_call_target="tpu_custom_call" | custom-call | flops 536870912 | bytes 6291456 | tf_op jit(solution)/shard_map/pallas_call | solution.py:47
  4.4 0.0 copy-start
  4.4 11.5 %all-to-all-start = ((f32[128,32,128]{2,1,0:T(8,128)}), f32[128,32,128]{2,1,0:T(8,128)S(1)}, u32[]{:S(2)}, u32[]{:S(2)}) async-start(f32[128,32,128]{2,1,0:T(8,128)} %bitcast.4), calls=%async_computation | async-start | bytes 4194304 | tf_op jit(solution)/shard_map/all_to_all | solution.py:223
  15.9 0.0 copy-done
  16.0 0.6 dynamic_slice.3
  17.2 29.5 %all-to-all-done.g_ref = f32[128,32,128]{2,1,0:T(8,128)S(1)} async-done(((f32[128,32,128]{2,1,0:T(8,128)}), f32[128,32,128]{2,1,0:T(8,128)S(1)}, u32[]{:S(2)}, u32[]{:S(2)}) %all-to-all-start) | async-done | bytes 2097184 | tf_op jit(solution)/shard_map/all_to_all | solution.py:223
  46.8 1.4 %shard_map.57 = f32[128,32,128]{2,1,0:T(8,128)} custom-call(f32[1]{0:T(128)S(6)} %exp.3.carry_ref, f32[128,32,128]{2,1,0:T(8,128)S(1)} %all-to-all-done.g_ref), custom_call_target="tpu_custom_call" | custom-call | flops 1048576 | bytes 4194304 | tf_op jit(solution)/shard_map/pallas_call | solution.py:195
  48.2 3.9 %all-to-all-start.1 = ((f32[128,32,128]{2,1,0:T(8,128)}), f32[128,32,128]{2,1,0:T(8,128)S(1)}, u32[]{:S(2)}, u32[]{:S(2)}) async-start(f32[128,32,128]{2,1,0:T(8,128)} %shard_map.57), calls=%async_computation.1 | async-start | bytes 4194304 | tf_op jit(solution)/shard_map/all_to_all | solution.py:228
  52.1 6.3 %shard_map.55.intra_ref = f32[256,4096]{1,0:T(8,128)} custom-call(f32[32]{0:T(128)} %rates_ref.5, bf16[256,4096]{1,0:T(8,128)(2,1)} %q_ref.3, bf16[256,4096]{1,0:T(8,128)(2,1)} %k_ref.3, bf16[256,4096]{1,0:T(8,128)(2,1)} %v_ref.3), custom_call_target="tpu_custom_call" | custom-call | flops 1073741824 | bytes 10485760 | tf_op jit(solution)/shard_map/pallas_call | solution.py:90
  58.4 24.7 %all-to-all-done.1 = f32[128,32,128]{2,1,0:T(8,128)S(1)} async-done(((f32[128,32,128]{2,1,0:T(8,128)}), f32[128,32,128]{2,1,0:T(8,128)S(1)}, u32[]{:S(2)}, u32[]{:S(2)}) %all-to-all-start.1) | async-done | bytes 2097184 | tf_op jit(solution)/shard_map/all_to_all | solution.py:228
  83.0 6.0 %shard_map.58 = bf16[256,4096]{1,0:T(8,128)(2,1)} custom-call(f32[32]{0:T(128)} %rates_ref.5, f32[256,4096]{1,0:T(8,128)} %shard_map.55.intra_ref, bf16[256,4096]{1,0:T(8,128)(2,1)} %q_ref.3, f32[32,128,128]{2,1,0:T(8,128)S(1)} %bitcast.3, f32[32,128]{1,0:T(8,128)} %bitcast.5), custom_call_target="tpu_custom_call" | custom-call | flops 536870912 | bytes 10485760 | tf_op jit(solution)/shard_map/pallas_call | solution.py:143
Async XLA Ops:
  4.4 11.5 %copy-start = (f32[32]{0:T(128)S(1)}, f32[32]{0:T(128)}, u32[]{:S(2)}) copy-start(f32[32]{0:T(128)} %rates_ref.5) | copy-start | bytes 388
  4.4 42.3 %all-to-all-start = ((f32[128,32,128]{2,1,0:T(8,128)}), f32[128,32,128]{2,1,0:T(8,128)S(1)}, u32[]{:S(2)}, u32[]{:S(2)}) async-start(f32[128,32,128]{2,1,0:T(8,128)} %bitcast.4), calls=%async_computation | async-start | bytes 4194304 | tf_op jit(solution)/shard_map/all_to_all | solution.py:223
  48.2 34.8 %all-to-all-start.1 = ((f32[128,32,128]{2,1,0:T(8,128)}), f32[128,32,128]{2,1,0:T(8,128)S(1)}, u32[]{:S(2)}, u32[]{:S(2)}) async-start(f32[128,32,128]{2,1,0:T(8,128)} %shard_map.57), calls=%async_computation.1 | async-start | bytes 4194304 | tf_op jit(solution)/shard_map/all_to_all | solution.py:228

commit v19 on v13

--- a/solution.py
+++ b/solution.py
@@ -147,7 +147,7 @@
     )(decay_rates, intra, q, pltpu.with_memory_space_constraint(incoming, pltpu.VMEM), gains)
 
 
-def chain_kernel(carry_ref, g_ref, out_hbm, out_vmem, out_sems):
+def chain_kernel(carry_ref, g_ref, after_ref, out_hbm, out_vmem, out_sems):
     blocks = g_ref.shape[0]
     size = blocks // STREAMS
     stores = [
@@ -173,13 +173,14 @@
         copy.wait()
 
 
-def block_chain(carry, gathered):
+def block_chain(carry, gathered, after):
     blocks, rows, width = gathered.shape
     return pl.pallas_call(
         chain_kernel,
         in_specs=[
             pl.BlockSpec(memory_space=pltpu.SMEM),
             pl.BlockSpec(memory_space=pltpu.VMEM),
+            pl.BlockSpec(memory_space=pl.ANY),
         ],
         out_specs=pl.BlockSpec(memory_space=pl.ANY),
         out_shape=jax.ShapeDtypeStruct((blocks, rows, width), jnp.float32),
@@ -192,7 +193,7 @@
             transcendentals=0,
             bytes_accessed=8 * blocks * rows * width,
         ),
-    )(carry, pltpu.with_memory_space_constraint(gathered, pltpu.VMEM))
+    )(carry, pltpu.with_memory_space_constraint(gathered, pltpu.VMEM), after)
 
 
 def body(n, queries, key_rows, value_rows, decay_rates, norm_gain):
@@ -207,7 +208,7 @@
     intra = block_intra(decay_rates, queries, key_rows, value_rows)
     head_of_chunk = me // (n // HEADS)
     rate = lax.dynamic_slice_in_dim(decay_rates, head_of_chunk, 1)
-    before = block_chain(jnp.exp(-rate * float(span)), gathered)
+    before = block_chain(jnp.exp(-rate * float(span)), gathered, intra)
     incoming = lax.all_to_all(before, AXES, 0, 0, tiled=True)
     incoming = incoming.reshape(HEADS, HEAD_DIM, HEAD_DIM)
 

time: 88.8 us -> 89 us (level)
  blocking collectives: 0 us -> 35.1 us
  waiting for transfers between devices: 54.2 us -> 23.2 us
  starting transfers between devices: 15.4 us -> 11.5 us
    all_to_all x0 -> x1, blocking collectives: none -> 35.1 us  [body(): incoming = lax.all_to_all(before, AXES, 0, 0, tiled=True)]
    all_to_all x1 -> x0, waiting for transfers between devices: 24.7 us -> none  [body(): incoming = lax.all_to_all(before, AXES, 0, 0, tiled=True)]
    all_to_all x1, waiting for transfers between devices: 29.5 us -> 23.2 us  [body(): gathered = lax.all_to_all(chunks, AXES, 0, 0, tiled=True)]
    all_to_all x1 -> x0, starting transfers between devices: 3.86 us -> none  [body(): incoming = lax.all_to_all(before, AXES, 0, 0, tiled=True)]
  transfers between devices with their start and end apart: 2 -> 1, of which waited for: 2 -> 1; matrix products, arithmetic and copies ran while one was open for 1% -> 1% of each run, Pallas kernels for 7% -> 7%
where the time goes in v19:
time: 89 us; the launch traced here: 88.7 us
  blocking collectives  35.1 us (39%)
  waiting for transfers between devices  23.2 us (26%)
  Pallas kernels  17.5 us (20%)
  starting transfers between devices  11.5 us (13%)
    all_to_all x1, blocking collectives, body(): incoming = lax.all_to_all(before, AXES, 0, 0, tiled=True)  35.1 us
    all_to_all x1, waiting for transfers between devices, body(): gathered = lax.all_to_all(chunks, AXES, 0, 0, tiled=True)  23.2 us
    all_to_all x1, starting transfers between devices, body(): gathered = lax.all_to_all(chunks, AXES, 0, 0, tiled=True)  11.5 us
    pallas_call x1, Pallas kernels, block_intra(): pl.pallas_call(intra_kernel, grid=(groups,), in_specs=[pl.BlockSpec(memor...  6.25 us
    pallas_call x1, Pallas kernels, block_output(): pl.pallas_call(output_kernel, grid=(groups,), in_specs=[pl.BlockSpec(memo...  5.39 us
    pallas_call x1, Pallas kernels, block_state(): pl.pallas_call(state_kernel, grid=(groups,), in_specs=[pl.BlockSpec(memor...  4.42 us
  transfers between devices with their start and end apart: 1, of which 1 were waited for; matrix products, arithmetic and copies ran while one was open for 1% of the time, Pallas kernels for 7%

profile of v19, /device:TPU:1, one launch (start us, length us, event | category | flops | bytes accessed | tf_op | source)
XLA Modules:
  0.0 88.7 jit_solution(2999144539053931780)
XLA Ops:
  0.0 4.4 %shard_map.56 = f32[32,128,128]{2,1,0:T(8,128)} custom-call(f32[32]{0:T(128)} %rates_ref.5, bf16[256,4096]{1,0:T(8,128)(2,1)} %k_ref.3, bf16[256,4096]{1,0:T(8,128)(2,1)} %v_ref.3), custom_call_target="tpu_custom_call" | custom-call | flops 536870912 | bytes 6291456 | tf_op jit(solution)/shard_map/pallas_call | solution.py:46
  4.4 0.0 copy-start
  4.4 11.5 %all-to-all-start = ((f32[128,32,128]{2,1,0:T(8,128)}), f32[128,32,128]{2,1,0:T(8,128)S(1)}, u32[]{:S(2)}, u32[]{:S(2)}) async-start(f32[128,32,128]{2,1,0:T(8,128)} %bitcast.4), calls=%async_computation | async-start | bytes 4194304 | tf_op jit(solution)/shard_map/all_to_all | solution.py:207
  15.9 0.0 copy-done
  16.0 0.7 dynamic_slice.3
  17.3 6.3 %shard_map.55.after_ref.intra_ref = f32[256,4096]{1,0:T(8,128)} custom-call(f32[32]{0:T(128)} %rates_ref.5, bf16[256,4096]{1,0:T(8,128)(2,1)} %q_ref.3, bf16[256,4096]{1,0:T(8,128)(2,1)} %k_ref.3, bf16[256,4096]{1,0:T(8,128)(2,1)} %v_ref.3), custom_call_target="tpu_custom_call" | custom-call | flops 1073741824 | bytes 10485760 | tf_op jit(solution)/shard_map/pallas_call | solution.py:89
  23.5 23.2 %all-to-all-done.g_ref = f32[128,32,128]{2,1,0:T(8,128)S(1)} async-done(((f32[128,32,128]{2,1,0:T(8,128)}), f32[128,32,128]{2,1,0:T(8,128)S(1)}, u32[]{:S(2)}, u32[]{:S(2)}) %all-to-all-start) | async-done | bytes 2097184 | tf_op jit(solution)/shard_map/all_to_all | solution.py:207
  46.8 1.4 %shard_map.57 = f32[128,32,128]{2,1,0:T(8,128)} custom-call(f32[1]{0:T(128)S(6)} %exp.3.carry_ref, f32[128,32,128]{2,1,0:T(8,128)S(1)} %all-to-all-done.g_ref, f32[256,4096]{1,0:T(8,128)} %shard_map.55.after_ref.intra_ref), custom_call_target="tpu_custom_call" | custom-call | flops 1048576 | bytes 4194304 | tf_op jit(solution)/shard_map/pallas_call | solution.py:178
  48.2 35.1 %all_to_all.10 = f32[128,32,128]{2,1,0:T(8,128)S(1)} all-to-all(f32[128,32,128]{2,1,0:T(8,128)} %shard_map.57), channel_id=1, replica_groups=mesh['seq'=32,'head'=4] {'seq','head'}, dimensions={0} | all-to-all | bytes 4194304 | tf_op jit(solution)/shard_map/all_to_all | solution.py:212
  83.3 5.4 %shard_map.58 = bf16[256,4096]{1,0:T(8,128)(2,1)} custom-call(f32[32]{0:T(128)} %rates_ref.5, f32[256,4096]{1,0:T(8,128)} %shard_map.55.after_ref.intra_ref, bf16[256,4096]{1,0:T(8,128)(2,1)} %q_ref.3, f32[32,128,128]{2,1,0:T(8,128)S(1)} %bitcast.3, f32[32,128]{1,0:T(8,128)} %bitcast.5), custom_call_target="tpu_custom_call" | custom-call | flops 536870912 | bytes 10485760 | tf_op jit(solution)/shard_map/pallas_call | solution.py:130
Async XLA Ops:
  4.4 11.5 %copy-start = (f32[32]{0:T(128)S(1)}, f32[32]{0:T(128)}, u32[]{:S(2)}) copy-start(f32[32]{0:T(128)} %rates_ref.5) | copy-start | bytes 388
  4.4 42.3 %all-to-all-start = ((f32[128,32,128]{2,1,0:T(8,128)}), f32[128,32,128]{2,1,0:T(8,128)S(1)}, u32[]{:S(2)}, u32[]{:S(2)}) async-start(f32[128,32,128]{2,1,0:T(8,128)} %bitcast.4), calls=%async_computation | async-start | bytes 4194304 | tf_op jit(solution)/shard_map/all_to_all | solution.py:207

commit v20 on v13

--- a/solution.py
+++ b/solution.py
@@ -10,6 +10,7 @@
 BLOCK = 256
 AXES = ("seq", "head")
 GROUP = 16
+OUT_GROUP = GROUP // 2
 STREAMS = 4
 
 
@@ -26,14 +27,15 @@
 def state_kernel(rates_ref, k_ref, v_ref, out_ref):
     g = pl.program_id(0)
     span = k_ref.shape[0]
+    half = g % 2
     tail = (span - 1.0) - lax.broadcasted_iota(jnp.int32, (span, 1), 0).astype(jnp.float32)
-    for hh in range(GROUP):
-        rate = rates_ref[g * GROUP + hh]
-        cols = slice(hh * HEAD_DIM, (hh + 1) * HEAD_DIM)
+    dims = (((0,), (0,)), ((), ()))
+    for hh in range(OUT_GROUP):
+        rate = rates_ref[g * OUT_GROUP + hh]
+        cols = pl.ds(pl.multiple_of((half * OUT_GROUP + hh) * HEAD_DIM, HEAD_DIM), HEAD_DIM)
         kd = k_ref[:, cols].astype(jnp.float32) * jnp.exp(-rate * tail)
         hi, lo = kernel_split(kd)
         v = v_ref[:, cols]
-        dims = (((0,), (0,)), ((), ()))
         out_ref[hh] = lax.dot_general(
             hi, v, dims, preferred_element_type=jnp.float32
         ) + lax.dot_general(lo, v, dims, preferred_element_type=jnp.float32)
@@ -41,17 +43,16 @@
 
 def block_state(decay_rates, k, v):
     span = k.shape[0]
-    groups = HEADS // GROUP
     width = GROUP * HEAD_DIM
     return pl.pallas_call(
         state_kernel,
-        grid=(groups,),
-        in_specs=[
-            pl.BlockSpec(memory_space=pltpu.SMEM),
-            pl.BlockSpec((span, width), lambda g: (0, g)),
-            pl.BlockSpec((span, width), lambda g: (0, g)),
-        ],
-        out_specs=pl.BlockSpec((GROUP, HEAD_DIM, HEAD_DIM), lambda g: (g, 0, 0)),
+        grid=(HEADS // OUT_GROUP,),
+        in_specs=[
+            pl.BlockSpec(memory_space=pltpu.SMEM),
+            pl.BlockSpec((span, width), lambda g: (0, g // 2)),
+            pl.BlockSpec((span, width), lambda g: (0, g // 2)),
+        ],
+        out_specs=pl.BlockSpec((OUT_GROUP, HEAD_DIM, HEAD_DIM), lambda g: (g, 0, 0)),
         out_shape=jax.ShapeDtypeStruct((HEADS, HEAD_DIM, HEAD_DIM), jnp.float32),
         cost_estimate=pl.CostEstimate(
             flops=4 * span * HEADS * HEAD_DIM * HEAD_DIM,

time: 88.8 us -> 90.4 us (1.018)
  Pallas kernels: 17.5 us -> 19.2 us
    pallas_call x1, Pallas kernels: 4.42 us -> 6.04 us  [block_state(): pl.pallas_call(state_kernel, grid=(HEADS // OUT_GROUP,), in_specs=[pl.Blo...]
where the time goes in v20:
time: 90.4 us; the launch traced here: 90.1 us
  waiting for transfers between devices  54.2 us (60%)
  Pallas kernels  19.2 us (21%)
  starting transfers between devices  15.4 us (17%)
    all_to_all x1, waiting for transfers between devices, body(): gathered = lax.all_to_all(chunks, AXES, 0, 0, tiled=True)  29.5 us
    all_to_all x1, waiting for transfers between devices, body(): incoming = lax.all_to_all(before, AXES, 0, 0, tiled=True)  24.7 us
    all_to_all x1, starting transfers between devices, body(): gathered = lax.all_to_all(chunks, AXES, 0, 0, tiled=True)  11.5 us
    pallas_call x1, Pallas kernels, block_intra(): pl.pallas_call(intra_kernel, grid=(groups,), in_specs=[pl.BlockSpec(memor...  6.28 us
    pallas_call x1, Pallas kernels, block_state(): pl.pallas_call(state_kernel, grid=(HEADS // OUT_GROUP,), in_specs=[pl.Blo...  6.04 us
    pallas_call x1, Pallas kernels, block_output(): pl.pallas_call(output_kernel, grid=(groups,), in_specs=[pl.BlockSpec(memo...  5.39 us
    all_to_all x1, starting transfers between devices, body(): incoming = lax.all_to_all(before, AXES, 0, 0, tiled=True)  3.86 us
  transfers between devices with their start and end apart: 2, of which 2 were waited for; matrix products, arithmetic and copies ran while one was open for 1% of the time, Pallas kernels for 7%

profile of v20, /device:TPU:1, one launch (start us, length us, event | category | flops | bytes accessed | tf_op | source)
XLA Modules:
  0.0 90.1 jit_solution(4572963093235842298)
XLA Ops:
  0.0 6.0 %shard_map.56 = f32[32,128,128]{2,1,0:T(8,128)} custom-call(f32[32]{0:T(128)} %rates_ref.5, bf16[256,4096]{1,0:T(8,128)(2,1)} %k_ref.3, bf16[256,4096]{1,0:T(8,128)(2,1)} %v_ref.3), custom_call_target="tpu_custom_call" | custom-call | flops 536870912 | bytes 6291456 | tf_op jit(solution)/shard_map/pallas_call | solution.py:47
  6.0 0.0 copy-start
  6.0 11.5 %all-to-all-start = ((f32[128,32,128]{2,1,0:T(8,128)}), f32[128,32,128]{2,1,0:T(8,128)S(1)}, u32[]{:S(2)}, u32[]{:S(2)}) async-start(f32[128,32,128]{2,1,0:T(8,128)} %bitcast.4), calls=%async_computation | async-start | bytes 4194304 | tf_op jit(solution)/shard_map/all_to_all | solution.py:207
  17.6 0.0 copy-done
  17.6 0.6 dynamic_slice.3
  18.8 29.5 %all-to-all-done.g_ref = f32[128,32,128]{2,1,0:T(8,128)S(1)} async-done(((f32[128,32,128]{2,1,0:T(8,128)}), f32[128,32,128]{2,1,0:T(8,128)S(1)}, u32[]{:S(2)}, u32[]{:S(2)}) %all-to-all-start) | async-done | bytes 2097184 | tf_op jit(solution)/shard_map/all_to_all | solution.py:207
  48.4 1.4 %shard_map.57 = f32[128,32,128]{2,1,0:T(8,128)} custom-call(f32[1]{0:T(128)S(6)} %exp.3.carry_ref, f32[128,32,128]{2,1,0:T(8,128)S(1)} %all-to-all-done.g_ref), custom_call_target="tpu_custom_call" | custom-call | flops 1048576 | bytes 4194304 | tf_op jit(solution)/shard_map/pallas_call | solution.py:179
  49.8 3.9 %all-to-all-start.1 = ((f32[128,32,128]{2,1,0:T(8,128)}), f32[128,32,128]{2,1,0:T(8,128)S(1)}, u32[]{:S(2)}, u32[]{:S(2)}) async-start(f32[128,32,128]{2,1,0:T(8,128)} %shard_map.57), calls=%async_computation.1 | async-start | bytes 4194304 | tf_op jit(solution)/shard_map/all_to_all | solution.py:212
  53.7 6.3 %shard_map.55.intra_ref = f32[256,4096]{1,0:T(8,128)} custom-call(f32[32]{0:T(128)} %rates_ref.5, bf16[256,4096]{1,0:T(8,128)(2,1)} %q_ref.3, bf16[256,4096]{1,0:T(8,128)(2,1)} %k_ref.3, bf16[256,4096]{1,0:T(8,128)(2,1)} %v_ref.3), custom_call_target="tpu_custom_call" | custom-call | flops 1073741824 | bytes 10485760 | tf_op jit(solution)/shard_map/pallas_call | solution.py:90
  60.0 24.7 %all-to-all-done.1 = f32[128,32,128]{2,1,0:T(8,128)S(1)} async-done(((f32[128,32,128]{2,1,0:T(8,128)}), f32[128,32,128]{2,1,0:T(8,128)S(1)}, u32[]{:S(2)}, u32[]{:S(2)}) %all-to-all-start.1) | async-done | bytes 2097184 | tf_op jit(solution)/shard_map/all_to_all | solution.py:212
  84.7 5.4 %shard_map.58 = bf16[256,4096]{1,0:T(8,128)(2,1)} custom-call(f32[32]{0:T(128)} %rates_ref.5, f32[256,4096]{1,0:T(8,128)} %shard_map.55.intra_ref, bf16[256,4096]{1,0:T(8,128)(2,1)} %q_ref.3, f32[32,128,128]{2,1,0:T(8,128)S(1)} %bitcast.3, f32[32,128]{1,0:T(8,128)} %bitcast.5), custom_call_target="tpu_custom_call" | custom-call | flops 536870912 | bytes 10485760 | tf_op jit(solution)/shard_map/pallas_call | solution.py:131
Async XLA Ops:
  6.0 11.5 %copy-start = (f32[32]{0:T(128)S(1)}, f32[32]{0:T(128)}, u32[]{:S(2)}) copy-start(f32[32]{0:T(128)} %rates_ref.5) | copy-start | bytes 388
  6.0 42.3 %all-to-all-start = ((f32[128,32,128]{2,1,0:T(8,128)}), f32[128,32,128]{2,1,0:T(8,128)S(1)}, u32[]{:S(2)}, u32[]{:S(2)}) async-start(f32[128,32,128]{2,1,0:T(8,128)} %bitcast.4), calls=%async_computation | async-start | bytes 4194304 | tf_op jit(solution)/shard_map/all_to_all | solution.py:207
  49.8 34.8 %all-to-all-start.1 = ((f32[128,32,128]{2,1,0:T(8,128)}), f32[128,32,128]{2,1,0:T(8,128)S(1)}, u32[]{:S(2)}, u32[]{:S(2)}) async-start(f32[128,32,128]{2,1,0:T(8,128)} %shard_map.57), calls=%async_computation.1 | async-start | bytes 4194304 | tf_op jit(solution)/shard_map/all_to_all | solution.py:212
